TPU v7x, 128 devices: a whole 4x4x4 slice. The times are simulated.
128 devices in a mesh: space: 16 (over y, z), tm: 8 (over x, core).
Axes of the slice: x: 4, y: 4, z: 4, core: 2. Of those that a mesh axis runs over, the one named last changes fastest.
Arguments:
- voxels: bfloat16 [2, 32, 96, 9216], P(None, 'tm', 'space'), may hold values from -6 to 6
- brain_list: int32 [2, 4096], P(None, 'space'), may hold values from -1 to 255, as said below
- owner_slot: int32 [2, 4096], P(None, 'space'), may hold values from -1 to 2047, as said below
- embed_weight: bfloat16 [864, 1024], P(None, 'tm'), may hold values from -0.21875 to 0.21875
- qkv_weight: bfloat16 [1024, 3072], P('space', 'tm'), may hold values from -3.75 to 3.75
- cotangent: bfloat16 [2, 8, 2048, 1024], P(None, 'tm', 'space'), may hold values from -6 to 6
Outputs:
- d_qkv_weight: float32 [1024, 3072], P('space', 'tm')
- d_embed_weight: float32 [864, 1024], P(None, 'tm')
Inputs may be any that keep to these rules, and one draw needn't show every extreme that they name: `brain_list`: in each block of 256 entries (one slab of one window) the listed patch numbers are distinct and stand first, -1 after them; a slab lists 128 // 2 to 192 patches, both ends reached in every window, and the slabs of a window list 2048 in all. `owner_slot`: -1 exactly where brain_list is -1. In a window each slot 0 to 2047 occurs once. Taking the window's listed patches slab by slab in list order, their owners (slot // 128) are dealt in turn, so one slab sends at most 12 patches to one owner, and in every window some slab sends exactly 12 to every owner.
All inputs are finite; a program needn't handle non-finite values.
Results may differ from a plain program's by a relative error of at most 0.018.
Values may be sent and summed in bfloat16 or wider, within the bound.
No kernel may reach another device: no remote copies, remote signals or barrier semaphores. Data moves between devices by JAX's collectives and lax.ppermute only.
A program may use at most 128 MiB of HBM per device.

v0:
```python
import jax
import jax.numpy as jnp
from jax import lax
from jax.sharding import PartitionSpec as P

D = 1024
HD = 64
PATCH = 864
GY = 96
GZ = 96
OWN = 128
PSLAB = 256


def for_sending(array):

    def short(part):
        return part.astype(jnp.bfloat16) if part.dtype == jnp.float32 else part

    return jax.tree.map(short, array)


def contract(left, right, left_dim, right_dim):
    return lax.dot_general(
        left, right, (((left_dim,), (right_dim,)), ((), ())), preferred_element_type=jnp.float32
    )


def bucket_index(slots, slab_count, capacity):
    owner_of = jnp.where(slots >= 0, slots // OWN, slab_count)
    hits = (owner_of[..., None] == jnp.arange(slab_count, dtype=jnp.int32)).astype(jnp.int32)
    earlier = jnp.cumsum(hits, axis=-2) - hits
    position = jnp.sum(earlier * hits, axis=-1)
    return jnp.where(slots >= 0, owner_of * capacity + position, slab_count * capacity)


def head_grads(queries, key_rows, value_rows, upstream):
    length = queries.shape[0]
    block_rows = min(512, length)
    factor = HD ** (-0.5)
    query_blocks = queries.reshape(length // block_rows, block_rows, HD)
    upstream_blocks = upstream.reshape(length // block_rows, block_rows, HD)

    def step(carried, inputs):
        key_acc, value_acc = carried
        query_part, upstream_part = inputs
        scores = contract(query_part, key_rows, 1, 1) * factor
        raised = jnp.exp(scores - jnp.max(scores, axis=1, keepdims=True))
        attention = raised / jnp.sum(raised, axis=1, keepdims=True)
        d_attention = contract(upstream_part, value_rows, 1, 1)
        inner_sum = jnp.sum(attention * d_attention, axis=1, keepdims=True)
        d_scores = (attention * (d_attention - inner_sum) * factor).astype(jnp.bfloat16)
        grad_query = contract(d_scores, key_rows, 1, 0).astype(jnp.bfloat16)
        key_acc = key_acc + contract(d_scores, query_part, 0, 0)
        value_acc = value_acc + contract(attention.astype(jnp.bfloat16), upstream_part, 0, 0)
        return ((key_acc, value_acc), grad_query)

    zeros_acc = jnp.zeros((length, HD), jnp.float32)
    (key_acc, value_acc), grad_blocks = lax.scan(
        step, (zeros_acc, zeros_acc), (query_blocks, upstream_blocks)
    )
    return (
        grad_blocks.reshape(length, HD),
        key_acc.astype(jnp.bfloat16),
        value_acc.astype(jnp.bfloat16),
    )


def window_grads(lanes, upstream):
    grad_query, grad_key, grad_value = head_grads(
        lanes[:, 0, 0:HD], lanes[:, 1, 0:HD], lanes[:, 2, 0:HD], upstream[:, 0, 0:HD]
    )
    pieces = [jnp.stack([grad_query, grad_key, grad_value], axis=1)]
    return jnp.concatenate(pieces, axis=2)


def heads_grad(exchanged):
    lanes, upstream = exchanged
    result = jax.vmap(window_grads)(lanes, upstream)
    return jax.tree.map(
        lambda part, own: part.astype(own.dtype),
        lax.all_to_all(for_sending(result), "space", split_axis=1, concat_axis=3, tiled=True),
        result,
    )


def body(voxels, brain_list, owner_slot, embed_weight, qkv_weight, cotangent):
    slab_count = lax.axis_size("space")
    my_slab = lax.axis_index("space")
    capacity = 3 * OWN // (2 * slab_count)
    windows = voxels.shape[0]
    row_total = windows * OWN
    side_y = GY // 6
    side_z = GZ // 6
    local_patches = (
        voxels.reshape(windows, 4, 6, side_y, 6, side_z, 6)
        .transpose(0, 3, 5, 1, 2, 4, 6)
        .reshape(windows, side_y * side_z, PATCH)
    )
    window_rows = jnp.arange(windows, dtype=jnp.int32)[:, None]
    my_buckets = bucket_index(owner_slot, slab_count, capacity)
    entries = jnp.broadcast_to(jnp.arange(PSLAB, dtype=jnp.int32)[None, :], (windows, PSLAB))
    sender = (
        jnp.full((windows, slab_count * capacity), -1, jnp.int32)
        .at[window_rows, my_buckets]
        .set(entries, mode="drop")
    )
    patch_id = brain_list[window_rows, jnp.maximum(sender, 0)]
    patch_rows = local_patches[window_rows, jnp.maximum(patch_id, 0)]
    patch_rows = jnp.where((sender >= 0)[:, :, None], patch_rows, jnp.zeros_like(patch_rows))
    all_slots = lax.all_gather(owner_slot, "space", axis=1, tiled=True).reshape(
        windows, slab_count, PSLAB
    )
    their_buckets = bucket_index(all_slots, slab_count, capacity)
    arrival = (
        jnp.arange(slab_count, dtype=jnp.int32)[None, :, None] * capacity + their_buckets % capacity
    )
    mine_flag = (all_slots >= 0) & (all_slots // OWN == my_slab)
    target = jnp.where(mine_flag, all_slots % OWN, OWN)
    placement = (
        jnp.zeros((windows, OWN), jnp.int32)
        .at[window_rows[:, :, None], target]
        .set(arrival, mode="drop")
    )
    sent_tokens = (
        jnp.einsum(
            "wnp,pd->wnd",
            patch_rows,
            lax.all_gather(embed_weight, "tm", axis=1, tiled=True),
            preferred_element_type=jnp.float32,
        )
        .astype(jnp.bfloat16)
        .reshape(windows, slab_count, capacity, D)
    )
    arrived = lax.all_to_all(sent_tokens, "space", split_axis=1, concat_axis=1, tiled=True).reshape(
        windows, slab_count * capacity, D
    )
    tokens = arrived[window_rows, placement]
    widened = tokens.reshape(row_total, D).astype(jnp.float32)
    center = widened - jnp.mean(widened, axis=1, keepdims=True)
    inverse = lax.rsqrt(jnp.mean(center * center, axis=1, keepdims=True) + 1e-05)
    normed = center * inverse
    hidden = normed.astype(jnp.bfloat16)
    wide_rows = lax.all_gather(qkv_weight, "tm", axis=1, tiled=True)
    section = hidden
    packed = jnp.dot(
        section,
        lax.all_gather(wide_rows, "space", axis=0, tiled=True),
        preferred_element_type=jnp.float32,
    ).astype(jnp.bfloat16)
    lanes_in = packed.reshape(windows, OWN, 3, D)
    upstream_in = cotangent.reshape(windows, OWN, 1, D)
    d_packed = heads_grad(
        (
            lax.all_to_all(lanes_in, "space", split_axis=3, concat_axis=1, tiled=True),
            lax.all_to_all(upstream_in, "space", split_axis=3, concat_axis=1, tiled=True),
        )
    ).reshape(row_total, 3 * D)
    d_hidden = contract(d_packed, lax.all_gather(wide_rows, "space", axis=0, tiled=True), 1, 1)
    section = hidden
    my_rows = lax.psum_scatter(
        contract(section, d_packed, 0, 0).astype(jnp.bfloat16),
        "space",
        scatter_dimension=0,
        tiled=True,
    )
    d_qkv_weight = lax.psum_scatter(my_rows, "tm", scatter_dimension=1, tiled=True).astype(
        jnp.float32
    )
    first_mean = jnp.mean(d_hidden, axis=1, keepdims=True)
    second_mean = jnp.mean(d_hidden * normed, axis=1, keepdims=True)
    d_tokens = (
        (inverse * (d_hidden - first_mean - normed * second_mean))
        .astype(jnp.bfloat16)
        .reshape(windows, OWN, D)
    )
    returned = (
        jnp.zeros((windows, slab_count * capacity, D), jnp.bfloat16)
        .at[window_rows, placement]
        .set(d_tokens)
    )
    came_back = lax.all_to_all(
        returned.reshape(windows, slab_count, capacity, D),
        "space",
        split_axis=1,
        concat_axis=1,
        tiled=True,
    ).reshape(windows, slab_count * capacity, D)
    embed_partial = jnp.einsum(
        "wnp,wnd->pd", patch_rows, came_back, preferred_element_type=jnp.float32
    )
    embed_cols_sum = lax.psum_scatter(
        embed_partial.astype(jnp.bfloat16), "tm", scatter_dimension=1, tiled=True
    )
    d_embed_weight = lax.psum(embed_cols_sum, "space").astype(jnp.float32)
    return (d_qkv_weight, d_embed_weight)


def solution(mesh):
    placed = (
        P(None, "tm", "space", None),
        P(None, "space"),
        P(None, "space"),
        P(None, "tm"),
        P("space", "tm"),
        P(None, "tm", "space", None),
    )
    return jax.shard_map(
        body,
        mesh=mesh,
        in_specs=placed,
        out_specs=(P("space", "tm"), P(None, "tm")),
        check_vma=False,
    )
```

profile of v0, /device:TPU:1, one launch (start us, length us, event | category | flops | bytes accessed | tf_op | source)
XLA Modules:
  0.0 806.3 jit_solution(14433915732774478614)
XLA Ops:
  8.0 16.0 %all_gather.15 = bf16[64,3072]{1,0:T(8,128)(2,1)} all-gather(bf16[64,384]{1,0:T(8,128)(2,1)} %param.12), channel_id=1, replica_groups=mesh['space'=16,'tm'=8] {'tm'}, dimensions={1}, use_global_device_ids=true | all-gather | bytes 442368 | tf_op jit(solution)/shard_map/all_gather | solution.py:144
  24.0 20.6 %all_gather.14 = s32[2,4096]{1,0:T(2,128)S(1)} all-gather(s32[2,256]{1,0:T(2,128)} %param.10), channel_id=1, replica_groups=mesh['space'=16,'tm'=8] {'space'}, dimensions={1}, use_global_device_ids=true | all-gather | bytes 34816 | tf_op jit(solution)/shard_map/all_gather | solution.py:111
  44.8 18.1 %reduce-window.16 = s32[2,16,16,2,128]{4,2,3,1,0:T(8,128)S(1)} reduce-window(s32[2,16,16,2,128]{4,2,3,1,0:T(8,128)S(1)} %fusion.82, s32[]{:T(128)} %constant.103.clone.1), window={size=1x1x1x1x128 pad=0_0x0_0x0_0x0_0x127_0}, to_apply=%region_4.5 | reduce-window | flops 16646144 | bytes 1048580 | tf_op jit(solution)/shard_map/reduce-window.2
  66.8 24.7 %scatter_fusion = s32[2,192]{1,0:T(2,128)S(1)} fusion(s32[2,192]{1,0:T(2,128)S(1)} %broadcast_in_dim.58, s32[512]{0:T(512)S(1)} %bitcast.264, s32[512]{0:T(512)S(1)} %bitcast.292), kind=kCustom, calls=%fused_computation.3 | custom fusion | bytes 10240 | tf_op jit(solution)/shard_map/scatter | solution.py:106
  95.5 44.1 %reshape.335 = bf16[2,4,6,16,6,16,6]{6,5,4,3,1,2,0:T(8,128)(2,1)} reshape(bf16[2,4,6,9216]{3,1,2,0:T(4,128)(2,1)S(1)} %copy-done.8) | data formatting | bytes 1769472 | tf_op jit(solution)/shard_map/reshape | solution.py:96
  139.6 34.5 %copy.48 = bf16[2,16,16,4,6,6,6]{2,1,6,5,4,3,0:T(8,128)(2,1)} copy(bf16[2,16,16,4,6,6,6]{6,2,5,1,3,4,0:T(8,128)(2,1)} %bitcast.263) | data formatting | bytes 1769472 | tf_op jit(solution)/shard_map/transpose | solution.py:97
  174.1 8.6 %reshape.336 = bf16[2,256,864]{1,2,0:T(8,128)(2,1)S(1)} reshape(bf16[2,16,16,4,6,6,6]{2,1,6,5,4,3,0:T(8,128)(2,1)} %copy.48) | data formatting | bytes 1769472 | tf_op jit(solution)/shard_map/reshape | solution.py:98
  183.4 5.1 gather_fusion.1
  193.2 4.9 all-to-all-start
  199.6 30.4 %scatter_custom_fusion.2 = s32[256]{0:T(256)S(1)} fusion(s32[8192]{0:T(1024)S(1)} %bitcast.291, s32[8192]{0:T(1024)S(1)} %bitcast.290, s32[]{:T(128)} %constant.103.clone.1), kind=kCustom, calls=%fused_computation.167 | custom fusion | bytes 1028
  230.6 6.8 all-to-all-start.2
  241.9 5.8 convolution_convert_fusion.1
  247.8 4.6 reshape.418
  252.4 4.1 copy.56
  256.4 6.7 all-to-all-start.1
  264.1 14.8 %all-to-all-done.1 = bf16[2,128,3,1024]{1,0,2,3:T(2,128)(2,1)S(1)} async-done(((bf16[2,128,3,1024]{1,0,2,3:T(2,128)(2,1)}), bf16[2,128,3,1024]{1,0,2,3:T(2,128)(2,1)S(1)}, u32[]{:S(2)}, u32[]{:S(2)}) %all-to-all-start.1) | async-done | bytes 1572896 | tf_op jit(solution)/shard_map/all_to_all | solution.py:155
  281.7 179.5 %while.15 = (s32[]{:T(128)}, f32[2,2048,64]{1,2,0:T(8,128)S(1)}, f32[2,2048,64]{1,2,0:T(8,128)}, bf16[4,2,512,64]{2,3,1,0:T(8,128)(2,1)}, bf16[4,2,512,64]{2,3,1...) while((s32[]{:T(128)}, f32[2,2048,64]{1,2,0:T(8,128)S(1)}, ...), condition=%wide.region_14.15_spmd.clone, body=%wide.region_10.14_spmd.clone.sunk | while | flops 1383145472 | bytes 107112112 | solution.py:59
  281.7 6.8 fusion.157
  288.5 4.5 fusion.156
  293.1 13.4 %fusion.160 = bf16[4,2,512,64]{2,3,1,0:T(8,128)(2,1)} fusion(bf16[4,2,512,64]{2,3,1,0:T(8,128)(2,1)} %get-tuple-element.198, s32[]{:T(128)} %get-tuple-element.195, bf16[2,2048,64]{1,2,0:T(8,128)(2,1)} %get-tuple-element.210, f32[2,512,2048]{2,1,0:T(8,128)} %fusion.156, f32[2,512,2048]{2,1,0:T(8,128)} %get-tuple-element.183, ...), kind=kOutput, calls=%fused_computation.24.clone.1 | convolution fusion | flops 283184128 | bytes 34218496 | tf_op jit(solution)/shard_map/vmap()/while/body/eval_jaxpr/dot_general | solution.py:24
  306.5 4.5 fusion.159
  310.9 15.6 %fusion.158 = f32[2,2048,64]{1,2,0:T(8,128)S(1)} fusion(f32[2,512,2048]{2,1,0:T(8,128)} %fusion.156, f32[2,2048,64]{1,2,0:T(8,128)S(1)} %get-tuple-element.196, pred[]{:T(512)S(6)} %compare.47, bf16[4,2,512,64]{2,3,1,0:T(8,128)(2,1)} %get-tuple-element.209, s32[]{:T(128)} %get-tuple-element.195, f32[2,512,2048]{2,1,0:T(8,128)} %get-tuple-element.183, ...), kind=kOutput, calls=%fused_computation.21.clone.1 | convolution fusion | flops 283642880 | bytes 35791360 | tf_op jit(solution)/shard_map/vmap()/while/body/eval_jaxpr/dot_general | solution.py:24
  326.6 6.8 fusion.157
  333.4 4.5 fusion.156
  337.9 13.4 %fusion.160 = bf16[4,2,512,64]{2,3,1,0:T(8,128)(2,1)} fusion(bf16[4,2,512,64]{2,3,1,0:T(8,128)(2,1)} %get-tuple-element.198, s32[]{:T(128)} %get-tuple-element.195, bf16[2,2048,64]{1,2,0:T(8,128)(2,1)} %get-tuple-element.210, f32[2,512,2048]{2,1,0:T(8,128)} %fusion.156, f32[2,512,2048]{2,1,0:T(8,128)} %get-tuple-element.183, ...), kind=kOutput, calls=%fused_computation.24.clone.1 | convolution fusion | flops 283184128 | bytes 34218496 | tf_op jit(solution)/shard_map/vmap()/while/body/eval_jaxpr/dot_general | solution.py:24
  351.3 4.5 fusion.159
  355.8 15.6 %fusion.158 = f32[2,2048,64]{1,2,0:T(8,128)S(1)} fusion(f32[2,512,2048]{2,1,0:T(8,128)} %fusion.156, f32[2,2048,64]{1,2,0:T(8,128)S(1)} %get-tuple-element.196, pred[]{:T(512)S(6)} %compare.47, bf16[4,2,512,64]{2,3,1,0:T(8,128)(2,1)} %get-tuple-element.209, s32[]{:T(128)} %get-tuple-element.195, f32[2,512,2048]{2,1,0:T(8,128)} %get-tuple-element.183, ...), kind=kOutput, calls=%fused_computation.21.clone.1 | convolution fusion | flops 283642880 | bytes 35791360 | tf_op jit(solution)/shard_map/vmap()/while/body/eval_jaxpr/dot_general | solution.py:24
  371.4 6.8 fusion.157
  378.3 4.5 fusion.156
  382.8 13.4 %fusion.160 = bf16[4,2,512,64]{2,3,1,0:T(8,128)(2,1)} fusion(bf16[4,2,512,64]{2,3,1,0:T(8,128)(2,1)} %get-tuple-element.198, s32[]{:T(128)} %get-tuple-element.195, bf16[2,2048,64]{1,2,0:T(8,128)(2,1)} %get-tuple-element.210, f32[2,512,2048]{2,1,0:T(8,128)} %fusion.156, f32[2,512,2048]{2,1,0:T(8,128)} %get-tuple-element.183, ...), kind=kOutput, calls=%fused_computation.24.clone.1 | convolution fusion | flops 283184128 | bytes 34218496 | tf_op jit(solution)/shard_map/vmap()/while/body/eval_jaxpr/dot_general | solution.py:24
  396.2 4.5 fusion.159
  400.7 15.6 %fusion.158 = f32[2,2048,64]{1,2,0:T(8,128)S(1)} fusion(f32[2,512,2048]{2,1,0:T(8,128)} %fusion.156, f32[2,2048,64]{1,2,0:T(8,128)S(1)} %get-tuple-element.196, pred[]{:T(512)S(6)} %compare.47, bf16[4,2,512,64]{2,3,1,0:T(8,128)(2,1)} %get-tuple-element.209, s32[]{:T(128)} %get-tuple-element.195, f32[2,512,2048]{2,1,0:T(8,128)} %get-tuple-element.183, ...), kind=kOutput, calls=%fused_computation.21.clone.1 | convolution fusion | flops 283642880 | bytes 35791360 | tf_op jit(solution)/shard_map/vmap()/while/body/eval_jaxpr/dot_general | solution.py:24
  416.3 6.8 fusion.157
  423.1 4.5 fusion.156
  427.7 13.4 %fusion.160 = bf16[4,2,512,64]{2,3,1,0:T(8,128)(2,1)} fusion(bf16[4,2,512,64]{2,3,1,0:T(8,128)(2,1)} %get-tuple-element.198, s32[]{:T(128)} %get-tuple-element.195, bf16[2,2048,64]{1,2,0:T(8,128)(2,1)} %get-tuple-element.210, f32[2,512,2048]{2,1,0:T(8,128)} %fusion.156, f32[2,512,2048]{2,1,0:T(8,128)} %get-tuple-element.183, ...), kind=kOutput, calls=%fused_computation.24.clone.1 | convolution fusion | flops 283184128 | bytes 34218496 | tf_op jit(solution)/shard_map/vmap()/while/body/eval_jaxpr/dot_general | solution.py:24
  441.1 4.5 fusion.159
  445.6 15.6 %fusion.158 = f32[2,2048,64]{1,2,0:T(8,128)S(1)} fusion(f32[2,512,2048]{2,1,0:T(8,128)} %fusion.156, f32[2,2048,64]{1,2,0:T(8,128)S(1)} %get-tuple-element.196, pred[]{:T(512)S(6)} %compare.47, bf16[4,2,512,64]{2,3,1,0:T(8,128)(2,1)} %get-tuple-element.209, s32[]{:T(128)} %get-tuple-element.195, f32[2,512,2048]{2,1,0:T(8,128)} %get-tuple-element.183, ...), kind=kOutput, calls=%fused_computation.21.clone.1 | convolution fusion | flops 283642880 | bytes 35791360 | tf_op jit(solution)/shard_map/vmap()/while/body/eval_jaxpr/dot_general | solution.py:24
  465.8 7.9 copy.65
  477.0 27.6 %all_to_all.58 = bf16[16,2,24576]{2,1,0:T(2,128)(2,1)S(1)} all-to-all(bf16[16,2,24576]{2,1,0:T(2,128)(2,1)} %reshape.426), channel_id=1, replica_groups=mesh['space'=16,'tm'=8] {'space'}, dimensions={0} | all-to-all | bytes 3145728 | tf_op jit(solution)/shard_map/all_to_all | solution.py:82
  508.0 7.3 copy.66
  515.4 4.8 fusion.118
  520.7 16.6 %scatter_fusion.1 = bf16[2,192,1024]{2,1,0:T(8,128)(2,1)S(1)} fusion(bf16[2,192,1024]{2,1,0:T(8,128)(2,1)S(1)} %broadcast_in_dim.119, s32[256]{0:T(256)S(1)} %copy-done.2, bf16[256,1024]{1,0:T(8,128)(2,1)S(1)} %multiply_convert_fusion.1), kind=kCustom, calls=%fused_computation.4 | custom fusion | bytes 1574912 | tf_op jit(solution)/shard_map/scatter | solution.py:180
  538.1 13.7 %all_to_all.59 = bf16[2,16,12,1024]{3,0,2,1:T(2,128)(2,1)S(1)} all-to-all(bf16[2,16,12,1024]{3,0,2,1:T(2,128)(2,1)S(1)} %bitcast.276), channel_id=1, replica_groups=mesh['space'=16,'tm'=8] {'space'}, dimensions={1} | all-to-all | bytes 1572864 | tf_op jit(solution)/shard_map/all_to_all | solution.py:182
  559.5 4.5 convolution_convert_fusion
  564.1 28.5 %reduce-scatter.12.cloned.1.call-done = bf16[128,864]{1,0:T(8,128)(2,1)} async-done(((bf16[1024,864]{1,0:T(8,128)(2,1)}), bf16[128,864]{1,0:T(8,128)(2,1)}) %reduce-scatter.12.cloned.1.call-update) | async-done | bytes 221200
  594.4 83.5 %reduce-scatter.8.cloned.1.call-done = bf16[64,3072]{1,0:T(8,128)(2,1)} async-done(((bf16[1024,3072]{1,0:T(8,128)(2,1)}), bf16[64,3072]{1,0:T(8,128)(2,1)}) %reduce-scatter.8.cloned.1.call-update) | async-done | bytes 393232 | tf_op jit(solution)/shard_map/reduce_scatter | solution.py:161
  680.1 85.6 %all-reduce.2.cloned.1.call-done = bf16[864,128]{1,0:T(8,128)(2,1)} async-done(((bf16[864,128]{1,0:T(8,128)(2,1)}), bf16[864,128]{1,0:T(8,128)(2,1)}) %all-reduce.2.cloned.1.call-update) | async-done | bytes 221200 | tf_op jit(solution)/shard_map/psum | solution.py:195
  767.5 30.2 %reduce-scatter.10.cloned.1.call-done = bf16[384,64]{1,0:T(8,128)(2,1)} async-done(((bf16[3072,64]{1,0:T(8,128)(2,1)}), bf16[384,64]{1,0:T(8,128)(2,1)}) %reduce-scatter.10.cloned.1.call-update) | async-done | bytes 49168
  (154 shorter events, 51.7 us)
Async XLA Ops:
  7.2 84.5 %copy-start = (s32[2,256]{1,0:T(2,128)S(1)}, s32[2,256]{1,0:T(2,128)}, u32[]{:S(2)}) copy-start(s32[2,256]{1,0:T(2,128)} %param.9) | copy-start | bytes 6148
  7.2 88.4 %copy-start.8 = (bf16[2,4,6,9216]{3,1,2,0:T(4,128)(2,1)S(1)}, bf16[2,4,6,9216]{3,1,2,0:T(4,128)(2,1)}, u32[]{:S(2)}) copy-start(bf16[2,4,6,9216]{3,1,2,0:T(4,128)(2,1)} %param.8) | copy-start | bytes 2654212
  7.2 181.8 %all-gather.3.cloned.1.call-start = ((), (), s32[]{:S(2)}) async-start(), calls=%async_computation.8 | async-start | bytes 1990656 | tf_op jit(solution)/shard_map/all_gather | solution.py:129
  7.9 233.4 %all-gather.5.cloned.1.call-start = ((), (), s32[]{:S(2)}) async-start(), calls=%async_computation.9 | async-start | bytes 6684672 | tf_op jit(solution)/shard_map/all_gather | solution.py:148
  183.3 14.9 %copy-start.21 = (s32[2]{0:T(128)S(1)}, s32[2]{0:T(128)}, u32[]{:S(2)}) copy-start(s32[2]{0:T(128)} %constant.119) | copy-start | bytes 28
  183.4 15.0 %copy-start.20 = (s32[2]{0:T(128)S(1)}, s32[2]{0:T(128)}, u32[]{:S(2)}) copy-start(s32[2]{0:T(128)} %constant.122) | copy-start | bytes 28
  183.4 15.1 %copy-start.10 = (bf16[2,1,128,1024]{3,2,1,0:T(8,128)(2,1)S(1)}, bf16[2,1,128,1024]{3,2,1,0:T(8,128)(2,1)}, u32[]{:S(2)}) copy-start(bf16[2,1,128,1024]{3,2,1,0:T(8,128)(2,1)} %param.13) | copy-start | bytes 1572868
  188.5 4.7 copy-start.9
  188.9 10.7 %copy-start.18 = (pred[2,192]{1,0:T(4,128)(4,1)}, pred[2,192]{1,0:T(4,128)(4,1)S(1)}, u32[]{:S(2)}) copy-start(pred[2,192]{1,0:T(4,128)(4,1)S(1)} %broadcast_compare_fusion) | copy-start | bytes 1156
  193.2 37.4 %all-to-all-start = ((bf16[2,16,12,1024]{3,0,2,1:T(2,128)(2,1)}), bf16[2,16,12,1024]{3,0,2,1:T(2,128)(2,1)S(1)}, u32[]{:S(2)}, u32[]{:S(2)}) async-start(bf16[2,16,12,1024]{3,0,2,1:T(2,128)(2,1)} %bitcast.6), calls=%async_computation | async-start | bytes 1572864 | tf_op jit(solution)/shard_map/all_to_all | solution.py:135
  230.6 25.9 %all-to-all-start.2 = ((bf16[2,128,1,1024]{1,0,2,3:T(2,128)(2,1)}), bf16[2,128,1,1024]{1,0,2,3:T(2,128)(2,1)S(1)}, u32[]{:S(2)}, u32[]{:S(2)}) async-start(bf16[2,128,1,1024]{1,0,2,3:T(2,128)(2,1)} %bitcast.21), calls=%async_computation.2 | async-start | bytes 1048576 | tf_op jit(solution)/shard_map/all_to_all | solution.py:156
  240.3 7.5 copy-start.3
  240.5 0.9 copy-start.13
  240.5 7.3 copy-start.11
  241.3 0.6 copy-start.15
  256.4 22.4 %all-to-all-start.1 = ((bf16[2,128,3,1024]{1,0,2,3:T(2,128)(2,1)}), bf16[2,128,3,1024]{1,0,2,3:T(2,128)(2,1)S(1)}, u32[]{:S(2)}, u32[]{:S(2)}) async-start(bf16[2,128,3,1024]{1,0,2,3:T(2,128)(2,1)} %copy.56), calls=%async_computation.1 | async-start | bytes 3145728 | tf_op jit(solution)/shard_map/all_to_all | solution.py:155
  263.1 329.4 %reduce-scatter.12.cloned.1.call-start = ((), (), s32[]{:S(2)}) async-start(), calls=%async_computation.13 | async-start | bytes 2064384
  264.1 17.6 %copy-start.5 = (f32[2,2048,64]{1,2,0:T(8,128)S(1)}, f32[2,2048,64]{1,2,0:T(8,128)}, u32[]{:S(2)}) copy-start(f32[2,2048,64]{1,2,0:T(8,128)} %custom-call.10) | copy-start | bytes 3145732
  293.0 13.4 %copy-start.6 = (f32[2,2048,64]{1,2,0:T(8,128)S(1)}, f32[2,2048,64]{1,2,0:T(8,128)}, u32[]{:S(2)}) copy-start(f32[2,2048,64]{1,2,0:T(8,128)} %get-tuple-element.197) | copy-start | bytes 3145732 | tf_op jit(solution)/shard_map/vmap()/while
  310.9 15.6 %copy-start.7 = (f32[2,2048,64]{1,2,0:T(8,128)}, f32[2,2048,64]{1,2,0:T(8,128)S(1)}, u32[]{:S(2)}) copy-start(f32[2,2048,64]{1,2,0:T(8,128)S(1)} %fusion.159) | copy-start | bytes 3145732 | tf_op jit(solution)/shard_map/vmap()/while
  337.9 13.4 %copy-start.6 = (f32[2,2048,64]{1,2,0:T(8,128)S(1)}, f32[2,2048,64]{1,2,0:T(8,128)}, u32[]{:S(2)}) copy-start(f32[2,2048,64]{1,2,0:T(8,128)} %get-tuple-element.197) | copy-start | bytes 3145732 | tf_op jit(solution)/shard_map/vmap()/while
  355.8 15.7 %copy-start.7 = (f32[2,2048,64]{1,2,0:T(8,128)}, f32[2,2048,64]{1,2,0:T(8,128)S(1)}, u32[]{:S(2)}) copy-start(f32[2,2048,64]{1,2,0:T(8,128)S(1)} %fusion.159) | copy-start | bytes 3145732 | tf_op jit(solution)/shard_map/vmap()/while
  382.8 13.4 %copy-start.6 = (f32[2,2048,64]{1,2,0:T(8,128)S(1)}, f32[2,2048,64]{1,2,0:T(8,128)}, u32[]{:S(2)}) copy-start(f32[2,2048,64]{1,2,0:T(8,128)} %get-tuple-element.197) | copy-start | bytes 3145732 | tf_op jit(solution)/shard_map/vmap()/while
  400.7 15.6 %copy-start.7 = (f32[2,2048,64]{1,2,0:T(8,128)}, f32[2,2048,64]{1,2,0:T(8,128)S(1)}, u32[]{:S(2)}) copy-start(f32[2,2048,64]{1,2,0:T(8,128)S(1)} %fusion.159) | copy-start | bytes 3145732 | tf_op jit(solution)/shard_map/vmap()/while
  427.7 13.4 %copy-start.6 = (f32[2,2048,64]{1,2,0:T(8,128)S(1)}, f32[2,2048,64]{1,2,0:T(8,128)}, u32[]{:S(2)}) copy-start(f32[2,2048,64]{1,2,0:T(8,128)} %get-tuple-element.197) | copy-start | bytes 3145732 | tf_op jit(solution)/shard_map/vmap()/while
  445.5 15.6 %copy-start.7 = (f32[2,2048,64]{1,2,0:T(8,128)}, f32[2,2048,64]{1,2,0:T(8,128)S(1)}, u32[]{:S(2)}) copy-start(f32[2,2048,64]{1,2,0:T(8,128)S(1)} %fusion.159) | copy-start | bytes 3145732 | tf_op jit(solution)/shard_map/vmap()/while
  477.0 38.3 %copy-start.4 = (bf16[256,1024]{1,0:T(8,128)(2,1)S(1)}, bf16[256,1024]{1,0:T(8,128)(2,1)}, u32[]{:S(2)}) copy-start(bf16[256,1024]{1,0:T(8,128)(2,1)} %copy-done.3) | copy-start | bytes 1572868
  477.0 38.4 %copy-start.14 = (f32[256]{0:T(256)S(1)}, f32[256]{0:T(256)}, u32[]{:S(2)}) copy-start(f32[256]{0:T(256)} %copy-done.13) | copy-start | bytes 3076
  477.0 38.4 %copy-start.16 = (f32[256]{0:T(256)S(1)}, f32[256]{0:T(256)}, u32[]{:S(2)}) copy-start(f32[256]{0:T(256)} %copy-done.15) | copy-start | bytes 3076
  515.3 5.3 copy-start.2
  520.7 31.1 %copy-start.19 = (pred[2,192]{1,0:T(4,128)(4,1)S(1)}, pred[2,192]{1,0:T(4,128)(4,1)}, u32[]{:S(2)}) copy-start(pred[2,192]{1,0:T(4,128)(4,1)} %copy-done.18) | copy-start | bytes 1156
  538.1 21.1 %copy-start.12 = (f32[2,128]{1,0:T(2,128)S(1)}, f32[2,128]{1,0:T(2,128)}, u32[]{:S(2)}) copy-start(f32[2,128]{1,0:T(2,128)} %copy-done.11) | copy-start | bytes 3076
  538.1 21.1 %copy-start.17 = (f32[2,128]{1,0:T(2,128)S(1)}, f32[2,128]{1,0:T(2,128)}, u32[]{:S(2)}) copy-start(f32[2,128]{1,0:T(2,128)} %get-tuple-element.126) | copy-start | bytes 3076
  559.1 118.8 %reduce-scatter.8.cloned.1.call-start = ((), (), s32[]{:S(2)}) async-start(), calls=%async_computation.10 | async-start | bytes 6684672 | tf_op jit(solution)/shard_map/reduce_scatter | solution.py:161
  559.4 239.8 %copy-start.1 = (s32[2,256]{1,0:T(2,128)S(1)}, s32[2,256]{1,0:T(2,128)}, u32[]{:S(2)}) copy-start(s32[2,256]{1,0:T(2,128)} %param.9) | copy-start | bytes 6148
  564.0 201.7 %all-reduce.2.cloned.1.call-start = ((), (), s32[]{:S(2)}) async-start(), calls=%async_computation.11 | async-start | bytes 442368 | tf_op jit(solution)/shard_map/psum | solution.py:195
  594.3 203.3 %reduce-scatter.10.cloned.1.call-start = ((), (), s32[]{:S(2)}) async-start(), calls=%async_computation.12 | async-start | bytes 884736
Sparse Core Ops, SparseCore 0:
  9.7 29.1 all-gather.2
  41.1 61.7 all-gather.4
  559.2 33.2 reduce-scatter.11
  595.8 82.0 reduce-scatter.7
  681.5 84.1 all-reduce.1
  768.0 29.5 reduce-scatter.9
where the time goes:
time: 818 us; the launch traced here: 806 us
  waiting for transfers between devices  243 us (30%)
  local copies, waits for them, and re-layouts  222 us (27%)
  matrix products  201 us (25%)
  blocking collectives  78 us (10%)
  other arithmetic  29 us (4%)
  starting transfers between devices  18.8 us (2%)
  between operations  15 us (2%)
    dot_general x18, matrix products, contract(): lax.dot_general(left, right, (((left_dim,), (right_dim,)), ((), ())), pre...  161 us
    psum x1, waiting for transfers between devices, body(): d_embed_weight = lax.psum(embed_cols_sum, 'space').astype(jnp.float32)  85.6 us
    reduce_scatter x1, waiting for transfers between devices, body(): lax.psum_scatter(contract(section, d_packed, 0, 0).astype(jnp.bfloat16),...  83.5 us
    unnamed x8, waiting for transfers between devices  59.4 us
    unnamed x54, local copies, waits for them, and re-layouts  47.7 us
    reshape x1, local copies, waits for them, and re-layouts, body(): voxels.reshape(windows, 4, 6, side_y, 6, side_z, 6)  44.1 us
    transpose x1, local copies, waits for them, and re-layouts, body(): local_patches = voxels.reshape(windows, 4, 6, side_y, 6, side_z, 6).trans...  34.5 us
    all_to_all x1, blocking collectives, heads_grad(): lax.all_to_all(for_sending(result), 'space', split_axis=1, concat_axis=3,...  27.6 us
  transfers between devices with their start and end apart: 9, of which 5 were waited for; matrix products, arithmetic and copies ran while one was open for 26% of the time, Pallas kernels for 0%

commit v1 on v0

--- a/solution.py
+++ b/solution.py
@@ -2,6 +2,8 @@
 import jax.numpy as jnp
 from jax import lax
 from jax.sharding import PartitionSpec as P
+from jax.experimental import pallas as pl
+from jax.experimental.pallas import tpu as pltpu
 
 D = 1024
 HD = 64
@@ -34,54 +36,74 @@
     return jnp.where(slots >= 0, owner_of * capacity + position, slab_count * capacity)
 
 
-def head_grads(queries, key_rows, value_rows, upstream):
-    length = queries.shape[0]
-    block_rows = min(512, length)
+QUERY_BLOCK = 256
+
+
+def attention_kernel(q_ref, k_ref, v_ref, g_ref, dq_ref, dk_ref, dv_ref, dk_acc, dv_acc):
+    step = pl.program_id(1)
     factor = HD ** (-0.5)
-    query_blocks = queries.reshape(length // block_rows, block_rows, HD)
-    upstream_blocks = upstream.reshape(length // block_rows, block_rows, HD)
-
-    def step(carried, inputs):
-        key_acc, value_acc = carried
-        query_part, upstream_part = inputs
-        scores = contract(query_part, key_rows, 1, 1) * factor
-        raised = jnp.exp(scores - jnp.max(scores, axis=1, keepdims=True))
-        attention = raised / jnp.sum(raised, axis=1, keepdims=True)
-        d_attention = contract(upstream_part, value_rows, 1, 1)
-        inner_sum = jnp.sum(attention * d_attention, axis=1, keepdims=True)
-        d_scores = (attention * (d_attention - inner_sum) * factor).astype(jnp.bfloat16)
-        grad_query = contract(d_scores, key_rows, 1, 0).astype(jnp.bfloat16)
-        key_acc = key_acc + contract(d_scores, query_part, 0, 0)
-        value_acc = value_acc + contract(attention.astype(jnp.bfloat16), upstream_part, 0, 0)
-        return ((key_acc, value_acc), grad_query)
-
-    zeros_acc = jnp.zeros((length, HD), jnp.float32)
-    (key_acc, value_acc), grad_blocks = lax.scan(
-        step, (zeros_acc, zeros_acc), (query_blocks, upstream_blocks)
-    )
-    return (
-        grad_blocks.reshape(length, HD),
-        key_acc.astype(jnp.bfloat16),
-        value_acc.astype(jnp.bfloat16),
-    )
-
-
-def window_grads(lanes, upstream):
-    grad_query, grad_key, grad_value = head_grads(
-        lanes[:, 0, 0:HD], lanes[:, 1, 0:HD], lanes[:, 2, 0:HD], upstream[:, 0, 0:HD]
-    )
-    pieces = [jnp.stack([grad_query, grad_key, grad_value], axis=1)]
-    return jnp.concatenate(pieces, axis=2)
+
+    @pl.when(step == 0)
+    def _():
+        dk_acc[...] = jnp.zeros_like(dk_acc)
+        dv_acc[...] = jnp.zeros_like(dv_acc)
+
+    queries = q_ref[0]
+    key_rows = k_ref[0]
+    value_rows = v_ref[0]
+    upstream = g_ref[0]
+    scores = contract(queries, key_rows, 1, 1) * factor
+    raised = jnp.exp(scores - jnp.max(scores, axis=1, keepdims=True))
+    attention = raised / jnp.sum(raised, axis=1, keepdims=True)
+    d_attention = contract(upstream, value_rows, 1, 1)
+    inner_sum = jnp.sum(attention * d_attention, axis=1, keepdims=True)
+    d_scores = (attention * (d_attention - inner_sum) * factor).astype(jnp.bfloat16)
+    dq_ref[0] = contract(d_scores, key_rows, 1, 0).astype(jnp.bfloat16)
+    dk_acc[...] += contract(d_scores, queries, 0, 0)
+    dv_acc[...] += contract(attention.astype(jnp.bfloat16), upstream, 0, 0)
+
+    @pl.when(step == pl.num_programs(1) - 1)
+    def _():
+        dk_ref[0] = dk_acc[...].astype(jnp.bfloat16)
+        dv_ref[0] = dv_acc[...].astype(jnp.bfloat16)
+
+
+def attention_grads(queries, key_rows, value_rows, upstream):
+    windows, length, width = queries.shape
+    block = min(QUERY_BLOCK, length)
+    row_spec = pl.BlockSpec((1, block, width), lambda w, i: (w, i, 0))
+    full_spec = pl.BlockSpec((1, length, width), lambda w, i: (w, 0, 0))
+    shape = jax.ShapeDtypeStruct((windows, length, width), jnp.bfloat16)
+    flops = 10 * windows * length * length * width
+    return pl.pallas_call(
+        attention_kernel,
+        grid=(windows, length // block),
+        in_specs=[row_spec, full_spec, full_spec, row_spec],
+        out_specs=[row_spec, full_spec, full_spec],
+        out_shape=[shape, shape, shape],
+        scratch_shapes=[
+            pltpu.VMEM((length, width), jnp.float32),
+            pltpu.VMEM((length, width), jnp.float32),
+        ],
+        compiler_params=pltpu.CompilerParams(
+            dimension_semantics=("arbitrary", "arbitrary"),
+            vmem_limit_bytes=48 * 1024 * 1024,
+        ),
+        cost_estimate=pl.CostEstimate(
+            flops=flops,
+            transcendentals=windows * length * length,
+            bytes_accessed=7 * windows * length * width * 2,
+        ),
+    )(queries, key_rows, value_rows, upstream)
 
 
 def heads_grad(exchanged):
     lanes, upstream = exchanged
-    result = jax.vmap(window_grads)(lanes, upstream)
-    return jax.tree.map(
-        lambda part, own: part.astype(own.dtype),
-        lax.all_to_all(for_sending(result), "space", split_axis=1, concat_axis=3, tiled=True),
-        result,
-    )
+    grad_query, grad_key, grad_value = attention_grads(
+        lanes[:, :, 0, :], lanes[:, :, 1, :], lanes[:, :, 2, :], upstream[:, :, 0, :]
+    )
+    result = jnp.stack([grad_query, grad_key, grad_value], axis=2)
+    return lax.all_to_all(result, "space", split_axis=1, concat_axis=3, tiled=True)
 
 
 def body(voxels, brain_list, owner_slot, embed_weight, qkv_weight, cotangent):
@@ -157,15 +179,19 @@
         )
     ).reshape(row_total, 3 * D)
     d_hidden = contract(d_packed, lax.all_gather(wide_rows, "space", axis=0, tiled=True), 1, 1)
-    section = hidden
-    my_rows = lax.psum_scatter(
-        contract(section, d_packed, 0, 0).astype(jnp.bfloat16),
-        "space",
-        scatter_dimension=0,
-        tiled=True,
-    )
-    d_qkv_weight = lax.psum_scatter(my_rows, "tm", scatter_dimension=1, tiled=True).astype(
-        jnp.float32
+    tm_count = lax.axis_size("tm")
+    partial = contract(hidden, d_packed, 0, 0).astype(jnp.bfloat16)
+    row_block = D // slab_count
+    col_block = 3 * D // tm_count
+    blocks = (
+        partial.reshape(slab_count, row_block, tm_count, col_block)
+        .transpose(0, 2, 1, 3)
+        .reshape(slab_count * tm_count, row_block, col_block)
+    )
+    d_qkv_weight = (
+        lax.psum_scatter(blocks, ("space", "tm"), scatter_dimension=0, tiled=True)
+        .reshape(row_block, col_block)
+        .astype(jnp.float32)
     )
     first_mean = jnp.mean(d_hidden, axis=1, keepdims=True)
     second_mean = jnp.mean(d_hidden * normed, axis=1, keepdims=True)

time: 818 us -> 796 us (0.973)
  matrix products: 201 us -> 17.6 us
  waiting for transfers between devices: 243 us -> 335 us
  Pallas kernels: 0 us -> 37.4 us
  local copies, waits for them, and re-layouts: 222 us -> 257 us
    dot_general x18 -> x2, matrix products: 161 us -> 6.68 us  [contract(): lax.dot_general(left, right, (((left_dim,), (right_dim,)), ((), ())), pre...]
    reduce_scatter x1, waiting for transfers between devices: 83.5 us -> 215 us  [body(): lax.psum_scatter(blocks, ('space', 'tm'), scatter_dimension=0, tiled=True)]
    pallas_call x0 -> x1, Pallas kernels: none -> 37.4 us  [attention_grads(): pl.pallas_call(attention_kernel, grid=(windows, length // block), in_spec...]
    unnamed x8 -> x6, waiting for transfers between devices: 59.4 us -> 27.7 us
    sub x4 -> x0, matrix products: 27.3 us -> none  [step(): raised = jnp.exp(scores - jnp.max(scores, axis=1, keepdims=True))]
    another operation x6, local copies, waits for them, and re-layouts: 8.58 us -> 29.1 us  [the longest x1 28.4 us: heads_grad(): result = jnp.stack([grad_query, grad_key, grad_value], axis=2)]
    unnamed x54 -> x30, local copies, waits for them, and re-layouts: 47.7 us -> 50.4 us
    another operation x6 -> x5, other arithmetic: 22.2 us -> 20.2 us
  transfers between devices with their start and end apart: 9 -> 8, of which waited for: 5 -> 4; matrix products, arithmetic and copies ran while one was open for 26% -> 27% of each run, Pallas kernels for 0% -> 0%
where the time goes in v1:
time: 796 us; the launch traced here: 784 us
  waiting for transfers between devices  335 us (42%)
  local copies, waits for them, and re-layouts  257 us (32%)
  blocking collectives  77.9 us (10%)
  Pallas kernels  37.4 us (5%)
  other arithmetic  25.4 us (3%)
  starting transfers between devices  18.5 us (2%)
  matrix products  17.6 us (2%)
  between operations  14.7 us (2%)
    reduce_scatter x1, waiting for transfers between devices, body(): lax.psum_scatter(blocks, ('space', 'tm'), scatter_dimension=0, tiled=True)  215 us
    psum x1, waiting for transfers between devices, body(): d_embed_weight = lax.psum(embed_cols_sum, 'space').astype(jnp.float32)  79 us
    unnamed x30, local copies, waits for them, and re-layouts  50.4 us
    reshape x1, local copies, waits for them, and re-layouts, body(): voxels.reshape(windows, 4, 6, side_y, 6, side_z, 6)  44.1 us
    pallas_call x1, Pallas kernels, attention_grads(): pl.pallas_call(attention_kernel, grid=(windows, length // block), in_spec...  37.4 us
    transpose x1, local copies, waits for them, and re-layouts, body(): local_patches = voxels.reshape(windows, 4, 6, side_y, 6, side_z, 6).trans...  34.5 us
    another operation x1, local copies, waits for them, and re-layouts, heads_grad(): result = jnp.stack([grad_query, grad_key, grad_value], axis=2)  28.4 us
    all_to_all x1, blocking collectives, heads_grad(): lax.all_to_all(result, 'space', split_axis=1, concat_axis=3, tiled=True)  27.7 us
  transfers between devices with their start and end apart: 8, of which 4 were waited for; matrix products, arithmetic and copies ran while one was open for 27% of the time, Pallas kernels for 0%

profile of v1, /device:TPU:1, one launch (start us, length us, event | category | flops | bytes accessed | tf_op | source)
XLA Modules:
  0.0 784.0 jit_solution(3437816802953976337)
XLA Ops:
  8.0 16.0 %all_gather.15 = bf16[64,3072]{1,0:T(8,128)(2,1)} all-gather(bf16[64,384]{1,0:T(8,128)(2,1)} %param.10), channel_id=1, replica_groups=mesh['space'=16,'tm'=8] {'tm'}, dimensions={1}, use_global_device_ids=true | all-gather | bytes 442368 | tf_op jit(solution)/shard_map/all_gather | solution.py:166
  24.0 20.6 %all_gather.14 = s32[2,4096]{1,0:T(2,128)S(1)} all-gather(s32[2,256]{1,0:T(2,128)} %param.8), channel_id=1, replica_groups=mesh['space'=16,'tm'=8] {'space'}, dimensions={1}, use_global_device_ids=true | all-gather | bytes 34816 | tf_op jit(solution)/shard_map/all_gather | solution.py:133
  44.8 18.1 %reduce-window.16 = s32[2,16,16,2,128]{4,2,3,1,0:T(8,128)S(1)} reduce-window(s32[2,16,16,2,128]{4,2,3,1,0:T(8,128)S(1)} %fusion.18, s32[]{:T(128)} %constant.85.clone.1), window={size=1x1x1x1x128 pad=0_0x0_0x0_0x0_0x127_0}, to_apply=%region_4.5 | reduce-window | flops 16646144 | bytes 1048580 | tf_op jit(solution)/shard_map/reduce-window.2
  63.9 1.2 reduce-window.14
  65.5 24.7 %scatter_fusion = s32[2,192]{1,0:T(2,128)S(1)} fusion(s32[2,192]{1,0:T(2,128)S(1)} %broadcast_in_dim.49, s32[512]{0:T(512)S(1)} %bitcast.219, s32[512]{0:T(512)S(1)} %bitcast.246), kind=kCustom, calls=%fused_computation.3 | custom fusion | bytes 10240 | tf_op jit(solution)/shard_map/scatter | solution.py:128
  90.3 3.7 gather_fusion
  94.2 44.1 %reshape.338 = bf16[2,4,6,16,6,16,6]{6,5,4,3,1,2,0:T(8,128)(2,1)} reshape(bf16[2,4,6,9216]{3,1,2,0:T(4,128)(2,1)S(1)} %copy-done.2) | data formatting | bytes 1769472 | tf_op jit(solution)/shard_map/reshape | solution.py:118
  138.3 34.5 %copy.45 = bf16[2,16,16,4,6,6,6]{2,1,6,5,4,3,0:T(8,128)(2,1)} copy(bf16[2,16,16,4,6,6,6]{6,2,5,1,3,4,0:T(8,128)(2,1)} %bitcast.217) | data formatting | bytes 1769472 | tf_op jit(solution)/shard_map/transpose | solution.py:119
  172.7 8.6 %reshape.339 = bf16[2,256,864]{1,2,0:T(8,128)(2,1)S(1)} reshape(bf16[2,16,16,4,6,6,6]{2,1,6,5,4,3,0:T(8,128)(2,1)} %copy.45) | data formatting | bytes 1769472 | tf_op jit(solution)/shard_map/reshape | solution.py:120
  182.0 5.1 gather_fusion.1
  187.6 2.6 fusion.5
  190.2 1.7 copy.47
  191.9 4.6 all-to-all-start
  196.8 1.1 copy.56
  198.0 30.4 %scatter_custom_fusion.2 = s32[256]{0:T(256)S(1)} fusion(s32[8192]{0:T(1024)S(1)} %bitcast.245, s32[8192]{0:T(1024)S(1)} %bitcast.244, s32[]{:T(128)} %constant.85.clone.1), kind=kCustom, calls=%fused_computation.124 | custom fusion | bytes 1028
  228.4 6.8 all-to-all-start.2
  235.4 2.8 gather_fusion.2
  238.6 5.8 convolution_convert_fusion.1
  244.5 4.6 reshape.423
  249.1 4.1 copy.53
  253.2 6.7 all-to-all-start.1
  260.2 1.4 copy.58
  261.6 13.9 %all-to-all-done.1 = bf16[2,128,3,1024]{1,0,2,3:T(2,128)(2,1)S(1)} async-done(((bf16[2,128,3,1024]{1,0,2,3:T(2,128)(2,1)}), bf16[2,128,3,1024]{1,0,2,3:T(2,128)(2,1)S(1)}, u32[]{:S(2)}, u32[]{:S(2)}) %all-to-all-start.1) | async-done | bytes 1572896 | tf_op jit(solution)/shard_map/all_to_all | solution.py:177
  275.4 1.3 copy.54
  276.8 4.1 copy.55
  280.9 3.0 slice_bitcast_fusion
  284.0 37.4 %shard_map.77 = (bf16[2,2048,64]{2,1,0:T(8,128)(2,1)S(1)}, bf16[2,2048,64]{2,1,0:T(8,128)(2,1)S(1)}, bf16[2,2048,64]{2,1,0:T(8,128)(2,1)S(1)}) custom-call(bf16[2,2048,64]{2,1,0:T(8,128)(2,1)S(1)} %get-tuple-element.12.q_ref, bf16[2,2048,64]{2,1,0:T(8,128)(2,1)S(1)} %get-tuple-element.11.k_ref, bf16[2,2048,64]{2,1,0:T(8,128)(2,1)} %get-tuple-element.10.v_ref, ...), custom_call_target="tpu_custom_call" | custom-call | flops 5368709120 | bytes 3670016 | tf_op jit(solution)/shard_map/pallas_call | solution.py:78
  322.2 28.4 %copy.102 = bf16[2,2048,3,64]{3,0,2,1:T(2,128)(2,1)} copy(bf16[2,2048,3,64]{3,1,0,2:T(8,128)(2,1)S(1)} %pad_maximum_fusion) | data formatting | bytes 3145728 | tf_op jit(solution)/shard_map/stack | solution.py:105
  350.6 4.0 reshape.429
  354.6 27.7 %all_to_all.58 = bf16[16,2,24576]{2,1,0:T(2,128)(2,1)} all-to-all(bf16[16,2,24576]{2,1,0:T(2,128)(2,1)S(1)} %reshape.429), channel_id=1, replica_groups=mesh['space'=16,'tm'=8] {'space'}, dimensions={0} | all-to-all | bytes 3145728 | tf_op jit(solution)/shard_map/all_to_all | solution.py:106
  382.3 4.9 reshape.430
  387.2 7.3 copy.60
  394.6 4.8 fusion.54
  399.8 16.6 %scatter_fusion.1 = bf16[2,192,1024]{2,1,0:T(8,128)(2,1)S(1)} fusion(bf16[2,192,1024]{2,1,0:T(8,128)(2,1)S(1)} %broadcast_in_dim.108, s32[256]{0:T(256)S(1)} %get-tuple-element.13, bf16[256,1024]{1,0:T(8,128)(2,1)S(1)} %multiply_convert_fusion), kind=kCustom, calls=%fused_computation.4 | custom fusion | bytes 1574912 | tf_op jit(solution)/shard_map/scatter | solution.py:206
  416.4 0.8 copy.62
  417.3 13.6 %all_to_all.59 = bf16[2,16,12,1024]{3,0,2,1:T(2,128)(2,1)S(1)} all-to-all(bf16[2,16,12,1024]{3,0,2,1:T(2,128)(2,1)S(1)} %bitcast.232), channel_id=1, replica_groups=mesh['space'=16,'tm'=8] {'space'}, dimensions={1} | all-to-all | bytes 1572864 | tf_op jit(solution)/shard_map/all_to_all | solution.py:208
  430.9 2.4 bitcast_convert_fusion
  433.3 3.8 copy.66
  437.4 1.9 convolution_convert_fusion
  439.3 4.3 copy.77
  443.6 26.9 %reduce-scatter.7.cloned.1.call-done = bf16[128,864]{1,0:T(8,128)(2,1)} async-done(((bf16[1024,864]{1,0:T(8,128)(2,1)}), bf16[128,864]{1,0:T(8,128)(2,1)}) %reduce-scatter.7.cloned.1.call-update) | async-done | bytes 221200
  470.5 1.8 copy.67
  472.3 3.5 bitcast_bitcast_fusion
  475.8 4.1 copy.61
  480.0 79.0 %all-reduce.2.cloned.1.call-done = bf16[864,128]{1,0:T(8,128)(2,1)} async-done(((bf16[864,128]{1,0:T(8,128)(2,1)}), bf16[864,128]{1,0:T(8,128)(2,1)}) %all-reduce.2.cloned.1.call-update) | async-done | bytes 221200 | tf_op jit(solution)/shard_map/psum | solution.py:221
  559.0 1.7 convert_element_type.86
  560.8 214.9 %reduce-scatter.5.cloned.1.call-done = bf16[1,64,384]{2,1,0:T(8,128)(2,1)} async-done(((bf16[128,64,384]{2,1,0:T(8,128)(2,1)}), bf16[1,64,384]{2,1,0:T(8,128)(2,1)}) %reduce-scatter.5.cloned.1.call-update) | async-done | bytes 49168 | tf_op jit(solution)/shard_map/reduce_scatter | solution.py:192
  775.6 1.4 bitcast_convert_fusion.1
  (83 shorter events, 6.3 us)
Async XLA Ops:
  7.2 83.1 %copy-start = (s32[2,256]{1,0:T(2,128)S(1)}, s32[2,256]{1,0:T(2,128)}, u32[]{:S(2)}) copy-start(s32[2,256]{1,0:T(2,128)} %param.7) | copy-start | bytes 6148
  7.2 56.6 %copy-start.6 = (s32[2,256]{1,0:T(2,128)S(1)}, s32[2,256]{1,0:T(2,128)}, u32[]{:S(2)}) copy-start(s32[2,256]{1,0:T(2,128)} %param.8) | copy-start | bytes 6148
  7.2 180.4 %all-gather.3.cloned.1.call-start = ((), (), s32[]{:S(2)}) async-start(), calls=%async_computation.7 | async-start | bytes 1990656 | tf_op jit(solution)/shard_map/all_gather | solution.py:151
  7.9 230.7 %all-gather.5.cloned.1.call-start = ((), (), s32[]{:S(2)}) async-start(), calls=%async_computation.8 | async-start | bytes 6684672 | tf_op jit(solution)/shard_map/all_gather | solution.py:170
  65.5 28.7 %copy-start.2 = (bf16[2,4,6,9216]{3,1,2,0:T(4,128)(2,1)S(1)}, bf16[2,4,6,9216]{3,1,2,0:T(4,128)(2,1)}, u32[]{:S(2)}) copy-start(bf16[2,4,6,9216]{3,1,2,0:T(4,128)(2,1)} %param.6) | copy-start | bytes 2654212
  187.1 4.7 copy-start.3
  187.6 9.0 %copy-start.8 = (s32[2]{0:T(128)S(1)}, s32[2]{0:T(128)}, u32[]{:S(2)}) copy-start(s32[2]{0:T(128)} %constant.101) | copy-start | bytes 28
  187.6 9.1 %copy-start.7 = (s32[2]{0:T(128)S(1)}, s32[2]{0:T(128)}, u32[]{:S(2)}) copy-start(s32[2]{0:T(128)} %constant.104) | copy-start | bytes 28
  187.6 9.2 %copy-start.5 = (bf16[2,1,128,1024]{3,2,1,0:T(8,128)(2,1)S(1)}, bf16[2,1,128,1024]{3,2,1,0:T(8,128)(2,1)}, u32[]{:S(2)}) copy-start(bf16[2,1,128,1024]{3,2,1,0:T(8,128)(2,1)} %param.11) | copy-start | bytes 1572868
  191.9 36.5 %all-to-all-start = ((bf16[2,16,12,1024]{3,0,2,1:T(2,128)(2,1)}), bf16[2,16,12,1024]{3,0,2,1:T(2,128)(2,1)S(1)}, u32[]{:S(2)}, u32[]{:S(2)}) async-start(bf16[2,16,12,1024]{3,0,2,1:T(2,128)(2,1)} %bitcast.6), calls=%async_computation | async-start | bytes 1572864 | tf_op jit(solution)/shard_map/all_to_all | solution.py:157
  228.4 24.8 %all-to-all-start.2 = ((bf16[2,128,1,1024]{1,0,2,3:T(2,128)(2,1)}), bf16[2,128,1,1024]{1,0,2,3:T(2,128)(2,1)S(1)}, u32[]{:S(2)}, u32[]{:S(2)}) async-start(bf16[2,128,1,1024]{1,0,2,3:T(2,128)(2,1)} %bitcast.23), calls=%async_computation.2 | async-start | bytes 1048576 | tf_op jit(solution)/shard_map/all_to_all | solution.py:178
  253.2 22.3 %all-to-all-start.1 = ((bf16[2,128,3,1024]{1,0,2,3:T(2,128)(2,1)}), bf16[2,128,3,1024]{1,0,2,3:T(2,128)(2,1)S(1)}, u32[]{:S(2)}, u32[]{:S(2)}) async-start(bf16[2,128,3,1024]{1,0,2,3:T(2,128)(2,1)} %copy.53), calls=%async_computation.1 | async-start | bytes 3145728 | tf_op jit(solution)/shard_map/all_to_all | solution.py:177
  259.8 210.7 %reduce-scatter.7.cloned.1.call-start = ((), (), s32[]{:S(2)}) async-start(), calls=%async_computation.11 | async-start | bytes 2064384
  416.4 14.4 %copy-start.4 = (bf16[384,864]{1,0:T(8,128)(2,1)S(1)}, bf16[384,864]{1,0:T(8,128)(2,1)}, u32[]{:S(2)}) copy-start(bf16[384,864]{1,0:T(8,128)(2,1)} %copy-done.3) | copy-start | bytes 1990660
  437.1 121.9 %all-reduce.2.cloned.1.call-start = ((), (), s32[]{:S(2)}) async-start(), calls=%async_computation.10 | async-start | bytes 442368 | tf_op jit(solution)/shard_map/psum | solution.py:221
  472.3 303.3 %reduce-scatter.5.cloned.1.call-start = ((), (), s32[]{:S(2)}) async-start(), calls=%async_computation.9 | async-start | bytes 6340608 | tf_op jit(solution)/shard_map/reduce_scatter | solution.py:192
  480.0 297.1 %copy-start.1 = (s32[2,256]{1,0:T(2,128)S(1)}, s32[2,256]{1,0:T(2,128)}, u32[]{:S(2)}) copy-start(s32[2,256]{1,0:T(2,128)} %param.7) | copy-start | bytes 6148
Sparse Core Ops, SparseCore 0:
  9.7 29.1 all-gather.2
  41.1 61.7 all-gather.4
  437.2 33.2 reduce-scatter.6
  474.1 84.8 all-reduce.1
  563.8 211.7 reduce-scatter.4

commit v2 on v1

--- a/solution.py
+++ b/solution.py
@@ -28,11 +28,18 @@
     )
 
 
+def select(onehot, rows):
+    return jnp.einsum("wab,wbc->wac", onehot, rows, preferred_element_type=jnp.float32)
+
+
 def bucket_index(slots, slab_count, capacity):
+    entries = slots.shape[-1]
     owner_of = jnp.where(slots >= 0, slots // OWN, slab_count)
-    hits = (owner_of[..., None] == jnp.arange(slab_count, dtype=jnp.int32)).astype(jnp.int32)
-    earlier = jnp.cumsum(hits, axis=-2) - hits
-    position = jnp.sum(earlier * hits, axis=-1)
+    hits = (owner_of[..., None] == jnp.arange(slab_count, dtype=jnp.int32)).astype(jnp.bfloat16)
+    order = jnp.arange(entries, dtype=jnp.int32)
+    before = (order[None, :] < order[:, None]).astype(jnp.bfloat16)
+    earlier = jnp.einsum("ij,wjo->wio", before, hits, preferred_element_type=jnp.float32)
+    position = jnp.sum(earlier * hits.astype(jnp.float32), axis=-1).astype(jnp.int32)
     return jnp.where(slots >= 0, owner_of * capacity + position, slab_count * capacity)
 
 
@@ -108,8 +115,9 @@
 
 def body(voxels, brain_list, owner_slot, embed_weight, qkv_weight, cotangent):
     slab_count = lax.axis_size("space")
-    my_slab = lax.axis_index("space")
+    tm_count = lax.axis_size("tm")
     capacity = 3 * OWN // (2 * slab_count)
+    buckets = slab_count * capacity
     windows = voxels.shape[0]
     row_total = windows * OWN
     side_y = GY // 6
@@ -119,57 +127,43 @@
         .transpose(0, 3, 5, 1, 2, 4, 6)
         .reshape(windows, side_y * side_z, PATCH)
     )
-    window_rows = jnp.arange(windows, dtype=jnp.int32)[:, None]
     my_buckets = bucket_index(owner_slot, slab_count, capacity)
-    entries = jnp.broadcast_to(jnp.arange(PSLAB, dtype=jnp.int32)[None, :], (windows, PSLAB))
-    sender = (
-        jnp.full((windows, slab_count * capacity), -1, jnp.int32)
-        .at[window_rows, my_buckets]
-        .set(entries, mode="drop")
-    )
-    patch_id = brain_list[window_rows, jnp.maximum(sender, 0)]
-    patch_rows = local_patches[window_rows, jnp.maximum(patch_id, 0)]
-    patch_rows = jnp.where((sender >= 0)[:, :, None], patch_rows, jnp.zeros_like(patch_rows))
-    all_slots = lax.all_gather(owner_slot, "space", axis=1, tiled=True).reshape(
-        windows, slab_count, PSLAB
-    )
-    their_buckets = bucket_index(all_slots, slab_count, capacity)
-    arrival = (
-        jnp.arange(slab_count, dtype=jnp.int32)[None, :, None] * capacity + their_buckets % capacity
-    )
-    mine_flag = (all_slots >= 0) & (all_slots // OWN == my_slab)
-    target = jnp.where(mine_flag, all_slots % OWN, OWN)
-    placement = (
-        jnp.zeros((windows, OWN), jnp.int32)
-        .at[window_rows[:, :, None], target]
-        .set(arrival, mode="drop")
-    )
-    sent_tokens = (
-        jnp.einsum(
-            "wnp,pd->wnd",
-            patch_rows,
-            lax.all_gather(embed_weight, "tm", axis=1, tiled=True),
-            preferred_element_type=jnp.float32,
-        )
-        .astype(jnp.bfloat16)
-        .reshape(windows, slab_count, capacity, D)
-    )
-    arrived = lax.all_to_all(sent_tokens, "space", split_axis=1, concat_axis=1, tiled=True).reshape(
-        windows, slab_count * capacity, D
-    )
-    tokens = arrived[window_rows, placement]
-    widened = tokens.reshape(row_total, D).astype(jnp.float32)
+    to_bucket = (
+        my_buckets[:, None, :] == jnp.arange(buckets, dtype=jnp.int32)[None, :, None]
+    ).astype(jnp.bfloat16)
+    is_patch = (
+        brain_list[:, :, None] == jnp.arange(PSLAB, dtype=jnp.int32)[None, None, :]
+    ).astype(jnp.bfloat16)
+    picks = select(to_bucket, is_patch).astype(jnp.bfloat16)
+    slot_code = (jnp.where(owner_slot >= 0, owner_slot % OWN, -1) + 1).astype(jnp.bfloat16)
+    bucket_code = select(to_bucket, slot_code[:, :, None])
+    width = -(-(PATCH + 1) // 128) * 128
+    payload = jnp.concatenate(
+        [
+            select(picks, local_patches).astype(jnp.bfloat16),
+            bucket_code.astype(jnp.bfloat16),
+            jnp.zeros((windows, buckets, width - PATCH - 1), jnp.bfloat16),
+        ],
+        axis=2,
+    ).reshape(windows, slab_count, capacity, width)
+    arrived = lax.all_to_all(payload, "space", split_axis=1, concat_axis=1, tiled=True).reshape(
+        windows, buckets, width
+    )
+    arrival_slot = arrived[:, :, PATCH].astype(jnp.int32) - 1
+    to_slot = (
+        arrival_slot[:, None, :] == jnp.arange(OWN, dtype=jnp.int32)[None, :, None]
+    ).astype(jnp.bfloat16)
+    chosen = select(to_slot, arrived[:, :, :PATCH]).astype(jnp.bfloat16).reshape(row_total, PATCH)
+    full_embed = lax.all_gather(embed_weight, "tm", axis=1, tiled=True)
+    tokens = jnp.dot(chosen, full_embed, preferred_element_type=jnp.float32).astype(jnp.bfloat16)
+    widened = tokens.astype(jnp.float32)
     center = widened - jnp.mean(widened, axis=1, keepdims=True)
     inverse = lax.rsqrt(jnp.mean(center * center, axis=1, keepdims=True) + 1e-05)
     normed = center * inverse
     hidden = normed.astype(jnp.bfloat16)
     wide_rows = lax.all_gather(qkv_weight, "tm", axis=1, tiled=True)
-    section = hidden
-    packed = jnp.dot(
-        section,
-        lax.all_gather(wide_rows, "space", axis=0, tiled=True),
-        preferred_element_type=jnp.float32,
-    ).astype(jnp.bfloat16)
+    full_qkv = lax.all_gather(wide_rows, "space", axis=0, tiled=True)
+    packed = jnp.dot(hidden, full_qkv, preferred_element_type=jnp.float32).astype(jnp.bfloat16)
     lanes_in = packed.reshape(windows, OWN, 3, D)
     upstream_in = cotangent.reshape(windows, OWN, 1, D)
     d_packed = heads_grad(
@@ -178,47 +172,37 @@
             lax.all_to_all(upstream_in, "space", split_axis=3, concat_axis=1, tiled=True),
         )
     ).reshape(row_total, 3 * D)
-    d_hidden = contract(d_packed, lax.all_gather(wide_rows, "space", axis=0, tiled=True), 1, 1)
-    tm_count = lax.axis_size("tm")
-    partial = contract(hidden, d_packed, 0, 0).astype(jnp.bfloat16)
-    row_block = D // slab_count
-    col_block = 3 * D // tm_count
-    blocks = (
-        partial.reshape(slab_count, row_block, tm_count, col_block)
-        .transpose(0, 2, 1, 3)
-        .reshape(slab_count * tm_count, row_block, col_block)
-    )
-    d_qkv_weight = (
-        lax.psum_scatter(blocks, ("space", "tm"), scatter_dimension=0, tiled=True)
-        .reshape(row_block, col_block)
-        .astype(jnp.float32)
-    )
+    my_rows = lax.psum_scatter(
+        contract(hidden, d_packed, 0, 0).astype(jnp.bfloat16),
+        "space",
+        scatter_dimension=0,
+        tiled=True,
+    )
+    d_qkv_weight = lax.psum_scatter(my_rows, "tm", scatter_dimension=1, tiled=True).astype(
+        jnp.float32
+    )
+    d_hidden = contract(d_packed, full_qkv, 1, 1)
     first_mean = jnp.mean(d_hidden, axis=1, keepdims=True)
     second_mean = jnp.mean(d_hidden * normed, axis=1, keepdims=True)
-    d_tokens = (
-        (inverse * (d_hidden - first_mean - normed * second_mean))
-        .astype(jnp.bfloat16)
-        .reshape(windows, OWN, D)
-    )
-    returned = (
-        jnp.zeros((windows, slab_count * capacity, D), jnp.bfloat16)
-        .at[window_rows, placement]
-        .set(d_tokens)
-    )
-    came_back = lax.all_to_all(
-        returned.reshape(windows, slab_count, capacity, D),
+    d_tokens = (inverse * (d_hidden - first_mean - normed * second_mean)).astype(jnp.bfloat16)
+    embed_partial = contract(chosen, d_tokens, 0, 0)
+    embed_cols = lax.psum_scatter(
+        embed_partial.astype(jnp.bfloat16), "tm", scatter_dimension=1, tiled=True
+    )
+    chunk = -(-PATCH // slab_count)
+    padded = jnp.pad(embed_cols, ((0, chunk * slab_count - PATCH), (0, 0)))
+    spread = lax.all_to_all(
+        padded.reshape(slab_count, chunk, -1), "space", split_axis=0, concat_axis=0, tiled=True
+    )
+    reduced = jnp.sum(spread.astype(jnp.float32), axis=0)
+    gathered = lax.all_to_all(
+        jnp.broadcast_to(reduced[None], (slab_count,) + reduced.shape),
         "space",
-        split_axis=1,
-        concat_axis=1,
+        split_axis=0,
+        concat_axis=0,
         tiled=True,
-    ).reshape(windows, slab_count * capacity, D)
-    embed_partial = jnp.einsum(
-        "wnp,wnd->pd", patch_rows, came_back, preferred_element_type=jnp.float32
-    )
-    embed_cols_sum = lax.psum_scatter(
-        embed_partial.astype(jnp.bfloat16), "tm", scatter_dimension=1, tiled=True
-    )
-    d_embed_weight = lax.psum(embed_cols_sum, "space").astype(jnp.float32)
+    )
+    d_embed_weight = gathered.reshape(chunk * slab_count, -1)[:PATCH]
     return (d_qkv_weight, d_embed_weight)
 
 

time: 796 us -> 462 us (0.58); the launches traced: 784 us -> 459 us
  waiting for transfers between devices: 335 us -> 139 us
  local copies, waits for them, and re-layouts: 257 us -> 157 us
  other arithmetic: 25.4 us -> 4.91 us
  blocking collectives: 77.9 us -> 65.6 us
    reduce_scatter x1, waiting for transfers between devices: 215 us -> 71.6 us  [body(): lax.psum_scatter(contract(hidden, d_packed, 0, 0).astype(jnp.bfloat16), '...]
    psum x1 -> x0, waiting for transfers between devices: 79 us -> none  [body(): d_embed_weight = lax.psum(embed_cols_sum, 'space').astype(jnp.float32)]
    scatter x3 -> x0, local copies, waits for them, and re-layouts: 42.1 us -> none  [the longest x1 24.7 us: body(): sender = jnp.full((windows, slab_count * capacity), -1, jnp.int32).at[win...]
    unnamed x30 -> x24, local copies, waits for them, and re-layouts: 50.4 us -> 17 us
    all_gather x1 -> x0, blocking collectives: 20.6 us -> none  [body(): lax.all_gather(owner_slot, 'space', axis=1, tiled=True)]
    another operation x4 -> x0, other arithmetic: 19.5 us -> none
    all_to_all x1 -> x2, blocking collectives: 13.6 us -> 25.5 us  [the longest x1 13.7 us: body(): lax.all_to_all(padded.reshape(slab_count, chunk, -1), 'space', split_axis...]
    gather x3 -> x0, local copies, waits for them, and re-layouts: 11.6 us -> none  [the longest x1 5.15 us: body(): patch_rows = local_patches[window_rows, jnp.maximum(patch_id, 0)]]
  transfers between devices with their start and end apart: 8 -> 8, of which waited for: 4 -> 5; matrix products, arithmetic and copies ran while one was open for 27% -> 27% of each run, Pallas kernels for 0% -> 0%
where the time goes in v2:
time: 462 us; the launch traced here: 459 us
  local copies, waits for them, and re-layouts  157 us (34%)
  waiting for transfers between devices  139 us (30%)
  blocking collectives  65.6 us (14%)
  Pallas kernels  37.1 us (8%)
  matrix products  21.8 us (5%)
  starting transfers between devices  19.1 us (4%)
  between operations  14.1 us (3%)
  other arithmetic  4.91 us (1%)
    reduce_scatter x1, waiting for transfers between devices, body(): lax.psum_scatter(contract(hidden, d_packed, 0, 0).astype(jnp.bfloat16), '...  71.6 us
    reshape x1, local copies, waits for them, and re-layouts, body(): voxels.reshape(windows, 4, 6, side_y, 6, side_z, 6)  44.1 us
    unnamed x7, waiting for transfers between devices  38.2 us
    pallas_call x1, Pallas kernels, attention_grads(): pl.pallas_call(attention_kernel, grid=(windows, length // block), in_spec...  37.1 us
    transpose x1, local copies, waits for them, and re-layouts, body(): local_patches = voxels.reshape(windows, 4, 6, side_y, 6, side_z, 6).trans...  34.5 us
    another operation x1, local copies, waits for them, and re-layouts, heads_grad(): result = jnp.stack([grad_query, grad_key, grad_value], axis=2)  28.6 us
    all_to_all x1, blocking collectives, heads_grad(): lax.all_to_all(result, 'space', split_axis=1, concat_axis=3, tiled=True)  24 us
    all_to_all x1, waiting for transfers between devices, body(): lax.all_to_all(lanes_in, 'space', split_axis=3, concat_axis=1, tiled=True)  19 us
  transfers between devices with their start and end apart: 8, of which 5 were waited for; matrix products, arithmetic and copies ran while one was open for 27% of the time, Pallas kernels for 0%

profile of v2, /device:TPU:1, one launch (start us, length us, event | category | flops | bytes accessed | tf_op | source)
XLA Modules:
  0.0 459.1 jit_solution(7141499755209994228)
XLA Ops:
  7.2 0.7 all-gather.3.cloned.1.call-update
  8.0 16.0 %all_gather.10 = bf16[64,3072]{1,0:T(8,128)(2,1)} all-gather(bf16[64,384]{1,0:T(8,128)(2,1)} %param.10), channel_id=1, replica_groups=mesh['space'=16,'tm'=8] {'tm'}, dimensions={1}, use_global_device_ids=true | all-gather | bytes 442368 | tf_op jit(solution)/shard_map/all_gather | solution.py:164
  24.0 0.7 fusion.36
  24.9 0.7 fusion.37
  26.2 44.1 %reshape.75 = bf16[2,4,6,16,6,16,6]{6,5,4,3,1,2,0:T(8,128)(2,1)} reshape(bf16[2,4,6,9216]{3,1,2,0:T(4,128)(2,1)S(1)} %copy-done.5) | data formatting | bytes 1769472 | tf_op jit(solution)/shard_map/reshape | solution.py:126
  70.3 34.5 %copy.48 = bf16[2,16,16,4,6,6,6]{2,1,6,5,4,3,0:T(8,128)(2,1)} copy(bf16[2,16,16,4,6,6,6]{6,2,5,1,3,4,0:T(8,128)(2,1)} %bitcast.75) | data formatting | bytes 1769472 | tf_op jit(solution)/shard_map/transpose | solution.py:127
  104.8 8.7 %reshape.76 = bf16[2,256,864]{1,2,0:T(8,128)(2,1)S(1)} reshape(bf16[2,16,16,4,6,6,6]{2,1,6,5,4,3,0:T(8,128)(2,1)} %copy.48) | data formatting | bytes 1769472 | tf_op jit(solution)/shard_map/reshape | solution.py:128
  113.5 0.6 convolution_convert_fusion.3
  114.1 0.7 copy.49
  114.9 1.8 maximum_maximum_fusion
  116.6 7.8 %all-to-all-start = ((bf16[2,16,12,896]{3,0,2,1:T(2,128)(2,1)}), bf16[2,16,12,896]{3,0,2,1:T(2,128)(2,1)S(1)}, u32[]{:S(2)}, u32[]{:S(2)}) async-start(bf16[2,16,12,896]{3,0,2,1:T(2,128)(2,1)} %maximum_maximum_fusion), calls=%async_computation | async-start | bytes 1376256 | tf_op jit(solution)/shard_map/all_to_all | solution.py:149
  124.4 1.1 copy.58
  125.5 10.5 %all-to-all-done = bf16[2,16,12,896]{3,0,2,1:T(2,128)(2,1)S(1)} async-done(((bf16[2,16,12,896]{3,0,2,1:T(2,128)(2,1)}), bf16[2,16,12,896]{3,0,2,1:T(2,128)(2,1)S(1)}, u32[]{:S(2)}, u32[]{:S(2)}) %all-to-all-start) | async-done | bytes 688160 | tf_op jit(solution)/shard_map/all_to_all | solution.py:149
  136.1 4.5 all-to-all-start.2
  140.8 0.6 convolution_convert_fusion.5
  141.7 2.4 convert_reduce_fusion
  145.0 5.8 %convolution_convert_fusion.1 = bf16[256,3072]{1,0:T(8,128)(2,1)} fusion(bf16[1024,3072]{1,0:T(8,128)(2,1)} %all-gather.5.cloned.1.call-done, bf16[256,1024]{1,0:T(8,128)(2,1)S(1)} %get-tuple-element.16, f32[256]{0:T(256)S(1)} %add_rsqrt_fusion, f32[256]{0:T(256)S(1)} %broadcast_multiply_fusion.2), kind=kOutput, calls=%fused_computation.1 | convolution fusion | flops 1612447744 | bytes 8390656 | tf_op jit(solution)/shard_map/dot_general | solution.py:166
  150.8 4.6 reshape.87
  155.4 4.1 copy.55
  159.5 6.7 %all-to-all-start.1 = ((bf16[2,128,3,1024]{1,0,2,3:T(2,128)(2,1)}), bf16[2,128,3,1024]{1,0,2,3:T(2,128)(2,1)S(1)}, u32[]{:S(2)}, u32[]{:S(2)}) async-start(bf16[2,128,3,1024]{1,0,2,3:T(2,128)(2,1)} %copy.55), calls=%async_computation.1 | async-start | bytes 3145728 | tf_op jit(solution)/shard_map/all_to_all | solution.py:171
  166.3 1.3 copy.60
  167.6 19.0 %all-to-all-done.1 = bf16[2,128,3,1024]{1,0,2,3:T(2,128)(2,1)S(1)} async-done(((bf16[2,128,3,1024]{1,0,2,3:T(2,128)(2,1)}), bf16[2,128,3,1024]{1,0,2,3:T(2,128)(2,1)S(1)}, u32[]{:S(2)}, u32[]{:S(2)}) %all-to-all-start.1) | async-done | bytes 1572896 | tf_op jit(solution)/shard_map/all_to_all | solution.py:171
  186.6 1.4 copy.56
  187.9 3.1 copy.57
  191.0 1.2 slice_bitcast_fusion
  192.2 37.1 %shard_map.77 = (bf16[2,2048,64]{2,1,0:T(8,128)(2,1)S(1)}, bf16[2,2048,64]{2,1,0:T(8,128)(2,1)S(1)}, bf16[2,2048,64]{2,1,0:T(8,128)(2,1)S(1)}) custom-call(bf16[2,2048,64]{2,1,0:T(8,128)(2,1)S(1)} %get-tuple-element.12.q_ref, bf16[2,2048,64]{2,1,0:T(8,128)(2,1)S(1)} %get-tuple-element.11.k_ref, bf16[2,2048,64]{2,1,0:T(8,128)(2,1)} %get-tuple-element.10.v_ref, ...), custom_call_target="tpu_custom_call" | custom-call | flops 5368709120 | bytes 3670016 | tf_op jit(solution)/shard_map/pallas_call | solution.py:85
  229.3 0.8 pad_maximum_fusion
  230.1 28.6 %copy.91 = bf16[2,2048,3,64]{3,0,2,1:T(2,128)(2,1)S(1)} copy(bf16[2,2048,3,64]{3,1,0,2:T(8,128)(2,1)S(1)} %pad_maximum_fusion) | data formatting | bytes 3145728 | tf_op jit(solution)/shard_map/stack | solution.py:112
  258.7 3.2 reshape.92
  261.9 24.0 %all_to_all.63 = bf16[16,2,24576]{2,1,0:T(2,128)(2,1)} all-to-all(bf16[16,2,24576]{2,1,0:T(2,128)(2,1)} %reshape.92), channel_id=1, replica_groups=mesh['space'=16,'tm'=8] {'space'}, dimensions={0} | all-to-all | bytes 3145728 | tf_op jit(solution)/shard_map/all_to_all | solution.py:113
  286.0 3.8 reshape.93
  289.8 6.2 %copy.62 = bf16[2,16,128,3,64]{2,0,4,1,3:T(2,128)(2,1)} copy(bf16[2,16,128,3,64]{4,0,3,2,1:T(2,128)(2,1)S(1)} %bitcast.78) | data formatting | bytes 3145728 | tf_op jit(solution)/shard_map/all_to_all | solution.py:113
  296.0 6.3 %convolution_convert_fusion = bf16[1024,3072]{1,0:T(8,128)(2,1)} fusion(bf16[384,8,2,128]{3,2,1,0:T(2,128)(2,1)} %bitcast.81, bf16[256,1024]{1,0:T(8,128)(2,1)} %copy-done, f32[256]{0:T(256)S(1)} %add_rsqrt_fusion, f32[256]{0:T(256)S(1)} %broadcast_multiply_fusion.2), kind=kOutput, calls=%fused_computation | convolution fusion | flops 1614807040 | bytes 8390656 | tf_op jit(solution)/shard_map/dot_general | solution.py:26
  302.3 1.0 copy-done.1
  303.3 0.5 copy-done.2
  303.8 4.8 %fusion.40 = (f32[256]{0:T(256)S(1)}, f32[256]{0:T(256)S(1)}, f32[256,1024]{1,0:T(8,128)S(1)}) fusion(f32[256]{0:T(256)S(1)} %add_rsqrt_fusion, f32[256]{0:T(256)S(1)} %broadcast_multiply_fusion.2, bf16[256,1024]{1,0:T(8,128)(2,1)S(1)} %copy-done.1, bf16[1024,3072]{1,0:T(8,128)(2,1)} %all-gather.5.cloned.1.call-done, bf16[384,8,2,128]{3,2,1,0:T(2,128)(2,1)S(1)} %bitcast.82), kind=kOutput, calls=%fused_computation.71 | convolution fusion | flops 1612185088 | bytes 9441280 | tf_op jit(solution)/shard_map/dot_general | solution.py:26
  308.6 0.9 convolution_convert_fusion.2
  309.5 2.5 copy.69
  312.1 71.6 %reduce-scatter.8.cloned.1.call-done = bf16[64,3072]{1,0:T(8,128)(2,1)} async-done(((bf16[1024,3072]{1,0:T(8,128)(2,1)}), bf16[64,3072]{1,0:T(8,128)(2,1)}) %reduce-scatter.8.cloned.1.call-update) | async-done | bytes 393232 | tf_op jit(solution)/shard_map/reduce_scatter | solution.py:175
  383.7 2.2 copy.67
  385.9 31.7 %reduce-scatter.12.cloned.1.call-done = bf16[128,864]{1,0:T(8,128)(2,1)} async-done(((bf16[1024,864]{1,0:T(8,128)(2,1)}), bf16[128,864]{1,0:T(8,128)(2,1)}) %reduce-scatter.12.cloned.1.call-update) | async-done | bytes 221200
  417.6 1.1 copy.70
  418.7 13.7 %all_to_all.64 = bf16[16,54,128]{2,1,0:T(8,128)(2,1)S(1)} all-to-all(bf16[16,54,128]{2,1,0:T(8,128)(2,1)S(1)} %reshape.82), channel_id=1, replica_groups=mesh['space'=16,'tm'=8] {'space'}, dimensions={0} | all-to-all | bytes 442368 | tf_op jit(solution)/shard_map/all_to_all | solution.py:194
  432.5 11.8 %all_to_all.65 = f32[16,54,128]{2,1,0:T(8,128)S(1)} all-to-all(f32[16,54,128]{2,1,0:T(8,128)S(1)} %broadcast_in_dim.15), channel_id=1, replica_groups=mesh['space'=16,'tm'=8] {'space'}, dimensions={0} | all-to-all | bytes 884736 | tf_op jit(solution)/shard_map/all_to_all | solution.py:198
  444.4 0.8 reshape.83
  445.1 5.8 %reduce-scatter.10.cloned.1.call-done = bf16[384,64]{1,0:T(8,128)(2,1)} async-done(((bf16[3072,64]{1,0:T(8,128)(2,1)}), bf16[384,64]{1,0:T(8,128)(2,1)}) %reduce-scatter.10.cloned.1.call-update) | async-done | bytes 49168
  450.9 1.0 copy.68
  451.9 0.7 convert_element_type.78
  (45 shorter events, 2.8 us)
Async XLA Ops:
  7.2 19.1 %copy-start.5 = (bf16[2,4,6,9216]{3,1,2,0:T(4,128)(2,1)S(1)}, bf16[2,4,6,9216]{3,1,2,0:T(4,128)(2,1)}, u32[]{:S(2)}) copy-start(bf16[2,4,6,9216]{3,1,2,0:T(4,128)(2,1)} %param.6) | copy-start | bytes 2654212
  7.2 134.5 %all-gather.3.cloned.1.call-start = ((), (), s32[]{:S(2)}) async-start(), calls=%async_computation.9 | async-start | bytes 1990656 | tf_op jit(solution)/shard_map/all_gather | solution.py:157
  7.9 136.6 %all-gather.5.cloned.1.call-start = ((), (), s32[]{:S(2)}) async-start(), calls=%async_computation.10 | async-start | bytes 6684672 | tf_op jit(solution)/shard_map/all_gather | solution.py:165
  104.8 8.7 %copy-start.7 = (s32[2,256]{1,0:T(2,128)S(1)}, s32[2,256]{1,0:T(2,128)}, u32[]{:S(2)}) copy-start(s32[2,256]{1,0:T(2,128)} %param.7) | copy-start | bytes 6148
  114.8 9.6 %copy-start.6 = (bf16[2,1,128,1024]{3,2,1,0:T(8,128)(2,1)S(1)}, bf16[2,1,128,1024]{3,2,1,0:T(8,128)(2,1)}, u32[]{:S(2)}) copy-start(bf16[2,1,128,1024]{3,2,1,0:T(8,128)(2,1)} %param.11) | copy-start | bytes 1572868
  116.6 19.4 %all-to-all-start = ((bf16[2,16,12,896]{3,0,2,1:T(2,128)(2,1)}), bf16[2,16,12,896]{3,0,2,1:T(2,128)(2,1)S(1)}, u32[]{:S(2)}, u32[]{:S(2)}) async-start(bf16[2,16,12,896]{3,0,2,1:T(2,128)(2,1)} %maximum_maximum_fusion), calls=%async_computation | async-start | bytes 1376256 | tf_op jit(solution)/shard_map/all_to_all | solution.py:149
  136.1 23.4 %all-to-all-start.2 = ((bf16[2,128,1,1024]{1,0,2,3:T(2,128)(2,1)}), bf16[2,128,1,1024]{1,0,2,3:T(2,128)(2,1)S(1)}, u32[]{:S(2)}, u32[]{:S(2)}) async-start(bf16[2,128,1,1024]{1,0,2,3:T(2,128)(2,1)} %bitcast.15), calls=%async_computation.2 | async-start | bytes 1048576 | tf_op jit(solution)/shard_map/all_to_all | solution.py:172
  141.7 2.8 copy-start.3
  144.1 0.9 copy-start
  159.5 27.1 %all-to-all-start.1 = ((bf16[2,128,3,1024]{1,0,2,3:T(2,128)(2,1)}), bf16[2,128,3,1024]{1,0,2,3:T(2,128)(2,1)S(1)}, u32[]{:S(2)}, u32[]{:S(2)}) async-start(bf16[2,128,3,1024]{1,0,2,3:T(2,128)(2,1)} %copy.55), calls=%async_computation.1 | async-start | bytes 3145728 | tf_op jit(solution)/shard_map/all_to_all | solution.py:171
  166.1 217.5 %reduce-scatter.8.cloned.1.call-start = ((), (), s32[]{:S(2)}) async-start(), calls=%async_computation.11 | async-start | bytes 6684672 | tf_op jit(solution)/shard_map/reduce_scatter | solution.py:175
  302.2 1.0 copy-start.1
  302.2 1.6 copy-start.2
  302.3 6.4 %copy-start.4 = (bf16[2,128,864]{2,1,0:T(8,128)(2,1)S(1)}, bf16[2,128,864]{2,1,0:T(8,128)(2,1)}, u32[]{:S(2)}) copy-start(bf16[2,128,864]{2,1,0:T(8,128)(2,1)} %copy-done.3) | copy-start | bytes 1327108
  302.3 115.3 %reduce-scatter.12.cloned.1.call-start = ((), (), s32[]{:S(2)}) async-start(), calls=%async_computation.13 | async-start | bytes 2064384
  312.0 138.9 %reduce-scatter.10.cloned.1.call-start = ((), (), s32[]{:S(2)}) async-start(), calls=%async_computation.12 | async-start | bytes 884736
Sparse Core Ops, SparseCore 0:
  9.7 29.1 all-gather.2
  41.1 61.8 all-gather.4
  302.4 81.2 reduce-scatter.7
  386.0 31.5 reduce-scatter.11
  419.8 31.0 reduce-scatter.9

commit v3 on v2

--- a/solution.py
+++ b/solution.py
@@ -46,51 +46,61 @@
 QUERY_BLOCK = 256
 
 
-def attention_kernel(q_ref, k_ref, v_ref, g_ref, dq_ref, dk_ref, dv_ref, dk_acc, dv_acc):
+def attention_kernel(lanes_ref, g_ref, out_ref, k_s, v_s, dk_acc, dv_acc):
     step = pl.program_id(1)
+    owners, _, slots, _ = lanes_ref.shape
+    per_block = g_ref.shape[0]
+    length = owners * slots
+    block = per_block * slots
     factor = HD ** (-0.5)
 
     @pl.when(step == 0)
     def _():
+        k_s[...] = lanes_ref[:, 0, :, HD : 2 * HD].reshape(length, HD)
+        v_s[...] = lanes_ref[:, 0, :, 2 * HD : 3 * HD].reshape(length, HD)
         dk_acc[...] = jnp.zeros_like(dk_acc)
         dv_acc[...] = jnp.zeros_like(dv_acc)
 
-    queries = q_ref[0]
-    key_rows = k_ref[0]
-    value_rows = v_ref[0]
-    upstream = g_ref[0]
+    first = pl.multiple_of(step * per_block, per_block)
+    queries = lanes_ref[pl.ds(first, per_block), 0, :, 0:HD].reshape(block, HD)
+    upstream = g_ref[:, 0, :, :].reshape(block, HD)
+    key_rows = k_s[...]
+    value_rows = v_s[...]
     scores = contract(queries, key_rows, 1, 1) * factor
     raised = jnp.exp(scores - jnp.max(scores, axis=1, keepdims=True))
     attention = raised / jnp.sum(raised, axis=1, keepdims=True)
     d_attention = contract(upstream, value_rows, 1, 1)
     inner_sum = jnp.sum(attention * d_attention, axis=1, keepdims=True)
     d_scores = (attention * (d_attention - inner_sum) * factor).astype(jnp.bfloat16)
-    dq_ref[0] = contract(d_scores, key_rows, 1, 0).astype(jnp.bfloat16)
+    grad_query = contract(d_scores, key_rows, 1, 0).astype(jnp.bfloat16)
+    out_ref[pl.ds(first, per_block), 0, :, 0:HD] = grad_query.reshape(per_block, slots, HD)
     dk_acc[...] += contract(d_scores, queries, 0, 0)
     dv_acc[...] += contract(attention.astype(jnp.bfloat16), upstream, 0, 0)
 
     @pl.when(step == pl.num_programs(1) - 1)
     def _():
-        dk_ref[0] = dk_acc[...].astype(jnp.bfloat16)
-        dv_ref[0] = dv_acc[...].astype(jnp.bfloat16)
-
-
-def attention_grads(queries, key_rows, value_rows, upstream):
-    windows, length, width = queries.shape
-    block = min(QUERY_BLOCK, length)
-    row_spec = pl.BlockSpec((1, block, width), lambda w, i: (w, i, 0))
-    full_spec = pl.BlockSpec((1, length, width), lambda w, i: (w, 0, 0))
-    shape = jax.ShapeDtypeStruct((windows, length, width), jnp.bfloat16)
-    flops = 10 * windows * length * length * width
+        out_ref[:, 0, :, HD : 2 * HD] = dk_acc[...].astype(jnp.bfloat16).reshape(owners, slots, HD)
+        out_ref[:, 0, :, 2 * HD : 3 * HD] = dv_acc[...].astype(jnp.bfloat16).reshape(owners, slots, HD)
+
+
+def attention_grads(lanes, upstream):
+    owners, windows, slots, width = lanes.shape
+    length = owners * slots
+    per_block = max(1, QUERY_BLOCK // slots)
+    lanes_spec = pl.BlockSpec((owners, 1, slots, width), lambda w, i: (0, w, 0, 0))
+    g_spec = pl.BlockSpec((per_block, 1, slots, HD), lambda w, i: (i, w, 0, 0))
+    flops = 10 * windows * length * length * HD
     return pl.pallas_call(
         attention_kernel,
-        grid=(windows, length // block),
-        in_specs=[row_spec, full_spec, full_spec, row_spec],
-        out_specs=[row_spec, full_spec, full_spec],
-        out_shape=[shape, shape, shape],
+        grid=(windows, owners // per_block),
+        in_specs=[lanes_spec, g_spec],
+        out_specs=lanes_spec,
+        out_shape=jax.ShapeDtypeStruct(lanes.shape, jnp.bfloat16),
         scratch_shapes=[
-            pltpu.VMEM((length, width), jnp.float32),
-            pltpu.VMEM((length, width), jnp.float32),
+            pltpu.VMEM((length, HD), jnp.bfloat16),
+            pltpu.VMEM((length, HD), jnp.bfloat16),
+            pltpu.VMEM((length, HD), jnp.float32),
+            pltpu.VMEM((length, HD), jnp.float32),
         ],
         compiler_params=pltpu.CompilerParams(
             dimension_semantics=("arbitrary", "arbitrary"),
@@ -99,18 +109,9 @@
         cost_estimate=pl.CostEstimate(
             flops=flops,
             transcendentals=windows * length * length,
-            bytes_accessed=7 * windows * length * width * 2,
+            bytes_accessed=7 * windows * length * HD * 2,
         ),
-    )(queries, key_rows, value_rows, upstream)
-
-
-def heads_grad(exchanged):
-    lanes, upstream = exchanged
-    grad_query, grad_key, grad_value = attention_grads(
-        lanes[:, :, 0, :], lanes[:, :, 1, :], lanes[:, :, 2, :], upstream[:, :, 0, :]
-    )
-    result = jnp.stack([grad_query, grad_key, grad_value], axis=2)
-    return lax.all_to_all(result, "space", split_axis=1, concat_axis=3, tiled=True)
+    )(lanes, upstream)
 
 
 def body(voxels, brain_list, owner_slot, embed_weight, qkv_weight, cotangent):
@@ -163,38 +164,56 @@
     hidden = normed.astype(jnp.bfloat16)
     wide_rows = lax.all_gather(qkv_weight, "tm", axis=1, tiled=True)
     full_qkv = lax.all_gather(wide_rows, "space", axis=0, tiled=True)
-    packed = jnp.dot(hidden, full_qkv, preferred_element_type=jnp.float32).astype(jnp.bfloat16)
-    lanes_in = packed.reshape(windows, OWN, 3, D)
-    upstream_in = cotangent.reshape(windows, OWN, 1, D)
-    d_packed = heads_grad(
-        (
-            lax.all_to_all(lanes_in, "space", split_axis=3, concat_axis=1, tiled=True),
-            lax.all_to_all(upstream_in, "space", split_axis=3, concat_axis=1, tiled=True),
-        )
-    ).reshape(row_total, 3 * D)
+    heads = D // HD
+    head_qkv = full_qkv.reshape(D, 3, heads, HD).transpose(0, 2, 1, 3).reshape(D, 3 * D)
+    packed = jnp.dot(hidden, head_qkv, preferred_element_type=jnp.float32).astype(jnp.bfloat16)
+    lanes_out = packed.reshape(windows, OWN, heads, 3 * HD).transpose(2, 0, 1, 3)
+    upstream_out = cotangent.reshape(windows, OWN, heads, HD).transpose(2, 0, 1, 3)
+    lanes = lax.all_to_all(lanes_out, "space", split_axis=0, concat_axis=0, tiled=True)
+    upstream = lax.all_to_all(upstream_out, "space", split_axis=0, concat_axis=0, tiled=True)
+    grads = attention_grads(lanes, upstream)
+    returned = lax.all_to_all(grads, "space", split_axis=0, concat_axis=0, tiled=True)
+    d_packed = (
+        returned.reshape(heads, windows, OWN, 3, HD)
+        .transpose(1, 2, 3, 0, 4)
+        .reshape(row_total, 3 * D)
+    )
     my_rows = lax.psum_scatter(
         contract(hidden, d_packed, 0, 0).astype(jnp.bfloat16),
         "space",
         scatter_dimension=0,
         tiled=True,
     )
-    d_qkv_weight = lax.psum_scatter(my_rows, "tm", scatter_dimension=1, tiled=True).astype(
-        jnp.float32
-    )
+    row_block = my_rows.shape[0]
+    col_block = 3 * D // tm_count
+    qkv_parts = lax.all_to_all(
+        my_rows.reshape(row_block, tm_count, col_block).transpose(1, 0, 2),
+        "tm",
+        split_axis=0,
+        concat_axis=0,
+        tiled=True,
+    )
+    d_qkv_weight = jnp.sum(qkv_parts.astype(jnp.float32), axis=0)
     d_hidden = contract(d_packed, full_qkv, 1, 1)
     first_mean = jnp.mean(d_hidden, axis=1, keepdims=True)
     second_mean = jnp.mean(d_hidden * normed, axis=1, keepdims=True)
     d_tokens = (inverse * (d_hidden - first_mean - normed * second_mean)).astype(jnp.bfloat16)
     embed_partial = contract(chosen, d_tokens, 0, 0)
-    embed_cols = lax.psum_scatter(
-        embed_partial.astype(jnp.bfloat16), "tm", scatter_dimension=1, tiled=True
-    )
+    embed_block = D // tm_count
+    embed_parts = lax.all_to_all(
+        embed_partial.astype(jnp.bfloat16).reshape(PATCH, tm_count, embed_block).transpose(1, 0, 2),
+        "tm",
+        split_axis=0,
+        concat_axis=0,
+        tiled=True,
+    )
+    embed_cols = jnp.sum(embed_parts.astype(jnp.float32), axis=0)
     chunk = -(-PATCH // slab_count)
     padded = jnp.pad(embed_cols, ((0, chunk * slab_count - PATCH), (0, 0)))
     spread = lax.all_to_all(
         padded.reshape(slab_count, chunk, -1), "space", split_axis=0, concat_axis=0, tiled=True
     )
-    reduced = jnp.sum(spread.astype(jnp.float32), axis=0)
+    reduced = jnp.sum(spread, axis=0)
     gathered = lax.all_to_all(
         jnp.broadcast_to(reduced[None], (slab_count,) + reduced.shape),
         "space",

time: 462 us -> 374 us (0.81)
  waiting for transfers between devices: 139 us -> 66.2 us
  local copies, waits for them, and re-layouts: 157 us -> 119 us
  blocking collectives: 65.6 us -> 83.8 us
  starting transfers between devices: 19.1 us -> 31.5 us
  matrix products: 21.8 us -> 16.3 us
    reduce_scatter x1, waiting for transfers between devices: 71.6 us -> 29.5 us  [body(): lax.psum_scatter(contract(hidden, d_packed, 0, 0).astype(jnp.bfloat16), '...]
    unnamed x7 -> x3, waiting for transfers between devices: 38.2 us -> 0.71 us
    another operation x1 -> x0, local copies, waits for them, and re-layouts: 28.6 us -> none  [heads_grad(): result = jnp.stack([grad_query, grad_key, grad_value], axis=2)]
    all_to_all x2, blocking collectives: 35.9 us -> 53.8 us  [the longest x1 30.8 us: body(): lax.all_to_all(embed_partial.astype(jnp.bfloat16).reshape(PATCH, tm_count...]
    unnamed x24 -> x18, local copies, waits for them, and re-layouts: 17 us -> 1.73 us
    all_to_all x2 -> x4, starting transfers between devices: 11.1 us -> 23.6 us  [the longest x1 6.64 us: body(): lax.all_to_all(lanes_out, 'space', split_axis=0, concat_axis=0, tiled=True)]
    all_gather x0 -> x1, local copies, waits for them, and re-layouts: none -> 8.64 us  [body(): full_qkv = lax.all_gather(wide_rows, 'space', axis=0, tiled=True)]
    all_to_all x5 -> x2, local copies, waits for them, and re-layouts: 12 us -> 4.26 us  [the longest x1 2.74 us: body(): lax.all_to_all(lanes_out, 'space', split_axis=0, concat_axis=0, tiled=True)]
  transfers between devices with their start and end apart: 8 -> 8, of which waited for: 5 -> 4; matrix products, arithmetic and copies ran while one was open for 27% -> 34% of each run, Pallas kernels for 0% -> 0%
where the time goes in v3:
time: 374 us; the launch traced here: 373 us
  local copies, waits for them, and re-layouts  119 us (32%)
  blocking collectives  83.8 us (22%)
  waiting for transfers between devices  66.2 us (18%)
  Pallas kernels  37.4 us (10%)
  starting transfers between devices  31.5 us (8%)
  matrix products  16.3 us (4%)
  between operations  14.1 us (4%)
  other arithmetic  4.42 us (1%)
    reshape x1, local copies, waits for them, and re-layouts, body(): voxels.reshape(windows, 4, 6, side_y, 6, side_z, 6)  44.1 us
    pallas_call x1, Pallas kernels, attention_grads(): pl.pallas_call(attention_kernel, grid=(windows, owners // per_block), in_...  37.4 us
    transpose x1, local copies, waits for them, and re-layouts, body(): local_patches = voxels.reshape(windows, 4, 6, side_y, 6, side_z, 6).trans...  34.5 us
    all_to_all x1, blocking collectives, body(): lax.all_to_all(embed_partial.astype(jnp.bfloat16).reshape(PATCH, tm_count...  30.8 us
    reduce_scatter x1, waiting for transfers between devices, body(): lax.psum_scatter(contract(hidden, d_packed, 0, 0).astype(jnp.bfloat16), '...  29.5 us
    all_to_all x1, blocking collectives, body(): lax.all_to_all(grads, 'space', split_axis=0, concat_axis=0, tiled=True)  23 us
    all_to_all x1, waiting for transfers between devices, body(): lax.all_to_all(lanes_out, 'space', split_axis=0, concat_axis=0, tiled=True)  18.5 us
    all_gather x1, blocking collectives, body(): wide_rows = lax.all_gather(qkv_weight, 'tm', axis=1, tiled=True)  16 us
  transfers between devices with their start and end apart: 8, of which 4 were waited for; matrix products, arithmetic and copies ran while one was open for 34% of the time, Pallas kernels for 0%

profile of v3, /device:TPU:1, one launch (start us, length us, event | category | flops | bytes accessed | tf_op | source)
XLA Modules:
  0.0 372.6 jit_solution(1508165669451300590)
XLA Ops:
  7.2 0.7 all-gather.3.cloned.1.call-update
  8.0 16.0 %all_gather.10 = bf16[64,3072]{1,0:T(8,128)(2,1)} all-gather(bf16[64,384]{1,0:T(8,128)(2,1)} %param.10), channel_id=1, replica_groups=mesh['space'=16,'tm'=8] {'tm'}, dimensions={1}, use_global_device_ids=true | all-gather | bytes 442368 | tf_op jit(solution)/shard_map/all_gather | solution.py:165
  24.0 0.7 fusion.36
  24.9 0.7 fusion.37
  25.9 0.3 copy.56
  26.2 44.1 %reshape.88 = bf16[2,4,6,16,6,16,6]{6,5,4,3,1,2,0:T(8,128)(2,1)} reshape(bf16[2,4,6,9216]{3,1,2,0:T(4,128)(2,1)S(1)} %copy-done.5) | data formatting | bytes 1769472 | tf_op jit(solution)/shard_map/reshape | solution.py:127
  70.3 34.5 %copy.54 = bf16[2,16,16,4,6,6,6]{2,1,6,5,4,3,0:T(8,128)(2,1)} copy(bf16[2,16,16,4,6,6,6]{6,2,5,1,3,4,0:T(8,128)(2,1)} %bitcast.72) | data formatting | bytes 1769472 | tf_op jit(solution)/shard_map/transpose | solution.py:128
  104.8 8.7 %reshape.89 = bf16[2,256,864]{1,2,0:T(8,128)(2,1)S(1)} reshape(bf16[2,16,16,4,6,6,6]{2,1,6,5,4,3,0:T(8,128)(2,1)} %copy.54) | data formatting | bytes 1769472 | tf_op jit(solution)/shard_map/reshape | solution.py:129
  113.4 0.6 convolution_convert_fusion.2
  114.0 0.7 copy.55
  114.8 1.7 maximum_maximum_fusion
  116.6 7.8 %all-to-all-start = ((bf16[2,16,12,896]{3,0,2,1:T(2,128)(2,1)}), bf16[2,16,12,896]{3,0,2,1:T(2,128)(2,1)S(1)}, u32[]{:S(2)}, u32[]{:S(2)}) async-start(bf16[2,16,12,896]{3,0,2,1:T(2,128)(2,1)} %maximum_maximum_fusion), calls=%async_computation | async-start | bytes 1376256 | tf_op jit(solution)/shard_map/all_to_all | solution.py:150
  124.4 0.3 copy.64
  124.7 0.8 copy.65
  125.5 10.5 %all-to-all-done = bf16[2,16,12,896]{3,0,2,1:T(2,128)(2,1)S(1)} async-done(((bf16[2,16,12,896]{3,0,2,1:T(2,128)(2,1)}), bf16[2,16,12,896]{3,0,2,1:T(2,128)(2,1)S(1)}, u32[]{:S(2)}, u32[]{:S(2)}) %all-to-all-start) | async-done | bytes 688160 | tf_op jit(solution)/shard_map/all_to_all | solution.py:150
  136.0 4.5 %all-to-all-start.2 = ((bf16[16,2,128,64]{2,3,1,0:T(8,128)(2,1)}), bf16[16,2,128,64]{2,3,1,0:T(8,128)(2,1)}, u32[]{:S(2)}, u32[]{:S(2)}) async-start(bf16[16,2,128,64]{2,3,1,0:T(8,128)(2,1)} %copy.65), calls=%async_computation.2 | async-start | bytes 1048576 | tf_op jit(solution)/shard_map/all_to_all | solution.py:173
  140.8 0.6 convolution_convert_fusion.4
  141.7 2.4 convert_reduce_fusion.1
  144.2 0.3 fusion.16
  144.5 8.6 %copy.60 = bf16[1024,3072]{0,1:T(8,128)(2,1)} copy(bf16[1024,3072]{1,0:T(8,128)(2,1)} %all-gather.5.cloned.1.call-done) | data formatting | bytes 12582912 | tf_op jit(solution)/shard_map/all_gather | solution.py:166
  153.1 3.5 copy.61
  156.6 1.9 convolution_convert_fusion.1
  158.6 0.7 copy.62
  159.3 0.4 reshape.94
  159.7 1.5 copy.63
  161.3 6.6 %all-to-all-start.1 = ((bf16[16,2,128,192]{2,3,1,0:T(8,128)(2,1)}), bf16[16,2,128,192]{2,3,1,0:T(8,128)(2,1)}, u32[]{:S(2)}, u32[]{:S(2)}) async-start(bf16[16,2,128,192]{2,3,1,0:T(8,128)(2,1)} %copy.63), calls=%async_computation.1 | async-start | bytes 3145728 | tf_op jit(solution)/shard_map/all_to_all | solution.py:172
  168.0 1.5 copy.67.g_ref
  169.5 18.5 %all-to-all-done.1 = bf16[16,2,128,192]{2,3,1,0:T(8,128)(2,1)} async-done(((bf16[16,2,128,192]{2,3,1,0:T(8,128)(2,1)}), bf16[16,2,128,192]{2,3,1,0:T(8,128)(2,1)}, u32[]{:S(2)}, u32[]{:S(2)}) %all-to-all-start.1) | async-done | bytes 1572896 | tf_op jit(solution)/shard_map/all_to_all | solution.py:172
  188.0 2.7 copy.66.lanes_ref
  190.7 37.4 %shard_map.77 = bf16[16,2,128,192]{3,2,1,0:T(8,128)(2,1)S(1)} custom-call(bf16[16,2,128,192]{3,2,1,0:T(8,128)(2,1)S(1)} %copy.66.lanes_ref, bf16[16,2,128,64]{3,2,1,0:T(8,128)(2,1)S(1)} %copy.67.g_ref), custom_call_target="tpu_custom_call" | custom-call | flops 5368709120 | bytes 3670016 | tf_op jit(solution)/shard_map/pallas_call | solution.py:93
  228.1 1.3 copy-done
  229.5 3.1 copy.68
  232.6 23.0 %all_to_all.40 = bf16[16,2,128,192]{2,3,1,0:T(8,128)(2,1)S(1)} all-to-all(bf16[16,2,128,192]{2,3,1,0:T(8,128)(2,1)S(1)} %copy.68), channel_id=1, replica_groups=mesh['space'=16,'tm'=8] {'space'}, dimensions={0} | all-to-all | bytes 3145728 | tf_op jit(solution)/shard_map/all_to_all | solution.py:175
  255.6 1.6 copy.69
  257.2 4.7 %convolution_convert_fusion = bf16[1024,3072]{1,0:T(8,128)(2,1)} fusion(bf16[384,8,2,128]{3,2,1,0:T(2,128)(2,1)S(1)} %bitcast.78, bf16[256,1024]{1,0:T(8,128)(2,1)S(1)} %copy-done.2, f32[256]{0:T(256)S(1)} %add_rsqrt_fusion, f32[256]{0:T(256)S(1)} %broadcast_multiply_fusion.2), kind=kOutput, calls=%fused_computation | convolution fusion | flops 1614807040 | bytes 8390656 | tf_op jit(solution)/shard_map/dot_general | solution.py:26
  261.9 4.9 %fusion.40 = (f32[256]{0:T(256)S(1)}, f32[256]{0:T(256)S(1)}, f32[256,1024]{1,0:T(8,128)S(1)}) fusion(f32[256]{0:T(256)S(1)} %add_rsqrt_fusion, f32[256]{0:T(256)S(1)} %broadcast_multiply_fusion.2, bf16[256,1024]{1,0:T(8,128)(2,1)S(1)} %copy-done.2, bf16[1024,3072]{1,0:T(8,128)(2,1)} %all-gather.5.cloned.1.call-done, bf16[384,8,2,128]{3,2,1,0:T(2,128)(2,1)S(1)} %bitcast.79), kind=kOutput, calls=%fused_computation.70 | convolution fusion | flops 1612185088 | bytes 9441280 | tf_op jit(solution)/shard_map/dot_general | solution.py:26
  266.8 0.9 convert_bitcast_fusion
  267.7 0.3 copy.96
  268.0 30.8 %all_to_all.41 = bf16[8,864,128]{2,1,0:T(8,128)(2,1)S(1)} all-to-all(bf16[8,864,128]{2,1,0:T(8,128)(2,1)S(1)} %bitcast.74), channel_id=1, replica_groups=mesh['space'=16,'tm'=8] {'tm'}, dimensions={0} | all-to-all | bytes 3538944 | tf_op jit(solution)/shard_map/all_to_all | solution.py:203
  299.1 13.9 %all_to_all.42 = f32[16,54,128]{2,1,0:T(8,128)S(1)} all-to-all(f32[16,54,128]{2,1,0:T(8,128)S(1)} %reshape.100), channel_id=1, replica_groups=mesh['space'=16,'tm'=8] {'space'}, dimensions={0} | all-to-all | bytes 884736 | tf_op jit(solution)/shard_map/all_to_all | solution.py:213
  313.1 0.8 broadcast_in_dim.15
  313.9 5.9 %all-to-all-start.7 = ((f32[16,54,128]{2,1,0:T(8,128)}), f32[16,54,128]{2,1,0:T(8,128)S(1)}, u32[]{:S(2)}, u32[]{:S(2)}) async-start(f32[16,54,128]{2,1,0:T(8,128)} %broadcast_in_dim.15), calls=%async_computation.8 | async-start | bytes 917504 | tf_op jit(solution)/shard_map/all_to_all | solution.py:217
  319.8 29.5 %reduce-scatter.2.cloned.1.call-done = bf16[64,3072]{1,0:T(8,128)(2,1)} async-done(((bf16[1024,3072]{1,0:T(8,128)(2,1)}), bf16[64,3072]{1,0:T(8,128)(2,1)}) %reduce-scatter.2.cloned.1.call-update) | async-done | bytes 393232 | tf_op jit(solution)/shard_map/reduce_scatter | solution.py:181
  349.3 1.8 copy.97
  351.1 6.6 %all-to-all-start.4 = ((bf16[8,64,384]{2,1,0:T(8,128)(2,1)}), bf16[8,64,384]{2,1,0:T(8,128)(2,1)S(1)}, u32[]{:S(2)}, u32[]{:S(2)}) async-start(bf16[8,64,384]{2,1,0:T(8,128)(2,1)} %bitcast.69), calls=%async_computation.5 | async-start | bytes 786432 | tf_op jit(solution)/shard_map/all_to_all | solution.py:189
  357.7 0.8 reshape.101
  358.5 6.9 %all-to-all-done.4 = bf16[8,64,384]{2,1,0:T(8,128)(2,1)S(1)} async-done(((bf16[8,64,384]{2,1,0:T(8,128)(2,1)}), bf16[8,64,384]{2,1,0:T(8,128)(2,1)S(1)}, u32[]{:S(2)}, u32[]{:S(2)}) %all-to-all-start.4) | async-done | bytes 393248 | tf_op jit(solution)/shard_map/all_to_all | solution.py:189
  365.4 0.7 convert_reduce_fusion.2
  (40 shorter events, 1.7 us)
Async XLA Ops:
  7.2 19.1 %copy-start.5 = (bf16[2,4,6,9216]{3,1,2,0:T(4,128)(2,1)S(1)}, bf16[2,4,6,9216]{3,1,2,0:T(4,128)(2,1)}, u32[]{:S(2)}) copy-start(bf16[2,4,6,9216]{3,1,2,0:T(4,128)(2,1)} %param.6) | copy-start | bytes 2654212
  7.2 134.5 %all-gather.3.cloned.1.call-start = ((), (), s32[]{:S(2)}) async-start(), calls=%async_computation.9 | async-start | bytes 1990656 | tf_op jit(solution)/shard_map/all_gather | solution.py:158
  7.9 136.6 %all-gather.5.cloned.1.call-start = ((), (), s32[]{:S(2)}) async-start(), calls=%async_computation.10 | async-start | bytes 6684672 | tf_op jit(solution)/shard_map/all_gather | solution.py:166
  104.7 8.7 %copy-start.7 = (s32[2,256]{1,0:T(2,128)S(1)}, s32[2,256]{1,0:T(2,128)}, u32[]{:S(2)}) copy-start(s32[2,256]{1,0:T(2,128)} %param.7) | copy-start | bytes 6148
  114.7 9.6 %copy-start.6 = (bf16[2,1,128,1024]{3,2,1,0:T(8,128)(2,1)S(1)}, bf16[2,1,128,1024]{3,2,1,0:T(8,128)(2,1)}, u32[]{:S(2)}) copy-start(bf16[2,1,128,1024]{3,2,1,0:T(8,128)(2,1)} %param.11) | copy-start | bytes 1572868
  116.6 19.4 %all-to-all-start = ((bf16[2,16,12,896]{3,0,2,1:T(2,128)(2,1)}), bf16[2,16,12,896]{3,0,2,1:T(2,128)(2,1)S(1)}, u32[]{:S(2)}, u32[]{:S(2)}) async-start(bf16[2,16,12,896]{3,0,2,1:T(2,128)(2,1)} %maximum_maximum_fusion), calls=%async_computation | async-start | bytes 1376256 | tf_op jit(solution)/shard_map/all_to_all | solution.py:150
  136.0 25.2 %all-to-all-start.2 = ((bf16[16,2,128,64]{2,3,1,0:T(8,128)(2,1)}), bf16[16,2,128,64]{2,3,1,0:T(8,128)(2,1)}, u32[]{:S(2)}, u32[]{:S(2)}) async-start(bf16[16,2,128,64]{2,3,1,0:T(8,128)(2,1)} %copy.65), calls=%async_computation.2 | async-start | bytes 1048576 | tf_op jit(solution)/shard_map/all_to_all | solution.py:173
  141.7 2.8 copy-start.3
  144.1 12.5 %copy-start.1 = (bf16[256,1024]{1,0:T(8,128)(2,1)}, bf16[256,1024]{1,0:T(8,128)(2,1)S(1)}, u32[]{:S(2)}) copy-start(bf16[256,1024]{1,0:T(8,128)(2,1)S(1)} %get-tuple-element.7) | copy-start | bytes 1572868
  161.3 26.7 %all-to-all-start.1 = ((bf16[16,2,128,192]{2,3,1,0:T(8,128)(2,1)}), bf16[16,2,128,192]{2,3,1,0:T(8,128)(2,1)}, u32[]{:S(2)}, u32[]{:S(2)}) async-start(bf16[16,2,128,192]{2,3,1,0:T(8,128)(2,1)} %copy.63), calls=%async_computation.1 | async-start | bytes 3145728 | tf_op jit(solution)/shard_map/all_to_all | solution.py:172
  167.9 181.4 %reduce-scatter.2.cloned.1.call-start = ((), (), s32[]{:S(2)}) async-start(), calls=%async_computation.11 | async-start | bytes 6684672 | tf_op jit(solution)/shard_map/reduce_scatter | solution.py:181
  228.1 1.3 copy-start
  255.6 1.6 copy-start.2
  261.9 4.9 %copy-start.4 = (bf16[2,128,864]{2,1,0:T(8,128)(2,1)S(1)}, bf16[2,128,864]{2,1,0:T(8,128)(2,1)}, u32[]{:S(2)}) copy-start(bf16[2,128,864]{2,1,0:T(8,128)(2,1)} %copy-done.3) | copy-start | bytes 1327108
  313.9 37.2 %all-to-all-start.7 = ((f32[16,54,128]{2,1,0:T(8,128)}), f32[16,54,128]{2,1,0:T(8,128)S(1)}, u32[]{:S(2)}, u32[]{:S(2)}) async-start(f32[16,54,128]{2,1,0:T(8,128)} %broadcast_in_dim.15), calls=%async_computation.8 | async-start | bytes 917504 | tf_op jit(solution)/shard_map/all_to_all | solution.py:217
  351.1 14.3 %all-to-all-start.4 = ((bf16[8,64,384]{2,1,0:T(8,128)(2,1)}), bf16[8,64,384]{2,1,0:T(8,128)(2,1)S(1)}, u32[]{:S(2)}, u32[]{:S(2)}) async-start(bf16[8,64,384]{2,1,0:T(8,128)(2,1)} %bitcast.69), calls=%async_computation.5 | async-start | bytes 786432 | tf_op jit(solution)/shard_map/all_to_all | solution.py:189
Sparse Core Ops, SparseCore 0:
  9.7 29.1 all-gather.2
  41.1 61.8 all-gather.4
  262.0 87.1 reduce-scatter.1

commit v4 on v3

--- a/solution.py
+++ b/solution.py
@@ -123,25 +123,38 @@
     row_total = windows * OWN
     side_y = GY // 6
     side_z = GZ // 6
-    local_patches = (
-        voxels.reshape(windows, 4, 6, side_y, 6, side_z, 6)
-        .transpose(0, 3, 5, 1, 2, 4, 6)
-        .reshape(windows, side_y * side_z, PATCH)
-    )
+    frames = voxels.shape[1]
+    depth = voxels.shape[2]
+    lanes_b = -(-buckets // 128) * 128
     my_buckets = bucket_index(owner_slot, slab_count, capacity)
     to_bucket = (
-        my_buckets[:, None, :] == jnp.arange(buckets, dtype=jnp.int32)[None, :, None]
+        my_buckets[:, None, :] == jnp.arange(lanes_b, dtype=jnp.int32)[None, :, None]
     ).astype(jnp.bfloat16)
-    is_patch = (
-        brain_list[:, :, None] == jnp.arange(PSLAB, dtype=jnp.int32)[None, None, :]
-    ).astype(jnp.bfloat16)
-    picks = select(to_bucket, is_patch).astype(jnp.bfloat16)
     slot_code = (jnp.where(owner_slot >= 0, owner_slot % OWN, -1) + 1).astype(jnp.bfloat16)
-    bucket_code = select(to_bucket, slot_code[:, :, None])
+    bucket_code = select(to_bucket, slot_code[:, :, None])[:, :buckets]
+    patch_code = select(to_bucket, (brain_list + 1).astype(jnp.float32)[:, :, None].astype(jnp.bfloat16))
+    patch_of = patch_code[:, :, 0].astype(jnp.int32) - 1
+    py_of = jnp.where(patch_of >= 0, patch_of // side_z, -1)
+    pz_of = jnp.where(patch_of >= 0, patch_of % side_z, -1)
+    z_index = jnp.arange(GZ, dtype=jnp.int32)
+    inner = jnp.arange(6, dtype=jnp.int32)
+    pick_z = (
+        z_index[None, :, None, None]
+        == pz_of[:, None, None, :] * 6 + inner[None, None, :, None]
+    ).astype(jnp.bfloat16).reshape(windows, GZ, 6 * lanes_b)
+    rows = voxels.reshape(windows, frames * depth * GY, GZ)
+    by_z = jnp.einsum("wrz,wzk->wrk", rows, pick_z, preferred_element_type=jnp.float32)
+    by_z = by_z.astype(jnp.bfloat16).reshape(windows, frames * depth, GY, 6, lanes_b)
+    y_index = jnp.arange(GY, dtype=jnp.int32)
+    keep_y = (y_index[None, :, None] // 6 == py_of[:, None, :]).astype(jnp.bfloat16)
+    masked = by_z * keep_y[:, None, :, None, :]
+    fold_y = (y_index[None, :] % 6 == inner[:, None]).astype(jnp.bfloat16)
+    by_y = jnp.einsum("iy,wfyjb->wifjb", fold_y, masked, preferred_element_type=jnp.float32)
+    columns = by_y.astype(jnp.bfloat16).reshape(windows, PATCH, lanes_b)
     width = -(-(PATCH + 1) // 128) * 128
     payload = jnp.concatenate(
         [
-            select(picks, local_patches).astype(jnp.bfloat16),
+            jnp.swapaxes(columns, 1, 2)[:, :buckets],
             bucket_code.astype(jnp.bfloat16),
             jnp.zeros((windows, buckets, width - PATCH - 1), jnp.bfloat16),
         ],
@@ -155,7 +168,12 @@
         arrival_slot[:, None, :] == jnp.arange(OWN, dtype=jnp.int32)[None, :, None]
     ).astype(jnp.bfloat16)
     chosen = select(to_slot, arrived[:, :, :PATCH]).astype(jnp.bfloat16).reshape(row_total, PATCH)
-    full_embed = lax.all_gather(embed_weight, "tm", axis=1, tiled=True)
+    full_embed = (
+        lax.all_gather(embed_weight, "tm", axis=1, tiled=True)
+        .reshape(4, 6, 6, 6, D)
+        .transpose(2, 0, 1, 3, 4)
+        .reshape(PATCH, D)
+    )
     tokens = jnp.dot(chosen, full_embed, preferred_element_type=jnp.float32).astype(jnp.bfloat16)
     widened = tokens.astype(jnp.float32)
     center = widened - jnp.mean(widened, axis=1, keepdims=True)
@@ -221,7 +239,12 @@
         concat_axis=0,
         tiled=True,
     )
-    d_embed_weight = gathered.reshape(chunk * slab_count, -1)[:PATCH]
+    d_embed_weight = (
+        gathered.reshape(chunk * slab_count, -1)[:PATCH]
+        .reshape(6, 4, 6, 6, -1)
+        .transpose(1, 2, 0, 3, 4)
+        .reshape(PATCH, -1)
+    )
     return (d_qkv_weight, d_embed_weight)
 
 

time: 374 us -> 370 us (0.989)
  local copies, waits for them, and re-layouts: 119 us -> 92.3 us
  other arithmetic: 4.42 us -> 17.5 us
  matrix products: 16.3 us -> 24.8 us
    transpose x1 -> x2, local copies, waits for them, and re-layouts: 34.5 us -> 1.75 us  [the longest x1 1.71 us: body(): full_embed = lax.all_gather(embed_weight, 'tm', axis=1, tiled=True).resha...]
    convert_element_type x1 -> x2, local copies, waits for them, and re-layouts: 0.71 us -> 20.9 us  [the longest x1 18.7 us: body(): by_z.astype(jnp.bfloat16).reshape(windows, frames * depth, GY, 6, lanes_b)]
    reshape x3 -> x5, local copies, waits for them, and re-layouts: 53.5 us -> 36.2 us  [the longest x1 28.8 us: body(): by_z.astype(jnp.bfloat16).reshape(windows, frames * depth, GY, 6, lanes_b)]
    dot_general x0 -> x2, matrix products: none -> 10.5 us  [the longest x1 7.29 us: body(): jnp.einsum('wrz,wzk->wrk', rows, pick_z, preferred_element_type=jnp.float32)]
    mul x0 -> x1, other arithmetic: none -> 9.54 us  [body(): masked = by_z * keep_y[:, None, :, None, :]]
  transfers between devices with their start and end apart: 8 -> 8, of which waited for: 4 -> 4; matrix products, arithmetic and copies ran while one was open for 34% -> 33% of each run, Pallas kernels for 0% -> 0%
where the time goes in v4:
time: 370 us; the launch traced here: 367 us
  local copies, waits for them, and re-layouts  92.3 us (25%)
  blocking collectives  83.8 us (23%)
  waiting for transfers between devices  66 us (18%)
  Pallas kernels  37.4 us (10%)
  starting transfers between devices  31.6 us (9%)
  matrix products  24.8 us (7%)
  other arithmetic  17.5 us (5%)
  between operations  14.2 us (4%)
    pallas_call x1, Pallas kernels, attention_grads(): pl.pallas_call(attention_kernel, grid=(windows, owners // per_block), in_...  37.4 us
    all_to_all x1, blocking collectives, body(): lax.all_to_all(embed_partial.astype(jnp.bfloat16).reshape(PATCH, tm_count...  30.7 us
    reduce_scatter x1, waiting for transfers between devices, body(): lax.psum_scatter(contract(hidden, d_packed, 0, 0).astype(jnp.bfloat16), '...  29.5 us
    reshape x1, local copies, waits for them, and re-layouts, body(): by_z.astype(jnp.bfloat16).reshape(windows, frames * depth, GY, 6, lanes_b)  28.8 us
    all_to_all x1, blocking collectives, body(): lax.all_to_all(grads, 'space', split_axis=0, concat_axis=0, tiled=True)  23.2 us
    convert_element_type x1, local copies, waits for them, and re-layouts, body(): by_z.astype(jnp.bfloat16).reshape(windows, frames * depth, GY, 6, lanes_b)  18.7 us
    all_to_all x1, waiting for transfers between devices, body(): lax.all_to_all(lanes_out, 'space', split_axis=0, concat_axis=0, tiled=True)  18.5 us
    all_gather x1, blocking collectives, body(): wide_rows = lax.all_gather(qkv_weight, 'tm', axis=1, tiled=True)  16 us
  transfers between devices with their start and end apart: 8, of which 4 were waited for; matrix products, arithmetic and copies ran while one was open for 33% of the time, Pallas kernels for 0%

profile of v4, /device:TPU:1, one launch (start us, length us, event | category | flops | bytes accessed | tf_op | source)
XLA Modules:
  0.0 367.5 jit_solution(4517138684137126743)
XLA Ops:
  8.0 16.0 %all_gather.10 = bf16[64,3072]{1,0:T(8,128)(2,1)} all-gather(bf16[64,384]{1,0:T(8,128)(2,1)} %param.10), channel_id=1, replica_groups=mesh['space'=16,'tm'=8] {'tm'}, dimensions={1}, use_global_device_ids=true | all-gather | bytes 442368 | tf_op jit(solution)/shard_map/all_gather | solution.py:183
  24.0 0.7 fusion.53
  24.9 0.7 fusion.55
  25.6 0.7 fusion.57
  26.9 1.2 reshape.190
  28.1 7.3 %fusion.2 = bf16[2,2304,1536]{1,2,0:T(8,128)(2,1)} fusion(bf16[2,2304,96]{2,1,0:T(8,128)(2,1)S(1)} %reshape.190, s32[2,1536]{1,0:T(2,128)S(1)} %broadcast_add_fusion), kind=kOutput, calls=%fused_computation.3 | convolution fusion | flops 1366622208 | bytes 15052800 | tf_op jit(solution)/shard_map/wrz,wzk->wrk/dot_general | solution.py:146
  35.4 18.7 %copy.53 = bf16[2,2304,1536]{2,1,0:T(8,128)(2,1)} copy(bf16[2,2304,1536]{1,2,0:T(8,128)(2,1)} %fusion.2) | data formatting | bytes 28311552 | tf_op jit(solution)/shard_map/convert_element_type | solution.py:147
  54.1 28.8 %reshape.191 = bf16[2,24,96,6,256]{4,3,2,1,0:T(8,128)(2,1)} reshape(bf16[2,2304,1536]{2,1,0:T(8,128)(2,1)} %copy.53) | data formatting | bytes 28311552 | tf_op jit(solution)/shard_map/reshape | solution.py:147
  83.0 9.5 %broadcast_multiply_fusion = bf16[2,24,96,6,256]{4,3,2,1,0:T(8,128)(2,1)S(1)} fusion(bf16[2,24,96,6,256]{4,3,2,1,0:T(8,128)(2,1)} %reshape.191, bf16[2,96,256]{2,1,0:T(8,128)(2,1)S(1)} %compare_convert_fusion), kind=kLoop, calls=%fused_computation.4 | loop fusion | flops 7077888 | bytes 28409856 | tf_op jit(solution)/shard_map/mul | solution.py:150
  92.5 3.2 fusion.9
  95.7 2.2 copy.55
  98.2 4.4 %maximum_maximum_fusion = bf16[2,192,896]{1,0,2:T(2,128)(2,1)S(1)} fusion(bf16[2,192,1]{1,0,2:T(2,128)(2,1)S(1)} %bitcast.116, bf16[2,192,864]{1,0,2:T(2,128)(2,1)S(1)} %bitcast.107, bf16[896]{0:T(1024)(128)(2,1)S(1)} %pad.2.clone), kind=kLoop, calls=%fused_computation.36 | loop fusion | flops 688128 | bytes 1354240 | tf_op jit(solution)/shard_map/concatenate | solution.py:155
  102.6 3.4 copy.56
  106.0 7.7 %all-to-all-start = ((bf16[2,16,12,896]{3,0,2,1:T(2,128)(2,1)}), bf16[2,16,12,896]{3,0,2,1:T(2,128)(2,1)S(1)}, u32[]{:S(2)}, u32[]{:S(2)}) async-start(bf16[2,16,12,896]{3,0,2,1:T(2,128)(2,1)} %bitcast.13), calls=%async_computation | async-start | bytes 1376256 | tf_op jit(solution)/shard_map/all_to_all | solution.py:163
  114.1 0.9 copy.66
  114.9 10.5 %all-to-all-done = bf16[2,16,12,896]{3,0,2,1:T(2,128)(2,1)S(1)} async-done(((bf16[2,16,12,896]{3,0,2,1:T(2,128)(2,1)}), bf16[2,16,12,896]{3,0,2,1:T(2,128)(2,1)S(1)}, u32[]{:S(2)}, u32[]{:S(2)}) %all-to-all-start) | async-done | bytes 688160 | tf_op jit(solution)/shard_map/all_to_all | solution.py:163
  125.4 4.5 %all-to-all-start.2 = ((bf16[16,2,128,64]{2,3,1,0:T(8,128)(2,1)}), bf16[16,2,128,64]{2,3,1,0:T(8,128)(2,1)}, u32[]{:S(2)}, u32[]{:S(2)}) async-start(bf16[16,2,128,64]{2,3,1,0:T(8,128)(2,1)} %copy.66), calls=%async_computation.2 | async-start | bytes 1048576 | tf_op jit(solution)/shard_map/all_to_all | solution.py:191
  131.1 2.7 reshape.196
  133.8 1.7 copy.60
  135.5 2.7 reshape.197
  138.2 0.8 convert_reduce_fusion.1
  139.3 8.6 %copy.61 = bf16[1024,3072]{0,1:T(8,128)(2,1)} copy(bf16[1024,3072]{1,0:T(8,128)(2,1)} %all-gather.5.cloned.1.call-done) | data formatting | bytes 12582912 | tf_op jit(solution)/shard_map/all_gather | solution.py:184
  148.0 3.5 copy.62
  151.5 1.9 convolution_convert_fusion.2
  153.4 0.7 copy.63
  154.5 1.5 copy.64
  156.1 6.6 %all-to-all-start.1 = ((bf16[16,2,128,192]{2,3,1,0:T(8,128)(2,1)}), bf16[16,2,128,192]{2,3,1,0:T(8,128)(2,1)}, u32[]{:S(2)}, u32[]{:S(2)}) async-start(bf16[16,2,128,192]{2,3,1,0:T(8,128)(2,1)} %copy.64), calls=%async_computation.1 | async-start | bytes 3145728 | tf_op jit(solution)/shard_map/all_to_all | solution.py:190
  162.8 1.5 copy.68.g_ref
  164.3 18.5 %all-to-all-done.1 = bf16[16,2,128,192]{2,3,1,0:T(8,128)(2,1)} async-done(((bf16[16,2,128,192]{2,3,1,0:T(8,128)(2,1)}), bf16[16,2,128,192]{2,3,1,0:T(8,128)(2,1)}, u32[]{:S(2)}, u32[]{:S(2)}) %all-to-all-start.1) | async-done | bytes 1572896 | tf_op jit(solution)/shard_map/all_to_all | solution.py:190
  182.8 2.7 copy.67.lanes_ref
  185.6 37.4 %shard_map.77 = bf16[16,2,128,192]{3,2,1,0:T(8,128)(2,1)S(1)} custom-call(bf16[16,2,128,192]{3,2,1,0:T(8,128)(2,1)S(1)} %copy.67.lanes_ref, bf16[16,2,128,64]{3,2,1,0:T(8,128)(2,1)S(1)} %copy.68.g_ref), custom_call_target="tpu_custom_call" | custom-call | flops 5368709120 | bytes 3670016 | tf_op jit(solution)/shard_map/pallas_call | solution.py:93
  222.9 1.3 copy-done
  224.3 3.1 copy.69
  227.4 23.2 %all_to_all.40 = bf16[16,2,128,192]{2,3,1,0:T(8,128)(2,1)S(1)} all-to-all(bf16[16,2,128,192]{2,3,1,0:T(8,128)(2,1)S(1)} %copy.69), channel_id=1, replica_groups=mesh['space'=16,'tm'=8] {'space'}, dimensions={0} | all-to-all | bytes 3145728 | tf_op jit(solution)/shard_map/all_to_all | solution.py:193
  250.6 1.6 copy.70
  252.2 4.7 %convolution_convert_fusion.1 = bf16[1024,3072]{1,0:T(8,128)(2,1)} fusion(bf16[384,8,2,128]{3,2,1,0:T(2,128)(2,1)S(1)} %bitcast.105, bf16[256,1024]{1,0:T(8,128)(2,1)S(1)} %copy-done.2, f32[256]{0:T(256)S(1)} %add_rsqrt_fusion, f32[256]{0:T(256)S(1)} %broadcast_multiply_fusion.3), kind=kOutput, calls=%fused_computation.5 | convolution fusion | flops 1614807040 | bytes 8390656 | tf_op jit(solution)/shard_map/dot_general | solution.py:26
  256.9 4.9 %fusion.60 = (f32[256]{0:T(256)S(1)}, f32[256]{0:T(256)S(1)}, f32[256,1024]{1,0:T(8,128)S(1)}) fusion(f32[256]{0:T(256)S(1)} %add_rsqrt_fusion, f32[256]{0:T(256)S(1)} %broadcast_multiply_fusion.3, bf16[256,1024]{1,0:T(8,128)(2,1)S(1)} %copy-done.2, bf16[1024,3072]{1,0:T(8,128)(2,1)} %all-gather.5.cloned.1.call-done, bf16[384,8,2,128]{3,2,1,0:T(2,128)(2,1)S(1)} %bitcast.106), kind=kOutput, calls=%fused_computation.105 | convolution fusion | flops 1612185088 | bytes 9441280 | tf_op jit(solution)/shard_map/dot_general | solution.py:26
  261.8 0.9 convert_bitcast_fusion
  263.0 30.7 %all_to_all.41 = bf16[8,864,128]{2,1,0:T(8,128)(2,1)S(1)} all-to-all(bf16[8,864,128]{2,1,0:T(8,128)(2,1)S(1)} %bitcast.101), channel_id=1, replica_groups=mesh['space'=16,'tm'=8] {'tm'}, dimensions={0} | all-to-all | bytes 3538944 | tf_op jit(solution)/shard_map/all_to_all | solution.py:221
  294.0 13.8 %all_to_all.42 = f32[16,54,128]{2,1,0:T(8,128)S(1)} all-to-all(f32[16,54,128]{2,1,0:T(8,128)S(1)} %reshape.206), channel_id=1, replica_groups=mesh['space'=16,'tm'=8] {'space'}, dimensions={0} | all-to-all | bytes 884736 | tf_op jit(solution)/shard_map/all_to_all | solution.py:231
  307.9 0.8 broadcast_in_dim.17
  308.7 6.0 %all-to-all-start.7 = ((f32[16,54,128]{2,1,0:T(8,128)}), f32[16,54,128]{2,1,0:T(8,128)S(1)}, u32[]{:S(2)}, u32[]{:S(2)}) async-start(f32[16,54,128]{2,1,0:T(8,128)} %broadcast_in_dim.17), calls=%async_computation.8 | async-start | bytes 917504 | tf_op jit(solution)/shard_map/all_to_all | solution.py:235
  314.7 29.5 %reduce-scatter.2.cloned.1.call-done = bf16[64,3072]{1,0:T(8,128)(2,1)} async-done(((bf16[1024,3072]{1,0:T(8,128)(2,1)}), bf16[64,3072]{1,0:T(8,128)(2,1)}) %reduce-scatter.2.cloned.1.call-update) | async-done | bytes 393232 | tf_op jit(solution)/shard_map/reduce_scatter | solution.py:199
  344.1 1.8 copy.119
  345.9 6.6 %all-to-all-start.4 = ((bf16[8,64,384]{2,1,0:T(8,128)(2,1)}), bf16[8,64,384]{2,1,0:T(8,128)(2,1)S(1)}, u32[]{:S(2)}, u32[]{:S(2)}) async-start(bf16[8,64,384]{2,1,0:T(8,128)(2,1)} %bitcast.93), calls=%async_computation.5 | async-start | bytes 786432 | tf_op jit(solution)/shard_map/all_to_all | solution.py:207
  352.7 0.8 reshape.207
  353.5 6.8 %all-to-all-done.4 = bf16[8,64,384]{2,1,0:T(8,128)(2,1)S(1)} async-done(((bf16[8,64,384]{2,1,0:T(8,128)(2,1)}), bf16[8,64,384]{2,1,0:T(8,128)(2,1)S(1)}, u32[]{:S(2)}, u32[]{:S(2)}) %all-to-all-start.4) | async-done | bytes 393248 | tf_op jit(solution)/shard_map/all_to_all | solution.py:207
  360.3 0.7 convert_reduce_fusion.2
  (56 shorter events, 4.9 us)
Async XLA Ops:
  7.2 19.4 %copy-start.5 = (bf16[2,4,6,9216]{3,1,2,0:T(4,128)(2,1)S(1)}, bf16[2,4,6,9216]{3,1,2,0:T(4,128)(2,1)}, u32[]{:S(2)}) copy-start(bf16[2,4,6,9216]{3,1,2,0:T(4,128)(2,1)} %param.6) | copy-start | bytes 2654212
  7.2 123.9 %all-gather.3.cloned.1.call-start = ((), (), s32[]{:S(2)}) async-start(), calls=%async_computation.9 | async-start | bytes 1990656 | tf_op jit(solution)/shard_map/all_gather | solution.py:172
  7.9 131.4 %all-gather.5.cloned.1.call-start = ((), (), s32[]{:S(2)}) async-start(), calls=%async_computation.10 | async-start | bytes 6684672 | tf_op jit(solution)/shard_map/all_gather | solution.py:184
  102.6 11.1 %copy-start.6 = (bf16[2,1,128,1024]{3,2,1,0:T(8,128)(2,1)S(1)}, bf16[2,1,128,1024]{3,2,1,0:T(8,128)(2,1)}, u32[]{:S(2)}) copy-start(bf16[2,1,128,1024]{3,2,1,0:T(8,128)(2,1)} %param.11) | copy-start | bytes 1572868
  106.0 19.4 %all-to-all-start = ((bf16[2,16,12,896]{3,0,2,1:T(2,128)(2,1)}), bf16[2,16,12,896]{3,0,2,1:T(2,128)(2,1)S(1)}, u32[]{:S(2)}, u32[]{:S(2)}) async-start(bf16[2,16,12,896]{3,0,2,1:T(2,128)(2,1)} %bitcast.13), calls=%async_computation | async-start | bytes 1376256 | tf_op jit(solution)/shard_map/all_to_all | solution.py:163
  125.4 30.7 %all-to-all-start.2 = ((bf16[16,2,128,64]{2,3,1,0:T(8,128)(2,1)}), bf16[16,2,128,64]{2,3,1,0:T(8,128)(2,1)}, u32[]{:S(2)}, u32[]{:S(2)}) async-start(bf16[16,2,128,64]{2,3,1,0:T(8,128)(2,1)} %copy.66), calls=%async_computation.2 | async-start | bytes 1048576 | tf_op jit(solution)/shard_map/all_to_all | solution.py:191
  131.1 7.1 %copy-start.3 = (bf16[2,128,864]{2,1,0:T(8,128)(2,1)}, bf16[2,128,864]{2,1,0:T(8,128)(2,1)S(1)}, u32[]{:S(2)}) copy-start(bf16[2,128,864]{2,1,0:T(8,128)(2,1)S(1)} %copy.59) | copy-start | bytes 1327108
  139.0 12.5 %copy-start.1 = (bf16[256,1024]{1,0:T(8,128)(2,1)}, bf16[256,1024]{1,0:T(8,128)(2,1)S(1)}, u32[]{:S(2)}) copy-start(bf16[256,1024]{1,0:T(8,128)(2,1)S(1)} %get-tuple-element.9) | copy-start | bytes 1572868
  156.1 26.7 %all-to-all-start.1 = ((bf16[16,2,128,192]{2,3,1,0:T(8,128)(2,1)}), bf16[16,2,128,192]{2,3,1,0:T(8,128)(2,1)}, u32[]{:S(2)}, u32[]{:S(2)}) async-start(bf16[16,2,128,192]{2,3,1,0:T(8,128)(2,1)} %copy.64), calls=%async_computation.1 | async-start | bytes 3145728 | tf_op jit(solution)/shard_map/all_to_all | solution.py:190
  162.7 181.4 %reduce-scatter.2.cloned.1.call-start = ((), (), s32[]{:S(2)}) async-start(), calls=%async_computation.11 | async-start | bytes 6684672 | tf_op jit(solution)/shard_map/reduce_scatter | solution.py:199
  222.9 1.3 copy-start
  250.6 1.6 copy-start.2
  256.9 4.9 %copy-start.4 = (bf16[2,128,864]{2,1,0:T(8,128)(2,1)S(1)}, bf16[2,128,864]{2,1,0:T(8,128)(2,1)}, u32[]{:S(2)}) copy-start(bf16[2,128,864]{2,1,0:T(8,128)(2,1)} %copy-done.3) | copy-start | bytes 1327108
  308.7 37.2 %all-to-all-start.7 = ((f32[16,54,128]{2,1,0:T(8,128)}), f32[16,54,128]{2,1,0:T(8,128)S(1)}, u32[]{:S(2)}, u32[]{:S(2)}) async-start(f32[16,54,128]{2,1,0:T(8,128)} %broadcast_in_dim.17), calls=%async_computation.8 | async-start | bytes 917504 | tf_op jit(solution)/shard_map/all_to_all | solution.py:235
  345.9 14.3 %all-to-all-start.4 = ((bf16[8,64,384]{2,1,0:T(8,128)(2,1)}), bf16[8,64,384]{2,1,0:T(8,128)(2,1)S(1)}, u32[]{:S(2)}, u32[]{:S(2)}) async-start(bf16[8,64,384]{2,1,0:T(8,128)(2,1)} %bitcast.93), calls=%async_computation.5 | async-start | bytes 786432 | tf_op jit(solution)/shard_map/all_to_all | solution.py:207
Sparse Core Ops, SparseCore 0:
  9.7 29.1 all-gather.2
  41.1 61.7 all-gather.4
  257.1 87.0 reduce-scatter.1

commit v5 on v4

--- a/solution.py
+++ b/solution.py
@@ -41,6 +41,50 @@
     earlier = jnp.einsum("ij,wjo->wio", before, hits, preferred_element_type=jnp.float32)
     position = jnp.sum(earlier * hits.astype(jnp.float32), axis=-1).astype(jnp.int32)
     return jnp.where(slots >= 0, owner_of * capacity + position, slab_count * capacity)
+
+
+def patch_kernel(rows_ref, pick_ref, keep_ref, fold_ref, out_ref):
+    frames = rows_ref.shape[1]
+    depth = fold_ref.shape[0] // 6
+    lanes_b = out_ref.shape[1]
+    span = 6 * fold_ref.shape[0]
+    keep = keep_ref[0].astype(jnp.float32)[None]
+    for frame in range(frames):
+        by_z = jnp.dot(rows_ref[0, frame], pick_ref[0], preferred_element_type=jnp.float32)
+        rows_per = by_z.shape[0] // depth
+        masked = (by_z.reshape(depth, rows_per, -1) * keep).reshape(depth * rows_per, -1)
+        by_y = contract(masked.astype(jnp.bfloat16), fold_ref[...], 0, 1)
+        for inner in range(6):
+            start = frame * span + inner * fold_ref.shape[0]
+            out_ref[0, :, start : start + fold_ref.shape[0]] = by_y[
+                inner * lanes_b : (inner + 1) * lanes_b
+            ].astype(out_ref.dtype)
+
+
+def patch_columns(rows, pick_z, keep_y, fold):
+    windows = rows.shape[0]
+    lanes_b = pick_z.shape[2] // 6
+    return pl.pallas_call(
+        patch_kernel,
+        grid=(windows,),
+        in_specs=[
+            pl.BlockSpec((1,) + rows.shape[1:], lambda w: (w, 0, 0, 0)),
+            pl.BlockSpec((1,) + pick_z.shape[1:], lambda w: (w, 0, 0)),
+            pl.BlockSpec((1,) + keep_y.shape[1:], lambda w: (w, 0, 0)),
+            pl.BlockSpec(fold.shape, lambda w: (0, 0)),
+        ],
+        out_specs=pl.BlockSpec((1, lanes_b, PATCH), lambda w: (w, 0, 0)),
+        out_shape=jax.ShapeDtypeStruct((windows, lanes_b, PATCH), jnp.bfloat16),
+        compiler_params=pltpu.CompilerParams(
+            dimension_semantics=("arbitrary",),
+            vmem_limit_bytes=48 * 1024 * 1024,
+        ),
+        cost_estimate=pl.CostEstimate(
+            flops=2 * rows.shape[0] * rows.shape[1] * rows.shape[2] * pick_z.shape[1] * pick_z.shape[2] * 2,
+            transcendentals=0,
+            bytes_accessed=rows.size * 2 + windows * lanes_b * PATCH * 2,
+        ),
+    )(rows, pick_z, keep_y, fold)
 
 
 QUERY_BLOCK = 256
@@ -142,19 +186,22 @@
         z_index[None, :, None, None]
         == pz_of[:, None, None, :] * 6 + inner[None, None, :, None]
     ).astype(jnp.bfloat16).reshape(windows, GZ, 6 * lanes_b)
-    rows = voxels.reshape(windows, frames * depth * GY, GZ)
-    by_z = jnp.einsum("wrz,wzk->wrk", rows, pick_z, preferred_element_type=jnp.float32)
-    by_z = by_z.astype(jnp.bfloat16).reshape(windows, frames * depth, GY, 6, lanes_b)
+    rows = voxels.reshape(windows, frames, depth * GY, GZ)
     y_index = jnp.arange(GY, dtype=jnp.int32)
-    keep_y = (y_index[None, :, None] // 6 == py_of[:, None, :]).astype(jnp.bfloat16)
-    masked = by_z * keep_y[:, None, :, None, :]
-    fold_y = (y_index[None, :] % 6 == inner[:, None]).astype(jnp.bfloat16)
-    by_y = jnp.einsum("iy,wfyjb->wifjb", fold_y, masked, preferred_element_type=jnp.float32)
-    columns = by_y.astype(jnp.bfloat16).reshape(windows, PATCH, lanes_b)
+    keep_y = jnp.broadcast_to(
+        (y_index[None, :, None, None] // 6 == py_of[:, None, None, :]),
+        (windows, GY, 6, lanes_b),
+    ).astype(jnp.bfloat16).reshape(windows, GY, 6 * lanes_b)
+    slab_x = jnp.arange(depth, dtype=jnp.int32)
+    fold = (
+        (slab_x[:, None, None, None] == slab_x[None, None, :, None])
+        & (inner[None, :, None, None] == y_index[None, None, None, :] % 6)
+    ).astype(jnp.bfloat16).reshape(depth * 6, depth * GY)
+    picked = patch_columns(rows, pick_z, keep_y, fold)
     width = -(-(PATCH + 1) // 128) * 128
     payload = jnp.concatenate(
         [
-            jnp.swapaxes(columns, 1, 2)[:, :buckets],
+            picked[:, :buckets],
             bucket_code.astype(jnp.bfloat16),
             jnp.zeros((windows, buckets, width - PATCH - 1), jnp.bfloat16),
         ],
@@ -171,7 +218,7 @@
     full_embed = (
         lax.all_gather(embed_weight, "tm", axis=1, tiled=True)
         .reshape(4, 6, 6, 6, D)
-        .transpose(2, 0, 1, 3, 4)
+        .transpose(0, 3, 1, 2, 4)
         .reshape(PATCH, D)
     )
     tokens = jnp.dot(chosen, full_embed, preferred_element_type=jnp.float32).astype(jnp.bfloat16)
@@ -241,8 +288,8 @@
     )
     d_embed_weight = (
         gathered.reshape(chunk * slab_count, -1)[:PATCH]
-        .reshape(6, 4, 6, 6, -1)
-        .transpose(1, 2, 0, 3, 4)
+        .reshape(4, 6, 6, 6, -1)
+        .transpose(0, 2, 3, 1, 4)
         .reshape(PATCH, -1)
     )
     return (d_qkv_weight, d_embed_weight)

time: 370 us -> 335 us (0.905)
  local copies, waits for them, and re-layouts: 92.3 us -> 42.9 us
  waiting for transfers between devices: 66 us -> 95.4 us
  other arithmetic: 17.5 us -> 3.17 us
  matrix products: 24.8 us -> 14.3 us
  Pallas kernels: 37.4 us -> 46.8 us
    all_gather x1, waiting for transfers between devices: 0.02 us -> 28.2 us  [body(): full_qkv = lax.all_gather(wide_rows, 'space', axis=0, tiled=True)]
    reshape x2, local copies, waits for them, and re-layouts: 30 us -> 1.87 us  [the longest x1 1.23 us: body(): rows = voxels.reshape(windows, frames, depth * GY, GZ)]
    convert_element_type x2 -> x1, local copies, waits for them, and re-layouts: 20.9 us -> 0.12 us  [body(): fold = ((slab_x[:, None, None, None] == slab_x[None, None, :, None]) & (i...]
    dot_general x2 -> x0, matrix products: 10.5 us -> none  [the longest x1 7.29 us: body(): jnp.einsum('wrz,wzk->wrk', rows, pick_z, preferred_element_type=jnp.float32)]
    mul x1 -> x0, other arithmetic: 9.54 us -> none  [body(): masked = by_z * keep_y[:, None, :, None, :]]
    pallas_call x0 -> x1, Pallas kernels: none -> 9.42 us  [patch_columns(): pl.pallas_call(patch_kernel, grid=(windows,), in_specs=[pl.BlockSpec((1,)...]
    concatenate x1, other arithmetic: 4.44 us -> 0.16 us  [body(): jnp.concatenate([picked[:, :buckets], bucket_code.astype(jnp.bfloat16), j...]
  transfers between devices with their start and end apart: 8 -> 8, of which waited for: 4 -> 5; matrix products, arithmetic and copies ran while one was open for 33% -> 14% of each run, Pallas kernels for 0% -> 3%
where the time goes in v5:
time: 335 us; the launch traced here: 333 us
  waiting for transfers between devices  95.4 us (28%)
  blocking collectives  85.3 us (25%)
  Pallas kernels  46.8 us (14%)
  local copies, waits for them, and re-layouts  42.9 us (13%)
  starting transfers between devices  31.5 us (9%)
  matrix products  14.3 us (4%)
  between operations  14.2 us (4%)
    pallas_call x1, Pallas kernels, attention_grads(): pl.pallas_call(attention_kernel, grid=(windows, owners // per_block), in_...  37.4 us
    all_to_all x1, blocking collectives, body(): lax.all_to_all(embed_partial.astype(jnp.bfloat16).reshape(PATCH, tm_count...  31.6 us
    reduce_scatter x1, waiting for transfers between devices, body(): lax.psum_scatter(contract(hidden, d_packed, 0, 0).astype(jnp.bfloat16), '...  29.4 us
    all_gather x1, waiting for transfers between devices, body(): full_qkv = lax.all_gather(wide_rows, 'space', axis=0, tiled=True)  28.2 us
    all_to_all x1, blocking collectives, body(): lax.all_to_all(grads, 'space', split_axis=0, concat_axis=0, tiled=True)  23.9 us
    all_to_all x1, waiting for transfers between devices, body(): lax.all_to_all(lanes_out, 'space', split_axis=0, concat_axis=0, tiled=True)  19.2 us
    all_gather x1, blocking collectives, body(): wide_rows = lax.all_gather(qkv_weight, 'tm', axis=1, tiled=True)  16 us
    all_to_all x1, blocking collectives, body(): lax.all_to_all(padded.reshape(slab_count, chunk, -1), 'space', split_axis...  13.7 us
  transfers between devices with their start and end apart: 8, of which 5 were waited for; matrix products, arithmetic and copies ran while one was open for 14% of the time, Pallas kernels for 3%

profile of v5, /device:TPU:1, one launch (start us, length us, event | category | flops | bytes accessed | tf_op | source)
XLA Modules:
  0.0 333.4 jit_solution(2574301048777876396)
XLA Ops:
  7.2 0.7 all-gather.3.cloned.1.call-update
  8.0 16.0 %all_gather.10 = bf16[64,3072]{1,0:T(8,128)(2,1)} all-gather(bf16[64,384]{1,0:T(8,128)(2,1)} %param.10), channel_id=1, replica_groups=mesh['space'=16,'tm'=8] {'tm'}, dimensions={1}, use_global_device_ids=true | all-gather | bytes 442368 | tf_op jit(solution)/shard_map/all_gather | solution.py:230
  24.0 0.7 fusion.39
  24.9 0.7 fusion.43
  26.3 1.2 reshape.231.rows_ref
  28.1 0.6 reshape.232.keep_ref
  29.1 9.4 %shard_map.77 = bf16[2,256,864]{2,1,0:T(8,128)(2,1)S(1)} custom-call(bf16[2,4,576,96]{3,2,1,0:T(8,128)(2,1)S(1)} %reshape.231.rows_ref, bf16[2,96,1536]{2,1,0:T(8,128)(2,1)S(1)} %fusion.10.pick_ref, bf16[2,96,1536]{2,1,0:T(8,128)(2,1)S(1)} %reshape.232.keep_ref, bf16[36,576]{1,0:T(8,128)(2,1)S(1)} %reshape.248.fold_ref), custom_call_target="tpu_custom_call" | custom-call | flops 2717908992 | bytes 1769472 | tf_op jit(solution)/shard_map/pallas_call | solution.py:67
  38.8 1.6 copy.47
  40.5 7.8 %all-to-all-start = ((bf16[2,16,12,896]{3,0,2,1:T(2,128)(2,1)}), bf16[2,16,12,896]{3,0,2,1:T(2,128)(2,1)S(1)}, u32[]{:S(2)}, u32[]{:S(2)}) async-start(bf16[2,16,12,896]{3,0,2,1:T(2,128)(2,1)} %bitcast.7), calls=%async_computation | async-start | bytes 1376256 | tf_op jit(solution)/shard_map/all_to_all | solution.py:210
  48.5 0.9 copy.57
  49.4 11.1 %all-to-all-done = bf16[2,16,12,896]{3,0,2,1:T(2,128)(2,1)S(1)} async-done(((bf16[2,16,12,896]{3,0,2,1:T(2,128)(2,1)}), bf16[2,16,12,896]{3,0,2,1:T(2,128)(2,1)S(1)}, u32[]{:S(2)}, u32[]{:S(2)}) %all-to-all-start) | async-done | bytes 688160 | tf_op jit(solution)/shard_map/all_to_all | solution.py:210
  60.5 6.1 %all-to-all-start.2 = ((bf16[16,2,128,64]{2,3,1,0:T(8,128)(2,1)}), bf16[16,2,128,64]{2,3,1,0:T(8,128)(2,1)}, u32[]{:S(2)}, u32[]{:S(2)}) async-start(bf16[16,2,128,64]{2,3,1,0:T(8,128)(2,1)} %copy.57), calls=%async_computation.2 | async-start | bytes 1048576 | tf_op jit(solution)/shard_map/all_to_all | solution.py:238
  66.9 0.6 convolution_convert_fusion.3
  67.8 2.7 reshape.236
  70.5 2.4 copy.51
  72.9 2.7 reshape.237
  75.6 0.8 convert_reduce_fusion.1
  76.4 0.3 fusion.17
  76.7 28.2 %all-gather.5.cloned.1.call-done = bf16[1024,3072]{1,0:T(8,128)(2,1)} async-done(((bf16[64,3072]{1,0:T(8,128)(2,1)}), bf16[1024,3072]{1,0:T(8,128)(2,1)}) %all-gather.5.cloned.1.call-update) | async-done | bytes 6291472 | tf_op jit(solution)/shard_map/all_gather | solution.py:231
  105.0 8.6 %copy.52 = bf16[1024,3072]{0,1:T(8,128)(2,1)} copy(bf16[1024,3072]{1,0:T(8,128)(2,1)} %all-gather.5.cloned.1.call-done) | data formatting | bytes 12582912 | tf_op jit(solution)/shard_map/all_gather | solution.py:231
  113.6 3.5 %copy.53 = bf16[1024,16,3,64]{0,3,2,1:T(8,128)(2,1)S(1)} copy(bf16[1024,16,3,64]{0,3,1,2:T(8,128)(2,1)} %bitcast.85) | data formatting | bytes 12582912 | tf_op jit(solution)/shard_map/transpose | solution.py:233
  117.1 1.9 convolution_convert_fusion.1
  119.0 0.7 copy.54
  119.7 0.4 reshape.240
  120.2 1.5 copy.55
  121.7 5.0 %all-to-all-start.1 = ((bf16[16,2,128,192]{2,3,1,0:T(8,128)(2,1)}), bf16[16,2,128,192]{2,3,1,0:T(8,128)(2,1)}, u32[]{:S(2)}, u32[]{:S(2)}) async-start(bf16[16,2,128,192]{2,3,1,0:T(8,128)(2,1)} %copy.55), calls=%async_computation.1 | async-start | bytes 3145728 | tf_op jit(solution)/shard_map/all_to_all | solution.py:237
  126.8 1.5 copy.59.g_ref
  128.3 19.2 %all-to-all-done.1 = bf16[16,2,128,192]{2,3,1,0:T(8,128)(2,1)} async-done(((bf16[16,2,128,192]{2,3,1,0:T(8,128)(2,1)}), bf16[16,2,128,192]{2,3,1,0:T(8,128)(2,1)}, u32[]{:S(2)}, u32[]{:S(2)}) %all-to-all-start.1) | async-done | bytes 1572896 | tf_op jit(solution)/shard_map/all_to_all | solution.py:237
  147.5 2.7 copy.58.lanes_ref
  150.3 37.4 %shard_map.78 = bf16[16,2,128,192]{3,2,1,0:T(8,128)(2,1)S(1)} custom-call(bf16[16,2,128,192]{3,2,1,0:T(8,128)(2,1)S(1)} %copy.58.lanes_ref, bf16[16,2,128,64]{3,2,1,0:T(8,128)(2,1)S(1)} %copy.59.g_ref), custom_call_target="tpu_custom_call" | custom-call | flops 5368709120 | bytes 3670016 | tf_op jit(solution)/shard_map/pallas_call | solution.py:137
  187.6 1.3 copy-done
  189.0 3.1 copy.60
  192.1 23.9 %all_to_all.40 = bf16[16,2,128,192]{2,3,1,0:T(8,128)(2,1)S(1)} all-to-all(bf16[16,2,128,192]{2,3,1,0:T(8,128)(2,1)S(1)} %copy.60), channel_id=1, replica_groups=mesh['space'=16,'tm'=8] {'space'}, dimensions={0} | all-to-all | bytes 3145728 | tf_op jit(solution)/shard_map/all_to_all | solution.py:240
  216.0 1.6 copy.61
  217.7 4.7 %convolution_convert_fusion = bf16[1024,3072]{1,0:T(8,128)(2,1)} fusion(bf16[384,8,2,128]{3,2,1,0:T(2,128)(2,1)S(1)} %bitcast.91, bf16[256,1024]{1,0:T(8,128)(2,1)S(1)} %copy-done.2, f32[256]{0:T(256)S(1)} %add_rsqrt_fusion, f32[256]{0:T(256)S(1)} %broadcast_multiply_fusion.2), kind=kOutput, calls=%fused_computation | convolution fusion | flops 1614807040 | bytes 8390656 | tf_op jit(solution)/shard_map/dot_general | solution.py:26
  222.4 4.9 %fusion.46 = (f32[256]{0:T(256)S(1)}, f32[256]{0:T(256)S(1)}, f32[256,1024]{1,0:T(8,128)S(1)}) fusion(f32[256]{0:T(256)S(1)} %add_rsqrt_fusion, f32[256]{0:T(256)S(1)} %broadcast_multiply_fusion.2, bf16[256,1024]{1,0:T(8,128)(2,1)S(1)} %copy-done.2, bf16[1024,3072]{1,0:T(8,128)(2,1)} %all-gather.5.cloned.1.call-done, bf16[384,8,2,128]{3,2,1,0:T(2,128)(2,1)S(1)} %bitcast.92), kind=kOutput, calls=%fused_computation.97 | convolution fusion | flops 1612185088 | bytes 9441280 | tf_op jit(solution)/shard_map/dot_general | solution.py:26
  227.2 0.9 convert_bitcast_fusion
  228.1 0.3 copy.102
  228.4 31.6 %all_to_all.41 = bf16[8,864,128]{2,1,0:T(8,128)(2,1)S(1)} all-to-all(bf16[8,864,128]{2,1,0:T(8,128)(2,1)S(1)} %bitcast.87), channel_id=1, replica_groups=mesh['space'=16,'tm'=8] {'tm'}, dimensions={0} | all-to-all | bytes 3538944 | tf_op jit(solution)/shard_map/all_to_all | solution.py:268
  260.4 13.7 %all_to_all.42 = f32[16,54,128]{2,1,0:T(8,128)S(1)} all-to-all(f32[16,54,128]{2,1,0:T(8,128)S(1)} %reshape.246), channel_id=1, replica_groups=mesh['space'=16,'tm'=8] {'space'}, dimensions={0} | all-to-all | bytes 884736 | tf_op jit(solution)/shard_map/all_to_all | solution.py:278
  274.1 0.8 broadcast_in_dim.20
  274.9 5.8 %all-to-all-start.7 = ((f32[16,54,128]{2,1,0:T(8,128)}), f32[16,54,128]{2,1,0:T(8,128)S(1)}, u32[]{:S(2)}, u32[]{:S(2)}) async-start(f32[16,54,128]{2,1,0:T(8,128)} %broadcast_in_dim.20), calls=%async_computation.8 | async-start | bytes 917504 | tf_op jit(solution)/shard_map/all_to_all | solution.py:282
  280.7 29.4 %reduce-scatter.2.cloned.1.call-done = bf16[64,3072]{1,0:T(8,128)(2,1)} async-done(((bf16[1024,3072]{1,0:T(8,128)(2,1)}), bf16[64,3072]{1,0:T(8,128)(2,1)}) %reduce-scatter.2.cloned.1.call-update) | async-done | bytes 393232 | tf_op jit(solution)/shard_map/reduce_scatter | solution.py:246
  310.1 1.8 copy.103
  311.9 6.6 %all-to-all-start.4 = ((bf16[8,64,384]{2,1,0:T(8,128)(2,1)}), bf16[8,64,384]{2,1,0:T(8,128)(2,1)S(1)}, u32[]{:S(2)}, u32[]{:S(2)}) async-start(bf16[8,64,384]{2,1,0:T(8,128)(2,1)} %bitcast.80), calls=%async_computation.5 | async-start | bytes 786432 | tf_op jit(solution)/shard_map/all_to_all | solution.py:254
  318.7 0.8 reshape.247
  319.6 6.7 %all-to-all-done.4 = bf16[8,64,384]{2,1,0:T(8,128)(2,1)S(1)} async-done(((bf16[8,64,384]{2,1,0:T(8,128)(2,1)}), bf16[8,64,384]{2,1,0:T(8,128)(2,1)S(1)}, u32[]{:S(2)}, u32[]{:S(2)}) %all-to-all-start.4) | async-done | bytes 393248 | tf_op jit(solution)/shard_map/all_to_all | solution.py:254
  326.2 0.7 convert_reduce_fusion.2
  (62 shorter events, 3.5 us)
Async XLA Ops:
  7.2 18.8 %copy-start.5 = (bf16[2,4,6,9216]{3,1,2,0:T(4,128)(2,1)S(1)}, bf16[2,4,6,9216]{3,1,2,0:T(4,128)(2,1)}, u32[]{:S(2)}) copy-start(bf16[2,4,6,9216]{3,1,2,0:T(4,128)(2,1)} %param.6) | copy-start | bytes 2654212
  7.2 60.6 %all-gather.3.cloned.1.call-start = ((), (), s32[]{:S(2)}) async-start(), calls=%async_computation.9 | async-start | bytes 1990656 | tf_op jit(solution)/shard_map/all_gather | solution.py:219
  7.9 97.1 %all-gather.5.cloned.1.call-start = ((), (), s32[]{:S(2)}) async-start(), calls=%async_computation.10 | async-start | bytes 6684672 | tf_op jit(solution)/shard_map/all_gather | solution.py:231
  26.0 1.5 copy-start.7
  38.7 9.6 %copy-start.6 = (bf16[2,1,128,1024]{3,2,1,0:T(8,128)(2,1)S(1)}, bf16[2,1,128,1024]{3,2,1,0:T(8,128)(2,1)}, u32[]{:S(2)}) copy-start(bf16[2,1,128,1024]{3,2,1,0:T(8,128)(2,1)} %param.11) | copy-start | bytes 1572868
  40.5 20.1 %all-to-all-start = ((bf16[2,16,12,896]{3,0,2,1:T(2,128)(2,1)}), bf16[2,16,12,896]{3,0,2,1:T(2,128)(2,1)S(1)}, u32[]{:S(2)}, u32[]{:S(2)}) async-start(bf16[2,16,12,896]{3,0,2,1:T(2,128)(2,1)} %bitcast.7), calls=%async_computation | async-start | bytes 1376256 | tf_op jit(solution)/shard_map/all_to_all | solution.py:210
  60.5 61.2 %all-to-all-start.2 = ((bf16[16,2,128,64]{2,3,1,0:T(8,128)(2,1)}), bf16[16,2,128,64]{2,3,1,0:T(8,128)(2,1)}, u32[]{:S(2)}, u32[]{:S(2)}) async-start(bf16[16,2,128,64]{2,3,1,0:T(8,128)(2,1)} %copy.57), calls=%async_computation.2 | async-start | bytes 1048576 | tf_op jit(solution)/shard_map/all_to_all | solution.py:238
  67.8 7.9 %copy-start.3 = (bf16[2,128,864]{2,1,0:T(8,128)(2,1)}, bf16[2,128,864]{2,1,0:T(8,128)(2,1)S(1)}, u32[]{:S(2)}) copy-start(bf16[2,128,864]{2,1,0:T(8,128)(2,1)S(1)} %copy.50) | copy-start | bytes 1327108
  76.4 40.7 %copy-start.1 = (bf16[256,1024]{1,0:T(8,128)(2,1)}, bf16[256,1024]{1,0:T(8,128)(2,1)S(1)}, u32[]{:S(2)}) copy-start(bf16[256,1024]{1,0:T(8,128)(2,1)S(1)} %get-tuple-element.9) | copy-start | bytes 1572868
  121.7 25.8 %all-to-all-start.1 = ((bf16[16,2,128,192]{2,3,1,0:T(8,128)(2,1)}), bf16[16,2,128,192]{2,3,1,0:T(8,128)(2,1)}, u32[]{:S(2)}, u32[]{:S(2)}) async-start(bf16[16,2,128,192]{2,3,1,0:T(8,128)(2,1)} %copy.55), calls=%async_computation.1 | async-start | bytes 3145728 | tf_op jit(solution)/shard_map/all_to_all | solution.py:237
  126.8 183.3 %reduce-scatter.2.cloned.1.call-start = ((), (), s32[]{:S(2)}) async-start(), calls=%async_computation.11 | async-start | bytes 6684672 | tf_op jit(solution)/shard_map/reduce_scatter | solution.py:246
  187.6 1.4 copy-start
  216.0 1.6 copy-start.2
  222.4 4.9 %copy-start.4 = (bf16[2,128,864]{2,1,0:T(8,128)(2,1)S(1)}, bf16[2,128,864]{2,1,0:T(8,128)(2,1)}, u32[]{:S(2)}) copy-start(bf16[2,128,864]{2,1,0:T(8,128)(2,1)} %copy-done.3) | copy-start | bytes 1327108
  274.9 37.0 %all-to-all-start.7 = ((f32[16,54,128]{2,1,0:T(8,128)}), f32[16,54,128]{2,1,0:T(8,128)S(1)}, u32[]{:S(2)}, u32[]{:S(2)}) async-start(f32[16,54,128]{2,1,0:T(8,128)} %broadcast_in_dim.20), calls=%async_computation.8 | async-start | bytes 917504 | tf_op jit(solution)/shard_map/all_to_all | solution.py:282
  311.9 14.3 %all-to-all-start.4 = ((bf16[8,64,384]{2,1,0:T(8,128)(2,1)}), bf16[8,64,384]{2,1,0:T(8,128)(2,1)S(1)}, u32[]{:S(2)}, u32[]{:S(2)}) async-start(bf16[8,64,384]{2,1,0:T(8,128)(2,1)} %bitcast.80), calls=%async_computation.5 | async-start | bytes 786432 | tf_op jit(solution)/shard_map/all_to_all | solution.py:254
Sparse Core Ops, SparseCore 0:
  9.7 29.2 all-gather.2
  41.1 63.8 all-gather.4
  222.5 87.5 reduce-scatter.1

commit v6 on v5

--- a/solution.py
+++ b/solution.py
@@ -110,20 +110,24 @@
     upstream = g_ref[:, 0, :, :].reshape(block, HD)
     key_rows = k_s[...]
     value_rows = v_s[...]
-    scores = contract(queries, key_rows, 1, 1) * factor
+    scores = contract(queries * jnp.asarray(factor, queries.dtype), key_rows, 1, 1)
     raised = jnp.exp(scores - jnp.max(scores, axis=1, keepdims=True))
     attention = raised / jnp.sum(raised, axis=1, keepdims=True)
     d_attention = contract(upstream, value_rows, 1, 1)
     inner_sum = jnp.sum(attention * d_attention, axis=1, keepdims=True)
-    d_scores = (attention * (d_attention - inner_sum) * factor).astype(jnp.bfloat16)
-    grad_query = contract(d_scores, key_rows, 1, 0).astype(jnp.bfloat16)
-    out_ref[pl.ds(first, per_block), 0, :, 0:HD] = grad_query.reshape(per_block, slots, HD)
+    d_scores = (attention * (d_attention - inner_sum)).astype(jnp.bfloat16)
+    grad_query = contract(d_scores, key_rows, 1, 0) * factor
+    out_ref[pl.ds(first, per_block), 0, :, 0:HD] = grad_query.astype(jnp.bfloat16).reshape(
+        per_block, slots, HD
+    )
     dk_acc[...] += contract(d_scores, queries, 0, 0)
     dv_acc[...] += contract(attention.astype(jnp.bfloat16), upstream, 0, 0)
 
     @pl.when(step == pl.num_programs(1) - 1)
     def _():
-        out_ref[:, 0, :, HD : 2 * HD] = dk_acc[...].astype(jnp.bfloat16).reshape(owners, slots, HD)
+        out_ref[:, 0, :, HD : 2 * HD] = (dk_acc[...] * factor).astype(jnp.bfloat16).reshape(
+            owners, slots, HD
+        )
         out_ref[:, 0, :, 2 * HD : 3 * HD] = dv_acc[...].astype(jnp.bfloat16).reshape(owners, slots, HD)
 
 
@@ -243,16 +247,19 @@
         .transpose(1, 2, 3, 0, 4)
         .reshape(row_total, 3 * D)
     )
-    my_rows = lax.psum_scatter(
-        contract(hidden, d_packed, 0, 0).astype(jnp.bfloat16),
-        "space",
-        scatter_dimension=0,
-        tiled=True,
-    )
+    col_block = 3 * D // tm_count
+    parity = lax.axis_index("tm") % 2
+    partial = contract(hidden, d_packed, 0, 0).reshape(D, tm_count // 2, 2, col_block)
+    kept = jnp.where(parity == 0, partial[:, :, 0], partial[:, :, 1])
+    given = jnp.where(parity == 0, partial[:, :, 1], partial[:, :, 0]).astype(jnp.bfloat16)
+    partner = [(index, index ^ 1) for index in range(tm_count)]
+    pair_sum = (kept + lax.ppermute(given, "tm", partner).astype(jnp.float32)).astype(jnp.bfloat16)
+    my_rows = lax.psum_scatter(pair_sum, "space", scatter_dimension=0, tiled=True)
     row_block = my_rows.shape[0]
-    col_block = 3 * D // tm_count
+    side = (jnp.arange(2, dtype=jnp.int32) == parity)[None, :, None, None]
+    outgoing = jnp.where(side, my_rows.transpose(1, 0, 2)[:, None], jnp.zeros((), jnp.bfloat16))
     qkv_parts = lax.all_to_all(
-        my_rows.reshape(row_block, tm_count, col_block).transpose(1, 0, 2),
+        outgoing.reshape(tm_count, row_block, col_block),
         "tm",
         split_axis=0,
         concat_axis=0,

time: 335 us -> 338 us (level)
  blocking collectives: 85.3 us -> 55.4 us
  waiting for transfers between devices: 95.4 us -> 116 us
  other arithmetic: 3.17 us -> 10.7 us
  starting transfers between devices: 31.5 us -> 36.9 us
    all_to_all x1 -> x0, blocking collectives: 23.9 us -> none  [body(): lax.all_to_all(grads, 'space', split_axis=0, concat_axis=0, tiled=True)]
    all_to_all x1 -> x2, waiting for transfers between devices: 6.66 us -> 26.9 us  [the longest x1 20.3 us: body(): lax.all_to_all(grads, 'space', split_axis=0, concat_axis=0, tiled=True)]
    reduce_scatter x1, waiting for transfers between devices: 29.4 us -> 21.8 us  [body(): lax.psum_scatter(pair_sum, 'space', scatter_dimension=0, tiled=True)]
    all_to_all x1, blocking collectives: 31.6 us -> 25.6 us  [body(): lax.all_to_all(embed_partial.astype(jnp.bfloat16).reshape(PATCH, tm_count...]
    ppermute x0 -> x1, waiting for transfers between devices: none -> 5.42 us  [body(): lax.ppermute(given, 'tm', partner).astype(jnp.float32)]
    convert_element_type x0 -> x2, other arithmetic: none -> 5.02 us  [the longest x1 4.44 us: body(): (kept + lax.ppermute(given, 'tm', partner).astype(jnp.float32)).astype(jn...]
    ppermute x0 -> x1, starting transfers between devices: none -> 4.09 us  [body(): lax.ppermute(given, 'tm', partner).astype(jnp.float32)]
    unnamed x22 -> x25, local copies, waits for them, and re-layouts: 2.2 us -> 6.26 us
  transfers between devices with their start and end apart: 8 -> 10, of which waited for: 5 -> 7; matrix products, arithmetic and copies ran while one was open for 14% -> 14% of each run, Pallas kernels for 3% -> 3%
where the time goes in v6:
time: 338 us; the launch traced here: 337 us
  waiting for transfers between devices  116 us (34%)
  blocking collectives  55.4 us (16%)
  local copies, waits for them, and re-layouts  46.2 us (14%)
  Pallas kernels  46 us (14%)
  starting transfers between devices  36.9 us (11%)
  between operations  14.2 us (4%)
  matrix products  11.6 us (3%)
  other arithmetic  10.7 us (3%)
    pallas_call x1, Pallas kernels, attention_grads(): pl.pallas_call(attention_kernel, grid=(windows, owners // per_block), in_...  36.6 us
    all_gather x1, waiting for transfers between devices, body(): full_qkv = lax.all_gather(wide_rows, 'space', axis=0, tiled=True)  26.4 us
    all_to_all x1, blocking collectives, body(): lax.all_to_all(embed_partial.astype(jnp.bfloat16).reshape(PATCH, tm_count...  25.6 us
    reduce_scatter x1, waiting for transfers between devices, body(): lax.psum_scatter(pair_sum, 'space', scatter_dimension=0, tiled=True)  21.8 us
    all_to_all x1, waiting for transfers between devices, body(): lax.all_to_all(lanes_out, 'space', split_axis=0, concat_axis=0, tiled=True)  21.3 us
    all_to_all x1, waiting for transfers between devices, body(): lax.all_to_all(grads, 'space', split_axis=0, concat_axis=0, tiled=True)  20.3 us
    all_gather x1, blocking collectives, body(): wide_rows = lax.all_gather(qkv_weight, 'tm', axis=1, tiled=True)  16 us
    all_to_all x1, blocking collectives, body(): lax.all_to_all(padded.reshape(slab_count, chunk, -1), 'space', split_axis...  13.8 us
  transfers between devices with their start and end apart: 10, of which 7 were waited for; matrix products, arithmetic and copies ran while one was open for 14% of the time, Pallas kernels for 3%

profile of v6, /device:TPU:1, one launch (start us, length us, event | category | flops | bytes accessed | tf_op | source)
XLA Modules:
  0.0 337.0 jit_solution(18278886338074690345)
XLA Ops:
  7.9 16.0 %all_gather.10 = bf16[64,3072]{1,0:T(8,128)(2,1)} all-gather(bf16[64,384]{1,0:T(8,128)(2,1)} %param.10), channel_id=1, replica_groups=mesh['space'=16,'tm'=8] {'tm'}, dimensions={1}, use_global_device_ids=true | all-gather | bytes 442368 | tf_op jit(solution)/shard_map/all_gather | solution.py:234
  24.0 0.7 fusion.40
  25.6 0.7 fusion.44
  27.4 1.4 copy.83
  28.9 1.2 reshape.243.rows_ref
  30.5 9.4 %shard_map.77 = bf16[2,256,864]{2,1,0:T(8,128)(2,1)S(1)} custom-call(bf16[2,4,576,96]{3,2,1,0:T(8,128)(2,1)S(1)} %reshape.243.rows_ref, bf16[2,96,1536]{2,1,0:T(8,128)(2,1)S(1)} %fusion.9.pick_ref, bf16[2,96,1536]{2,1,0:T(8,128)(2,1)S(1)} %reshape.244.keep_ref, bf16[36,576]{1,0:T(8,128)(2,1)S(1)} %reshape.259.fold_ref), custom_call_target="tpu_custom_call" | custom-call | flops 2717908992 | bytes 1769472 | tf_op jit(solution)/shard_map/pallas_call | solution.py:67
  40.6 1.6 copy.85
  42.3 7.8 %all-to-all-start = ((bf16[2,16,12,896]{3,0,2,1:T(2,128)(2,1)}), bf16[2,16,12,896]{3,0,2,1:T(2,128)(2,1)S(1)}, u32[]{:S(2)}, u32[]{:S(2)}) async-start(bf16[2,16,12,896]{3,0,2,1:T(2,128)(2,1)} %bitcast.7), calls=%async_computation | async-start | bytes 1376256 | tf_op jit(solution)/shard_map/all_to_all | solution.py:214
  50.4 0.9 copy.95
  51.3 13.4 %all-to-all-done = bf16[2,16,12,896]{3,0,2,1:T(2,128)(2,1)S(1)} async-done(((bf16[2,16,12,896]{3,0,2,1:T(2,128)(2,1)}), bf16[2,16,12,896]{3,0,2,1:T(2,128)(2,1)S(1)}, u32[]{:S(2)}, u32[]{:S(2)}) %all-to-all-start) | async-done | bytes 688160 | tf_op jit(solution)/shard_map/all_to_all | solution.py:214
  64.6 5.9 %all-to-all-start.2 = ((bf16[16,2,128,64]{2,3,1,0:T(8,128)(2,1)}), bf16[16,2,128,64]{2,3,1,0:T(8,128)(2,1)}, u32[]{:S(2)}, u32[]{:S(2)}) async-start(bf16[16,2,128,64]{2,3,1,0:T(8,128)(2,1)} %copy.95), calls=%async_computation.2 | async-start | bytes 1048576 | tf_op jit(solution)/shard_map/all_to_all | solution.py:242
  71.7 2.7 reshape.248
  74.4 2.5 copy.89
  76.9 2.8 reshape.249
  79.7 0.8 convert_reduce_fusion.1
  80.8 26.4 %all-gather.5.cloned.1.call-done = bf16[1024,3072]{1,0:T(8,128)(2,1)} async-done(((bf16[64,3072]{1,0:T(8,128)(2,1)}), bf16[1024,3072]{1,0:T(8,128)(2,1)}) %all-gather.5.cloned.1.call-update) | async-done | bytes 6291472 | tf_op jit(solution)/shard_map/all_gather | solution.py:235
  107.2 8.6 %copy.90 = bf16[1024,3072]{0,1:T(8,128)(2,1)} copy(bf16[1024,3072]{1,0:T(8,128)(2,1)} %all-gather.5.cloned.1.call-done) | data formatting | bytes 12582912 | tf_op jit(solution)/shard_map/all_gather | solution.py:235
  115.9 3.5 %copy.91 = bf16[1024,16,3,64]{0,3,2,1:T(8,128)(2,1)S(1)} copy(bf16[1024,16,3,64]{0,3,1,2:T(8,128)(2,1)} %bitcast.111) | data formatting | bytes 12582912 | tf_op jit(solution)/shard_map/transpose | solution.py:237
  119.4 1.9 convolution_convert_fusion
  121.3 0.7 copy.92
  122.5 1.5 copy.93
  124.0 4.4 %all-to-all-start.1 = ((bf16[16,2,128,192]{2,3,1,0:T(8,128)(2,1)}), bf16[16,2,128,192]{2,3,1,0:T(8,128)(2,1)}, u32[]{:S(2)}, u32[]{:S(2)}) async-start(bf16[16,2,128,192]{2,3,1,0:T(8,128)(2,1)} %copy.93), calls=%async_computation.1 | async-start | bytes 3145728 | tf_op jit(solution)/shard_map/all_to_all | solution.py:241
  128.4 1.5 copy.97.g_ref
  129.9 21.3 %all-to-all-done.1 = bf16[16,2,128,192]{2,3,1,0:T(8,128)(2,1)} async-done(((bf16[16,2,128,192]{2,3,1,0:T(8,128)(2,1)}), bf16[16,2,128,192]{2,3,1,0:T(8,128)(2,1)}, u32[]{:S(2)}, u32[]{:S(2)}) %all-to-all-start.1) | async-done | bytes 1572896 | tf_op jit(solution)/shard_map/all_to_all | solution.py:241
  151.3 2.7 copy.96.lanes_ref
  154.0 36.6 %shard_map.78 = bf16[16,2,128,192]{3,2,1,0:T(8,128)(2,1)S(1)} custom-call(bf16[16,2,128,192]{3,2,1,0:T(8,128)(2,1)S(1)} %copy.96.lanes_ref, bf16[16,2,128,64]{3,2,1,0:T(8,128)(2,1)S(1)} %copy.97.g_ref), custom_call_target="tpu_custom_call" | custom-call | flops 5368709120 | bytes 3670016 | tf_op jit(solution)/shard_map/pallas_call | solution.py:141
  190.6 1.3 copy-done
  191.9 3.9 %copy.98 = bf16[16,2,128,192]{2,3,1,0:T(8,128)(2,1)} copy(bf16[16,2,128,192]{3,2,1,0:T(8,128)(2,1)} %copy-done) | data formatting | bytes 3145728 | tf_op jit(solution)/shard_map/pallas_call | solution.py:141
  195.8 3.7 %all-to-all-start.3 = ((bf16[16,2,128,192]{2,3,1,0:T(8,128)(2,1)}), bf16[16,2,128,192]{2,3,1,0:T(8,128)(2,1)S(1)}, u32[]{:S(2)}, u32[]{:S(2)}) async-start(bf16[16,2,128,192]{2,3,1,0:T(8,128)(2,1)} %copy.98), calls=%async_computation.3 | async-start | bytes 3145728 | tf_op jit(solution)/shard_map/all_to_all | solution.py:244
  199.8 20.3 %all-to-all-done.3 = bf16[16,2,128,192]{2,3,1,0:T(8,128)(2,1)S(1)} async-done(((bf16[16,2,128,192]{2,3,1,0:T(8,128)(2,1)}), bf16[16,2,128,192]{2,3,1,0:T(8,128)(2,1)S(1)}, u32[]{:S(2)}, u32[]{:S(2)}) %all-to-all-start.3) | async-done | bytes 1572896 | tf_op jit(solution)/shard_map/all_to_all | solution.py:244
  220.1 1.6 copy.99
  221.9 0.9 copy-done.1
  223.1 2.0 fusion.19
  225.7 4.1 %collective-permute-start = (bf16[1024,4,384]{2,0,1:T(8,128)(2,1)S(1)}, bf16[1024,4,384]{2,0,1:T(8,128)(2,1)}, u32[]{:S(2)}, u32[]{:S(2)}) collective-permute-start(bf16[1024,4,384]{2,0,1:T(8,128)(2,1)S(1)} %fusion.3), channel_id=1, source_target_pairs={{0,1},{1,0},{2,3},{3,2},{4,5},{5,4},{6,7},{7,6},{8,9},{9,8},{10,11... | collective-permute-start | bytes 9437192 | tf_op jit(solution)/shard_map/ppermute | solution.py:256
  229.8 5.4 %collective-permute-done = bf16[1024,4,384]{2,0,1:T(8,128)(2,1)} collective-permute-done((bf16[1024,4,384]{2,0,1:T(8,128)(2,1)S(1)}, bf16[1024,4,384]{2,0,1:T(8,128)(2,1)}, u32[]{:S(2)}, u32[]{:S(2)}) %collective-permute-start) | collective-permute-done | bytes 3145760 | tf_op jit(solution)/shard_map/ppermute | solution.py:256
  235.2 4.4 %fusion.2 = bf16[1024,4,384]{2,0,1:T(8,128)(2,1)} fusion(bf16[1024,4,384]{2,0,1:T(8,128)(2,1)} %collective-permute-done, f32[1024,4,2,384]{3,0,2,1:T(8,128)S(1)} %fusion.19, pred[]{:T(512)S(6)} %eq.130), kind=kLoop, calls=%fused_computation.3 | loop fusion | flops 6291456 | bytes 18874368 | tf_op jit(solution)/shard_map/convert_element_type | solution.py:256
  239.7 1.4 copy-done.2
  241.2 4.9 %fusion.48 = (f32[256]{0:T(256)S(1)}, f32[256]{0:T(256)S(1)}, f32[256,1024]{1,0:T(8,128)S(1)}) fusion(f32[256]{0:T(256)S(1)} %add_rsqrt_fusion, f32[256]{0:T(256)S(1)} %broadcast_multiply_fusion.2, bf16[256,1024]{1,0:T(8,128)(2,1)S(1)} %copy-done.5, bf16[1024,3072]{1,0:T(8,128)(2,1)} %all-gather.5.cloned.1.call-done, bf16[384,8,2,128]{3,2,1,0:T(2,128)(2,1)S(1)} %bitcast.117), kind=kOutput, calls=%fused_computation.102 | convolution fusion | flops 1612185088 | bytes 9441280 | tf_op jit(solution)/shard_map/dot_general | solution.py:26
  246.1 0.9 convert_bitcast_fusion
  247.3 25.6 %all_to_all.40 = bf16[8,864,128]{2,1,0:T(8,128)(2,1)S(1)} all-to-all(bf16[8,864,128]{2,1,0:T(8,128)(2,1)S(1)} %bitcast.113), channel_id=1, replica_groups=mesh['space'=16,'tm'=8] {'tm'}, dimensions={0} | all-to-all | bytes 3538944 | tf_op jit(solution)/shard_map/all_to_all | solution.py:275
  273.2 13.8 %all_to_all.41 = f32[16,54,128]{2,1,0:T(8,128)S(1)} all-to-all(f32[16,54,128]{2,1,0:T(8,128)S(1)} %reshape.257), channel_id=1, replica_groups=mesh['space'=16,'tm'=8] {'space'}, dimensions={0} | all-to-all | bytes 884736 | tf_op jit(solution)/shard_map/all_to_all | solution.py:285
  287.0 0.8 broadcast_in_dim.85
  287.8 4.0 %all-to-all-start.7 = ((f32[16,54,128]{2,1,0:T(8,128)}), f32[16,54,128]{2,1,0:T(8,128)S(1)}, u32[]{:S(2)}, u32[]{:S(2)}) async-start(f32[16,54,128]{2,1,0:T(8,128)} %broadcast_in_dim.85), calls=%async_computation.8 | async-start | bytes 917504 | tf_op jit(solution)/shard_map/all_to_all | solution.py:289
  291.9 21.8 %reduce-scatter.2.cloned.1.call-done = bf16[64,4,384]{2,0,1:T(8,128)(2,1)} async-done(((bf16[1024,4,384]{2,0,1:T(8,128)(2,1)}), bf16[64,4,384]{2,0,1:T(8,128)(2,1)}) %reduce-scatter.2.cloned.1.call-update) | async-done | bytes 196624 | tf_op jit(solution)/shard_map/reduce_scatter | solution.py:257
  313.7 1.8 bitcast_select_fusion.1
  315.5 6.6 %all-to-all-start.4 = ((bf16[8,64,384]{2,1,0:T(8,128)(2,1)}), bf16[8,64,384]{2,1,0:T(8,128)(2,1)S(1)}, u32[]{:S(2)}, u32[]{:S(2)}) async-start(bf16[8,64,384]{2,1,0:T(8,128)(2,1)} %bitcast_select_fusion.1), calls=%async_computation.5 | async-start | bytes 786432 | tf_op jit(solution)/shard_map/all_to_all | solution.py:261
  322.3 0.8 reshape.258
  323.1 6.7 %all-to-all-done.4 = bf16[8,64,384]{2,1,0:T(8,128)(2,1)S(1)} async-done(((bf16[8,64,384]{2,1,0:T(8,128)(2,1)}), bf16[8,64,384]{2,1,0:T(8,128)(2,1)S(1)}, u32[]{:S(2)}, u32[]{:S(2)}) %all-to-all-start.4) | async-done | bytes 393248 | tf_op jit(solution)/shard_map/all_to_all | solution.py:261
  (73 shorter events, 9.0 us)
Async XLA Ops:
  7.2 64.6 %all-gather.3.cloned.1.call-start = ((), (), s32[]{:S(2)}) async-start(), calls=%async_computation.9 | async-start | bytes 1990656 | tf_op jit(solution)/shard_map/all_gather | solution.py:223
  7.9 99.3 %all-gather.5.cloned.1.call-start = ((), (), s32[]{:S(2)}) async-start(), calls=%async_computation.10 | async-start | bytes 6684672 | tf_op jit(solution)/shard_map/all_gather | solution.py:235
  40.5 9.6 %copy-start.8 = (bf16[2,1,128,1024]{3,2,1,0:T(8,128)(2,1)S(1)}, bf16[2,1,128,1024]{3,2,1,0:T(8,128)(2,1)}, u32[]{:S(2)}) copy-start(bf16[2,1,128,1024]{3,2,1,0:T(8,128)(2,1)} %param.11) | copy-start | bytes 1572868
  42.3 22.4 %all-to-all-start = ((bf16[2,16,12,896]{3,0,2,1:T(2,128)(2,1)}), bf16[2,16,12,896]{3,0,2,1:T(2,128)(2,1)S(1)}, u32[]{:S(2)}, u32[]{:S(2)}) async-start(bf16[2,16,12,896]{3,0,2,1:T(2,128)(2,1)} %bitcast.7), calls=%async_computation | async-start | bytes 1376256 | tf_op jit(solution)/shard_map/all_to_all | solution.py:214
  64.6 59.4 %all-to-all-start.2 = ((bf16[16,2,128,64]{2,3,1,0:T(8,128)(2,1)}), bf16[16,2,128,64]{2,3,1,0:T(8,128)(2,1)}, u32[]{:S(2)}, u32[]{:S(2)}) async-start(bf16[16,2,128,64]{2,3,1,0:T(8,128)(2,1)} %copy.95), calls=%async_computation.2 | async-start | bytes 1048576 | tf_op jit(solution)/shard_map/all_to_all | solution.py:242
  71.7 8.0 %copy-start.6 = (bf16[2,128,864]{2,1,0:T(8,128)(2,1)}, bf16[2,128,864]{2,1,0:T(8,128)(2,1)S(1)}, u32[]{:S(2)}) copy-start(bf16[2,128,864]{2,1,0:T(8,128)(2,1)S(1)} %copy.88) | copy-start | bytes 1327108
  80.5 38.9 %copy-start.3 = (bf16[256,1024]{1,0:T(8,128)(2,1)}, bf16[256,1024]{1,0:T(8,128)(2,1)S(1)}, u32[]{:S(2)}) copy-start(bf16[256,1024]{1,0:T(8,128)(2,1)S(1)} %get-tuple-element.9) | copy-start | bytes 1572868
  124.0 27.3 %all-to-all-start.1 = ((bf16[16,2,128,192]{2,3,1,0:T(8,128)(2,1)}), bf16[16,2,128,192]{2,3,1,0:T(8,128)(2,1)}, u32[]{:S(2)}, u32[]{:S(2)}) async-start(bf16[16,2,128,192]{2,3,1,0:T(8,128)(2,1)} %copy.93), calls=%async_computation.1 | async-start | bytes 3145728 | tf_op jit(solution)/shard_map/all_to_all | solution.py:241
  190.6 1.4 copy-start
  195.8 24.3 %all-to-all-start.3 = ((bf16[16,2,128,192]{2,3,1,0:T(8,128)(2,1)}), bf16[16,2,128,192]{2,3,1,0:T(8,128)(2,1)S(1)}, u32[]{:S(2)}, u32[]{:S(2)}) async-start(bf16[16,2,128,192]{2,3,1,0:T(8,128)(2,1)} %copy.98), calls=%async_computation.3 | async-start | bytes 3145728 | tf_op jit(solution)/shard_map/all_to_all | solution.py:244
  199.5 114.2 %reduce-scatter.2.cloned.1.call-start = ((), (), s32[]{:S(2)}) async-start(), calls=%async_computation.11 | async-start | bytes 3342336 | tf_op jit(solution)/shard_map/reduce_scatter | solution.py:257
  221.7 1.2 copy-start.1
  221.7 1.4 copy-start.4
  225.7 9.5 %collective-permute-start = (bf16[1024,4,384]{2,0,1:T(8,128)(2,1)S(1)}, bf16[1024,4,384]{2,0,1:T(8,128)(2,1)}, u32[]{:S(2)}, u32[]{:S(2)}) collective-permute-start(bf16[1024,4,384]{2,0,1:T(8,128)(2,1)S(1)} %fusion.3), channel_id=1, source_target_pairs={{0,1},{1,0},{2,3},{3,2},{4,5},{5,4},{6,7},{7,6},{8,9},{9,8},{10,11... | collective-permute-start | bytes 9437192 | tf_op jit(solution)/shard_map/ppermute | solution.py:256
  239.7 1.4 copy-start.2
  239.7 1.5 copy-start.5
  241.2 4.9 %copy-start.7 = (bf16[2,128,864]{2,1,0:T(8,128)(2,1)S(1)}, bf16[2,128,864]{2,1,0:T(8,128)(2,1)}, u32[]{:S(2)}) copy-start(bf16[2,128,864]{2,1,0:T(8,128)(2,1)} %copy-done.6) | copy-start | bytes 1327108
  287.8 27.7 %all-to-all-start.7 = ((f32[16,54,128]{2,1,0:T(8,128)}), f32[16,54,128]{2,1,0:T(8,128)S(1)}, u32[]{:S(2)}, u32[]{:S(2)}) async-start(f32[16,54,128]{2,1,0:T(8,128)} %broadcast_in_dim.85), calls=%async_computation.8 | async-start | bytes 917504 | tf_op jit(solution)/shard_map/all_to_all | solution.py:289
  315.5 14.3 %all-to-all-start.4 = ((bf16[8,64,384]{2,1,0:T(8,128)(2,1)}), bf16[8,64,384]{2,1,0:T(8,128)(2,1)S(1)}, u32[]{:S(2)}, u32[]{:S(2)}) async-start(bf16[8,64,384]{2,1,0:T(8,128)(2,1)} %bitcast_select_fusion.1), calls=%async_computation.5 | async-start | bytes 786432 | tf_op jit(solution)/shard_map/all_to_all | solution.py:261
Sparse Core Ops, SparseCore 0:
  9.6 29.1 all-gather.2
  41.0 66.1 all-gather.4
  239.8 73.8 reduce-scatter.1

commit v7 on v6

--- a/solution.py
+++ b/solution.py
@@ -85,6 +85,21 @@
             bytes_accessed=rows.size * 2 + windows * lanes_b * PATCH * 2,
         ),
     )(rows, pick_z, keep_y, fold)
+
+
+def halving_sum(array, steps):
+    for axis_name, count, bit, axis in steps:
+        index = lax.axis_index(axis_name)
+        side = (index >> bit) & 1
+        keep = jnp.squeeze(lax.dynamic_slice_in_dim(array, side, 1, axis=axis), axis)
+        send = jnp.squeeze(lax.dynamic_slice_in_dim(array, 1 - side, 1, axis=axis), axis)
+        partner = [(i, i ^ (1 << bit)) for i in range(count)]
+        array = keep + lax.ppermute(send.astype(jnp.bfloat16), axis_name, partner).astype(jnp.float32)
+    return array
+
+
+def bits_of(count):
+    return count.bit_length() - 1
 
 
 QUERY_BLOCK = 256
@@ -247,39 +262,41 @@
         .transpose(1, 2, 3, 0, 4)
         .reshape(row_total, 3 * D)
     )
-    col_block = 3 * D // tm_count
-    parity = lax.axis_index("tm") % 2
-    partial = contract(hidden, d_packed, 0, 0).reshape(D, tm_count // 2, 2, col_block)
-    kept = jnp.where(parity == 0, partial[:, :, 0], partial[:, :, 1])
-    given = jnp.where(parity == 0, partial[:, :, 1], partial[:, :, 0]).astype(jnp.bfloat16)
-    partner = [(index, index ^ 1) for index in range(tm_count)]
-    pair_sum = (kept + lax.ppermute(given, "tm", partner).astype(jnp.float32)).astype(jnp.bfloat16)
-    my_rows = lax.psum_scatter(pair_sum, "space", scatter_dimension=0, tiled=True)
-    row_block = my_rows.shape[0]
-    side = (jnp.arange(2, dtype=jnp.int32) == parity)[None, :, None, None]
-    outgoing = jnp.where(side, my_rows.transpose(1, 0, 2)[:, None], jnp.zeros((), jnp.bfloat16))
-    qkv_parts = lax.all_to_all(
-        outgoing.reshape(tm_count, row_block, col_block),
-        "tm",
-        split_axis=0,
-        concat_axis=0,
-        tiled=True,
-    )
-    d_qkv_weight = jnp.sum(qkv_parts.astype(jnp.float32), axis=0)
+    space_bits = bits_of(slab_count)
+    tm_bits = bits_of(tm_count)
+    assert (1 << space_bits) == slab_count and (1 << tm_bits) == tm_count
+    partial = contract(hidden, d_packed, 0, 0).reshape(
+        (2,) * space_bits + (D // slab_count,) + (2,) * tm_bits + (3 * D // tm_count,)
+    )
+
+    def space_axis(bit):
+        return space_bits - 1 - bit
+
+    def tm_axis(bit):
+        return space_bits + 1 + tm_bits - 1 - bit
+
+    order = [("tm", 0)] + [("space", b) for b in range(space_bits - 2, -1, -2)]
+    order += [("tm", b) for b in range(1, tm_bits - 1)]
+    order += [("space", b) for b in range(space_bits - 1, -1, -2)]
+    order += [("tm", b) for b in range(max(1, tm_bits - 1), tm_bits)]
+    steps = []
+    removed = []
+    for name, bit in order:
+        axis = space_axis(bit) if name == "space" else tm_axis(bit)
+        shift = sum(1 for done in removed if done < axis)
+        steps.append((name, slab_count if name == "space" else tm_count, bit, axis - shift))
+        removed.append(axis)
+    d_qkv_weight = halving_sum(partial, steps)
     d_hidden = contract(d_packed, full_qkv, 1, 1)
     first_mean = jnp.mean(d_hidden, axis=1, keepdims=True)
     second_mean = jnp.mean(d_hidden * normed, axis=1, keepdims=True)
     d_tokens = (inverse * (d_hidden - first_mean - normed * second_mean)).astype(jnp.bfloat16)
     embed_partial = contract(chosen, d_tokens, 0, 0)
-    embed_block = D // tm_count
-    embed_parts = lax.all_to_all(
-        embed_partial.astype(jnp.bfloat16).reshape(PATCH, tm_count, embed_block).transpose(1, 0, 2),
-        "tm",
-        split_axis=0,
-        concat_axis=0,
-        tiled=True,
-    )
-    embed_cols = jnp.sum(embed_parts.astype(jnp.float32), axis=0)
+    embed_partial = embed_partial.reshape((PATCH,) + (2,) * tm_bits + (D // tm_count,))
+    embed_steps = []
+    for bit in range(tm_bits):
+        embed_steps.append(("tm", tm_count, bit, tm_bits - bit))
+    embed_cols = halving_sum(embed_partial, embed_steps)
     chunk = -(-PATCH // slab_count)
     padded = jnp.pad(embed_cols, ((0, chunk * slab_count - PATCH), (0, 0)))
     spread = lax.all_to_all(

time: 338 us -> 371 us (1.098); the launches traced: 337 us -> 365 us
  blocking collectives: 55.4 us -> 16 us
  waiting for transfers between devices: 116 us -> 155 us
  local copies, waits for them, and re-layouts: 46.2 us -> 61.8 us
  other arithmetic: 10.7 us -> 17.6 us
  starting transfers between devices: 36.9 us -> 40.9 us
    ppermute x1 -> x10, waiting for transfers between devices: 5.42 us -> 60.8 us  [halving_sum(): lax.ppermute(send.astype(jnp.bfloat16), axis_name, partner)]
    all_to_all x2 -> x0, blocking collectives: 39.4 us -> none  [the longest x1 25.6 us: body(): lax.all_to_all(embed_partial.astype(jnp.bfloat16).reshape(PATCH, tm_count...]
    reduce_scatter x1 -> x0, waiting for transfers between devices: 21.8 us -> none  [body(): lax.psum_scatter(pair_sum, 'space', scatter_dimension=0, tiled=True)]
    add x0 -> x10, other arithmetic: none -> 13.5 us  [halving_sum(): keep + lax.ppermute(send.astype(jnp.bfloat16), axis_name, partner).astype...]
    unnamed x25 -> x29, local copies, waits for them, and re-layouts: 6.26 us -> 14.4 us
    ppermute x1 -> x10, starting transfers between devices: 4.09 us -> 11.4 us  [halving_sum(): lax.ppermute(send.astype(jnp.bfloat16), axis_name, partner)]
    all_to_all x1, waiting for transfers between devices: 0.01 us -> 6.41 us  [body(): lax.all_to_all(jnp.broadcast_to(reduced[None], (slab_count,) + reduced.sh...]
    convert_element_type x0 -> x11, local copies, waits for them, and re-layouts: none -> 6.06 us  [the longest x10 5.86 us: halving_sum(): send.astype(jnp.bfloat16)]
  transfers between devices with their start and end apart: 10 -> 18, of which waited for: 7 -> 11; matrix products, arithmetic and copies ran while one was open for 14% -> 15% of each run, Pallas kernels for 3% -> 3%
where the time goes in v7:
time: 371 us; the launch traced here: 365 us
  waiting for transfers between devices  155 us (42%)
  local copies, waits for them, and re-layouts  61.8 us (17%)
  Pallas kernels  46 us (12%)
  starting transfers between devices  40.9 us (11%)
  other arithmetic  17.6 us (5%)
  blocking collectives  16 us (4%)
  between operations  14.6 us (4%)
  matrix products  12.5 us (3%)
    ppermute x10, waiting for transfers between devices, halving_sum(): lax.ppermute(send.astype(jnp.bfloat16), axis_name, partner)  60.8 us
    pallas_call x1, Pallas kernels, attention_grads(): pl.pallas_call(attention_kernel, grid=(windows, owners // per_block), in_...  36.6 us
    all_gather x1, waiting for transfers between devices, body(): full_qkv = lax.all_gather(wide_rows, 'space', axis=0, tiled=True)  26.5 us
    all_to_all x1, waiting for transfers between devices, body(): lax.all_to_all(lanes_out, 'space', split_axis=0, concat_axis=0, tiled=True)  21.6 us
    all_to_all x1, waiting for transfers between devices, body(): lax.all_to_all(grads, 'space', split_axis=0, concat_axis=0, tiled=True)  20.4 us
    all_gather x1, blocking collectives, body(): wide_rows = lax.all_gather(qkv_weight, 'tm', axis=1, tiled=True)  16 us
    unnamed x29, local copies, waits for them, and re-layouts  14.4 us
    add x10, other arithmetic, halving_sum(): keep + lax.ppermute(send.astype(jnp.bfloat16), axis_name, partner).astype...  13.5 us
  transfers between devices with their start and end apart: 18, of which 11 were waited for; matrix products, arithmetic and copies ran while one was open for 15% of the time, Pallas kernels for 3%

profile of v7, /device:TPU:1, one launch (start us, length us, event | category | flops | bytes accessed | tf_op | source)
XLA Modules:
  0.0 364.7 jit_solution(8991722773333927696)
XLA Ops:
  7.9 16.0 %all_gather.10 = bf16[64,3072]{1,0:T(8,128)(2,1)} all-gather(bf16[64,384]{1,0:T(8,128)(2,1)} %param.10), channel_id=1, replica_groups=mesh['space'=16,'tm'=8] {'tm'}, dimensions={1}, use_global_device_ids=true | all-gather | bytes 442368 | tf_op jit(solution)/shard_map/all_gather | solution.py:249
  27.7 1.4 copy.51
  30.5 9.5 %shard_map.77 = bf16[2,256,864]{2,1,0:T(8,128)(2,1)S(1)} custom-call(bf16[2,4,576,96]{3,2,1,0:T(8,128)(2,1)S(1)} %reshape.240.rows_ref, bf16[2,96,1536]{2,1,0:T(8,128)(2,1)S(1)} %fusion.7.pick_ref, bf16[2,96,1536]{2,1,0:T(8,128)(2,1)S(1)} %reshape.241.keep_ref, bf16[36,576]{1,0:T(8,128)(2,1)S(1)} %reshape.255.fold_ref), custom_call_target="tpu_custom_call" | custom-call | flops 2717908992 | bytes 1769472 | tf_op jit(solution)/shard_map/pallas_call | solution.py:67
  40.7 1.6 copy.53
  42.3 7.8 %all-to-all-start = ((bf16[2,16,12,896]{3,0,2,1:T(2,128)(2,1)}), bf16[2,16,12,896]{3,0,2,1:T(2,128)(2,1)S(1)}, u32[]{:S(2)}, u32[]{:S(2)}) async-start(bf16[2,16,12,896]{3,0,2,1:T(2,128)(2,1)} %bitcast.7), calls=%async_computation | async-start | bytes 1376256 | tf_op jit(solution)/shard_map/all_to_all | solution.py:229
  51.2 13.0 %all-to-all-done = bf16[2,16,12,896]{3,0,2,1:T(2,128)(2,1)S(1)} async-done(((bf16[2,16,12,896]{3,0,2,1:T(2,128)(2,1)}), bf16[2,16,12,896]{3,0,2,1:T(2,128)(2,1)S(1)}, u32[]{:S(2)}, u32[]{:S(2)}) %all-to-all-start) | async-done | bytes 688160 | tf_op jit(solution)/shard_map/all_to_all | solution.py:229
  64.2 6.2 %all-to-all-start.2 = ((bf16[16,2,128,64]{2,3,1,0:T(8,128)(2,1)}), bf16[16,2,128,64]{2,3,1,0:T(8,128)(2,1)}, u32[]{:S(2)}, u32[]{:S(2)}) async-start(bf16[16,2,128,64]{2,3,1,0:T(8,128)(2,1)} %copy.64), calls=%async_computation.2 | async-start | bytes 1048576 | tf_op jit(solution)/shard_map/all_to_all | solution.py:257
  71.6 2.7 reshape.245
  74.3 2.5 copy.57
  76.8 2.9 reshape.246
  80.8 26.5 %all-gather.5.cloned.1.call-done = bf16[1024,3072]{1,0:T(8,128)(2,1)} async-done(((bf16[64,3072]{1,0:T(8,128)(2,1)}), bf16[1024,3072]{1,0:T(8,128)(2,1)}) %all-gather.5.cloned.1.call-update) | async-done | bytes 6291472 | tf_op jit(solution)/shard_map/all_gather | solution.py:250
  107.3 8.6 %copy.59 = bf16[1024,3072]{0,1:T(8,128)(2,1)} copy(bf16[1024,3072]{1,0:T(8,128)(2,1)} %all-gather.5.cloned.1.call-done) | data formatting | bytes 12582912 | tf_op jit(solution)/shard_map/all_gather | solution.py:250
  115.9 3.5 copy.60
  119.4 1.9 convolution_convert_fusion
  122.5 1.5 copy.62
  124.0 4.4 %all-to-all-start.1 = ((bf16[16,2,128,192]{2,3,1,0:T(8,128)(2,1)}), bf16[16,2,128,192]{2,3,1,0:T(8,128)(2,1)}, u32[]{:S(2)}, u32[]{:S(2)}) async-start(bf16[16,2,128,192]{2,3,1,0:T(8,128)(2,1)} %copy.62), calls=%async_computation.1 | async-start | bytes 3145728 | tf_op jit(solution)/shard_map/all_to_all | solution.py:256
  128.5 1.5 copy.66.g_ref
  130.0 21.6 %all-to-all-done.1 = bf16[16,2,128,192]{2,3,1,0:T(8,128)(2,1)} async-done(((bf16[16,2,128,192]{2,3,1,0:T(8,128)(2,1)}), bf16[16,2,128,192]{2,3,1,0:T(8,128)(2,1)}, u32[]{:S(2)}, u32[]{:S(2)}) %all-to-all-start.1) | async-done | bytes 1572896 | tf_op jit(solution)/shard_map/all_to_all | solution.py:256
  151.6 2.7 copy.65.lanes_ref
  154.3 36.6 %shard_map.78 = bf16[16,2,128,192]{3,2,1,0:T(8,128)(2,1)S(1)} custom-call(bf16[16,2,128,192]{3,2,1,0:T(8,128)(2,1)S(1)} %copy.65.lanes_ref, bf16[16,2,128,64]{3,2,1,0:T(8,128)(2,1)S(1)} %copy.66.g_ref), custom_call_target="tpu_custom_call" | custom-call | flops 5368709120 | bytes 3670016 | tf_op jit(solution)/shard_map/pallas_call | solution.py:156
  190.9 1.4 copy-done
  192.3 3.9 %copy.67 = bf16[16,2,128,192]{2,3,1,0:T(8,128)(2,1)} copy(bf16[16,2,128,192]{3,2,1,0:T(8,128)(2,1)} %copy-done) | data formatting | bytes 3145728 | tf_op jit(solution)/shard_map/pallas_call | solution.py:156
  196.2 3.9 %all-to-all-start.3 = ((bf16[16,2,128,192]{2,3,1,0:T(8,128)(2,1)}), bf16[16,2,128,192]{2,3,1,0:T(8,128)(2,1)S(1)}, u32[]{:S(2)}, u32[]{:S(2)}) async-start(bf16[16,2,128,192]{2,3,1,0:T(8,128)(2,1)} %copy.67), calls=%async_computation.3 | async-start | bytes 3145728 | tf_op jit(solution)/shard_map/all_to_all | solution.py:259
  200.1 20.4 %all-to-all-done.3 = bf16[16,2,128,192]{2,3,1,0:T(8,128)(2,1)S(1)} async-done(((bf16[16,2,128,192]{2,3,1,0:T(8,128)(2,1)}), bf16[16,2,128,192]{2,3,1,0:T(8,128)(2,1)S(1)}, u32[]{:S(2)}, u32[]{:S(2)}) %all-to-all-start.3) | async-done | bytes 1572896 | tf_op jit(solution)/shard_map/all_to_all | solution.py:259
  220.5 1.6 copy.68
  223.2 4.8 %fusion.48 = (f32[256]{0:T(256)S(1)}, f32[256]{0:T(256)S(1)}, f32[256,1024]{1,0:T(8,128)S(1)}) fusion(f32[256]{0:T(256)S(1)} %add_rsqrt_fusion, f32[256]{0:T(256)S(1)} %broadcast_multiply_fusion.2, bf16[256,1024]{1,0:T(8,128)(2,1)S(1)} %copy-done.7, bf16[1024,3072]{1,0:T(8,128)(2,1)} %all-gather.5.cloned.1.call-done, bf16[384,8,2,128]{3,2,1,0:T(2,128)(2,1)S(1)} %bitcast.137), kind=kOutput, calls=%fused_computation.116 | convolution fusion | flops 1612185088 | bytes 9441280 | tf_op jit(solution)/shard_map/dot_general | solution.py:26
  229.4 1.8 fusion.49
  231.3 4.5 %copy-done.1 = f32[2,2,2,2,64,2,2,2,384]{8,4,7,6,5,3,2,1,0:T(8,128)} copy-done((f32[2,2,2,2,64,2,2,2,384]{8,4,7,6,5,3,2,1,0:T(8,128)}, f32[2,2,2,2,64,2,2,2,384]{8,4,7,6,5,3,2,1,0:T(8,128)S(1)}, u32[]{:S(2)}) %copy-start.1) | copy-done | bytes 12582936
  236.3 4.1 %collective-permute-start = (bf16[2,2,2,2,64,2,2,384]{7,4,6,5,3,2,1,0:T(8,128)(2,1)S(1)}, bf16[2,2,2,2,64,2,2,384]{7,4,6,5,3,2,1,0:T(8,128)(2,1)}, u32[]{:S(2)}, u32[]{:S(2)}) collective-permute-start(bf16[2,2,2,2,64,2,2,384]{7,4,6,5,3,2,1,0:T(8,128)(2,1)S(1)} %fusion), channel_id=1, source_target_pairs={{0,1},{1,0},{2,3},{3,2},{4,5},{5,4},{6,7},{7,6},{8,9},{9,8},{10,11... | collective-permute-start | bytes 9437192 | tf_op jit(solution)/shard_map/ppermute | solution.py:97
  240.4 5.4 %collective-permute-done = bf16[2,2,2,2,64,2,2,384]{7,4,6,5,3,2,1,0:T(8,128)(2,1)} collective-permute-done((bf16[2,2,2,2,64,2,2,384]{7,4,6,5,3,2,1,0:T(8,128)(2,1)S(1)}, bf16[2,2,2,2,64,2,2,384]{7,4,6,5,3,2,1,0:T(8,128)(2,1)}, u32[]{:S(2)}, u32[]{:S(2)}) %collective-permute-start) | collective-permute-done | bytes 3145760 | tf_op jit(solution)/shard_map/ppermute | solution.py:97
  245.8 4.7 %bitcast_add_fusion = f32[2,2,2,2,64,2,2,384]{7,4,6,5,3,2,1,0:T(8,128)S(1)} fusion(bf16[2,2,2,2,64,2,2,384]{7,4,6,5,3,2,1,0:T(8,128)(2,1)} %collective-permute-done, f32[2,2,2,2,64,2,2,2,384]{8,4,7,6,5,3,2,1,0:T(8,128)} %copy-done.1, s32[]{:T(128)S(6)} %select_n.123), kind=kLoop, calls=%fused_computation | loop fusion | flops 3145728 | bytes 15728644 | tf_op jit(solution)/shard_map/add | solution.py:97
  250.5 2.6 copy-done.2
  253.2 1.5 fusion.1
  255.7 1.9 fusion.50
  259.0 31.6 %collective-permute-done.1 = bf16[2,2,2,64,2,2,384]{6,3,5,4,2,1,0:T(8,128)(2,1)} collective-permute-done((bf16[2,2,2,64,2,2,384]{6,3,5,4,2,1,0:T(8,128)(2,1)}, bf16[2,2,2,64,2,2,384]{6,3,5,4,2,1,0:T(8,128)(2,1)}, u32[]{:S(2)}, u32[]{:S(2)}) %collective-permute-start.1) | collective-permute-done | bytes 1572896 | tf_op jit(solution)/shard_map/ppermute | solution.py:97
  290.6 2.8 bitcast_add_fusion.1
  293.4 1.6 copy-done.3
  299.7 14.5 %collective-permute-done.2 = bf16[2,2,64,2,2,384]{5,2,4,3,1,0:T(8,128)(2,1)} collective-permute-done((bf16[2,2,64,2,2,384]{5,2,4,3,1,0:T(8,128)(2,1)}, bf16[2,2,64,2,2,384]{5,2,4,3,1,0:T(8,128)(2,1)}, u32[]{:S(2)}, u32[]{:S(2)}) %collective-permute-start.2) | collective-permute-done | bytes 786464 | tf_op jit(solution)/shard_map/ppermute | solution.py:97
  314.2 1.8 bitcast_add_fusion.3
  318.0 1.5 collective-permute-start.9
  319.5 6.2 %collective-permute-done.3 = bf16[2,2,64,2,384]{4,2,3,1,0:T(8,128)(2,1)} collective-permute-done((bf16[2,2,64,2,384]{4,2,3,1,0:T(8,128)(2,1)}, bf16[2,2,64,2,384]{4,2,3,1,0:T(8,128)(2,1)}, u32[]{:S(2)}, u32[]{:S(2)}) %collective-permute-start.3) | collective-permute-done | bytes 393248 | tf_op jit(solution)/shard_map/ppermute | solution.py:97
  327.1 3.0 collective-permute-done.9
  331.0 3.6 all-to-all-start.4
  334.6 2.8 collective-permute-start.5
  337.4 5.7 %all-to-all-done.4 = f32[16,54,128]{2,1,0:T(8,128)S(1)} async-done(((f32[16,54,128]{2,1,0:T(8,128)}), f32[16,54,128]{2,1,0:T(8,128)S(1)}, u32[]{:S(2)}, u32[]{:S(2)}) %all-to-all-start.4) | async-done | bytes 442400 | tf_op jit(solution)/shard_map/all_to_all | solution.py:302
  344.0 3.6 all-to-all-start.5
  347.7 2.1 collective-permute-start.6
  349.7 6.4 %all-to-all-done.5 = f32[16,54,128]{2,1,0:T(8,128)S(1)} async-done(((f32[16,54,128]{2,1,0:T(8,128)}), f32[16,54,128]{2,1,0:T(8,128)S(1)}, u32[]{:S(2)}, u32[]{:S(2)}) %all-to-all-start.5) | async-done | bytes 442400 | tf_op jit(solution)/shard_map/all_to_all | solution.py:306
  (104 shorter events, 27.6 us)
Async XLA Ops:
  7.2 64.4 %all-gather.3.cloned.1.call-start = ((), (), s32[]{:S(2)}) async-start(), calls=%async_computation.6 | async-start | bytes 1990656 | tf_op jit(solution)/shard_map/all_gather | solution.py:238
  7.9 99.4 %all-gather.5.cloned.1.call-start = ((), (), s32[]{:S(2)}) async-start(), calls=%async_computation.7 | async-start | bytes 6684672 | tf_op jit(solution)/shard_map/all_gather | solution.py:250
  40.5 9.6 %copy-start.10 = (bf16[2,1,128,1024]{3,2,1,0:T(8,128)(2,1)S(1)}, bf16[2,1,128,1024]{3,2,1,0:T(8,128)(2,1)}, u32[]{:S(2)}) copy-start(bf16[2,1,128,1024]{3,2,1,0:T(8,128)(2,1)} %param.11) | copy-start | bytes 1572868
  42.3 21.9 %all-to-all-start = ((bf16[2,16,12,896]{3,0,2,1:T(2,128)(2,1)}), bf16[2,16,12,896]{3,0,2,1:T(2,128)(2,1)S(1)}, u32[]{:S(2)}, u32[]{:S(2)}) async-start(bf16[2,16,12,896]{3,0,2,1:T(2,128)(2,1)} %bitcast.7), calls=%async_computation | async-start | bytes 1376256 | tf_op jit(solution)/shard_map/all_to_all | solution.py:229
  64.2 59.8 %all-to-all-start.2 = ((bf16[16,2,128,64]{2,3,1,0:T(8,128)(2,1)}), bf16[16,2,128,64]{2,3,1,0:T(8,128)(2,1)}, u32[]{:S(2)}, u32[]{:S(2)}) async-start(bf16[16,2,128,64]{2,3,1,0:T(8,128)(2,1)} %copy.64), calls=%async_computation.2 | async-start | bytes 1048576 | tf_op jit(solution)/shard_map/all_to_all | solution.py:257
  71.6 8.1 %copy-start.9 = (bf16[2,128,864]{2,1,0:T(8,128)(2,1)}, bf16[2,128,864]{2,1,0:T(8,128)(2,1)S(1)}, u32[]{:S(2)}) copy-start(bf16[2,128,864]{2,1,0:T(8,128)(2,1)S(1)} %copy.56) | copy-start | bytes 1327108
  80.5 39.0 %copy-start.6 = (bf16[256,1024]{1,0:T(8,128)(2,1)}, bf16[256,1024]{1,0:T(8,128)(2,1)S(1)}, u32[]{:S(2)}) copy-start(bf16[256,1024]{1,0:T(8,128)(2,1)S(1)} %get-tuple-element.11) | copy-start | bytes 1572868
  124.0 27.6 %all-to-all-start.1 = ((bf16[16,2,128,192]{2,3,1,0:T(8,128)(2,1)}), bf16[16,2,128,192]{2,3,1,0:T(8,128)(2,1)}, u32[]{:S(2)}, u32[]{:S(2)}) async-start(bf16[16,2,128,192]{2,3,1,0:T(8,128)(2,1)} %copy.62), calls=%async_computation.1 | async-start | bytes 3145728 | tf_op jit(solution)/shard_map/all_to_all | solution.py:256
  190.9 1.4 copy-start
  196.2 24.4 %all-to-all-start.3 = ((bf16[16,2,128,192]{2,3,1,0:T(8,128)(2,1)}), bf16[16,2,128,192]{2,3,1,0:T(8,128)(2,1)S(1)}, u32[]{:S(2)}, u32[]{:S(2)}) async-start(bf16[16,2,128,192]{2,3,1,0:T(8,128)(2,1)} %copy.67), calls=%async_computation.3 | async-start | bytes 3145728 | tf_op jit(solution)/shard_map/all_to_all | solution.py:259
  222.2 1.0 copy-start.7
  231.3 4.5 %copy-start.1 = (f32[2,2,2,2,64,2,2,2,384]{8,4,7,6,5,3,2,1,0:T(8,128)}, f32[2,2,2,2,64,2,2,2,384]{8,4,7,6,5,3,2,1,0:T(8,128)S(1)}, u32[]{:S(2)}) copy-start(f32[2,2,2,2,64,2,2,2,384]{8,4,7,6,5,3,2,1,0:T(8,128)S(1)} %fusion.49) | copy-start | bytes 37748740
  236.3 9.5 %collective-permute-start = (bf16[2,2,2,2,64,2,2,384]{7,4,6,5,3,2,1,0:T(8,128)(2,1)S(1)}, bf16[2,2,2,2,64,2,2,384]{7,4,6,5,3,2,1,0:T(8,128)(2,1)}, u32[]{:S(2)}, u32[]{:S(2)}) collective-permute-start(bf16[2,2,2,2,64,2,2,384]{7,4,6,5,3,2,1,0:T(8,128)(2,1)S(1)} %fusion), channel_id=1, source_target_pairs={{0,1},{1,0},{2,3},{3,2},{4,5},{5,4},{6,7},{7,6},{8,9},{9,8},{10,11... | collective-permute-start | bytes 9437192 | tf_op jit(solution)/shard_map/ppermute | solution.py:97
  250.5 2.6 copy-start.2
  253.2 1.5 copy-start.8
  254.7 35.9 %collective-permute-start.1 = (bf16[2,2,2,64,2,2,384]{6,3,5,4,2,1,0:T(8,128)(2,1)}, bf16[2,2,2,64,2,2,384]{6,3,5,4,2,1,0:T(8,128)(2,1)}, u32[]{:S(2)}, u32[]{:S(2)}) collective-permute-start(bf16[2,2,2,64,2,2,384]{6,3,5,4,2,1,0:T(8,128)(2,1)} %fusion.1), channel_id=1, source_target_pairs={{0,32},{8,40},{16,48},{24,56},{32,0},{40,8},{48,16},{56,24},{64,96... | collective-permute-start | bytes 4718600 | tf_op jit(solution)/shard_map/ppermute | solution.py:97
  258.6 37.7 %collective-permute-start.7 = (bf16[864,2,2,128]{3,0,2,1:T(8,128)(2,1)}, bf16[864,2,2,128]{3,0,2,1:T(8,128)(2,1)}, u32[]{:S(2)}, u32[]{:S(2)}) collective-permute-start(bf16[864,2,2,128]{3,0,2,1:T(8,128)(2,1)} %fusion.15), channel_id=1, source_target_pairs={{0,1},{1,0},{2,3},{3,2},{4,5},{5,4},{6,7},{7,6},{8,9},{9,8},{10,11... | collective-permute-start | bytes 2654216 | tf_op jit(solution)/shard_map/ppermute | solution.py:97
  293.4 1.6 copy-start.3
  296.0 18.2 %collective-permute-start.2 = (bf16[2,2,64,2,2,384]{5,2,4,3,1,0:T(8,128)(2,1)}, bf16[2,2,64,2,2,384]{5,2,4,3,1,0:T(8,128)(2,1)}, u32[]{:S(2)}, u32[]{:S(2)}) collective-permute-start(bf16[2,2,64,2,2,384]{5,2,4,3,1,0:T(8,128)(2,1)} %fusion.16), channel_id=1, source_target_pairs={{0,8},{8,0},{16,24},{24,16},{32,40},{40,32},{48,56},{56,48},{64,72... | collective-permute-start | bytes 2359304 | tf_op jit(solution)/shard_map/ppermute | solution.py:97
  297.6 1.2 copy-start.4
  299.7 17.2 %collective-permute-start.8 = (bf16[864,2,128]{2,0,1:T(8,128)(2,1)}, bf16[864,2,128]{2,0,1:T(8,128)(2,1)}, u32[]{:S(2)}, u32[]{:S(2)}) collective-permute-start(bf16[864,2,128]{2,0,1:T(8,128)(2,1)} %fusion.21), channel_id=1, source_target_pairs={{0,2},{1,3},{2,0},{3,1},{4,6},{5,7},{6,4},{7,5},{8,10},{9,11},{10,... | collective-permute-start | bytes 1327112 | tf_op jit(solution)/shard_map/ppermute | solution.py:97
  299.7 17.2 %copy-start.5 = (f32[864,2,2,128]{3,0,2,1:T(8,128)S(1)}, f32[864,2,2,128]{3,0,2,1:T(8,128)}, u32[]{:S(2)}) copy-start(f32[864,2,2,128]{3,0,2,1:T(8,128)} %copy-done.4) | copy-start | bytes 5308420
  316.9 8.9 %collective-permute-start.3 = (bf16[2,2,64,2,384]{4,2,3,1,0:T(8,128)(2,1)}, bf16[2,2,64,2,384]{4,2,3,1,0:T(8,128)(2,1)}, u32[]{:S(2)}, u32[]{:S(2)}) collective-permute-start(bf16[2,2,64,2,384]{4,2,3,1,0:T(8,128)(2,1)} %fusion.22), channel_id=1, source_target_pairs={{0,2},{1,3},{2,0},{3,1},{4,6},{5,7},{6,4},{7,5},{8,10},{9,11},{10,... | collective-permute-start | bytes 1179656 | tf_op jit(solution)/shard_map/ppermute | solution.py:97
  318.0 12.1 %collective-permute-start.9 = (bf16[864,128]{1,0:T(8,128)(2,1)S(1)}, bf16[864,128]{1,0:T(8,128)(2,1)S(1)}, u32[]{:S(2)}, u32[]{:S(2)}) collective-permute-start(bf16[864,128]{1,0:T(8,128)(2,1)S(1)} %fusion.27), channel_id=1, source_target_pairs={{0,4},{1,5},{2,6},{3,7},{4,0},{5,1},{6,2},{7,3},{8,12},{9,13},{10,... | collective-permute-start | bytes 663560 | tf_op jit(solution)/shard_map/ppermute | solution.py:97
  326.9 7.6 %collective-permute-start.4 = (bf16[2,64,2,384]{3,1,2,0:T(8,128)(2,1)S(1)}, bf16[2,64,2,384]{3,1,2,0:T(8,128)(2,1)S(1)}, u32[]{:S(2)}, u32[]{:S(2)}) collective-permute-start(bf16[2,64,2,384]{3,1,2,0:T(8,128)(2,1)S(1)} %fusion.28), channel_id=1, source_target_pairs={{0,64},{8,72},{16,80},{24,88},{32,96},{40,104},{48,112},{56,120},{... | collective-permute-start | bytes 589832 | tf_op jit(solution)/shard_map/ppermute | solution.py:97
  331.0 12.2 %all-to-all-start.4 = ((f32[16,54,128]{2,1,0:T(8,128)}), f32[16,54,128]{2,1,0:T(8,128)S(1)}, u32[]{:S(2)}, u32[]{:S(2)}) async-start(f32[16,54,128]{2,1,0:T(8,128)} %reshape.253), calls=%async_computation.4 | async-start | bytes 917504 | tf_op jit(solution)/shard_map/all_to_all | solution.py:302
  334.6 13.0 %collective-permute-start.5 = (bf16[64,2,384]{2,0,1:T(8,128)(2,1)S(1)}, bf16[64,2,384]{2,0,1:T(8,128)(2,1)S(1)}, u32[]{:S(2)}, u32[]{:S(2)}) collective-permute-start(bf16[64,2,384]{2,0,1:T(8,128)(2,1)S(1)} %fusion.29), channel_id=1, source_target_pairs={{0,16},{8,24},{16,0},{24,8},{32,48},{40,56},{48,32},{56,40},{64,80... | collective-permute-start | bytes 294920 | tf_op jit(solution)/shard_map/ppermute | solution.py:97
  344.0 12.1 %all-to-all-start.5 = ((f32[16,54,128]{2,1,0:T(8,128)}), f32[16,54,128]{2,1,0:T(8,128)S(1)}, u32[]{:S(2)}, u32[]{:S(2)}) async-start(f32[16,54,128]{2,1,0:T(8,128)} %broadcast_in_dim.20), calls=%async_computation.5 | async-start | bytes 917504 | tf_op jit(solution)/shard_map/all_to_all | solution.py:306
  347.7 9.5 %collective-permute-start.6 = (bf16[64,384]{1,0:T(8,128)(2,1)S(1)}, bf16[64,384]{1,0:T(8,128)(2,1)S(1)}, u32[]{:S(2)}, u32[]{:S(2)}) collective-permute-start(bf16[64,384]{1,0:T(8,128)(2,1)S(1)} %fusion.31), channel_id=1, source_target_pairs={{0,4},{1,5},{2,6},{3,7},{4,0},{5,1},{6,2},{7,3},{8,12},{9,13},{10,... | collective-permute-start | bytes 147464 | tf_op jit(solution)/shard_map/ppermute | solution.py:97
Sparse Core Ops, SparseCore 0:
  9.6 29.1 all-gather.2
  41.0 66.2 all-gather.4

commit v8 on v5

--- a/solution.py
+++ b/solution.py
@@ -110,20 +110,24 @@
     upstream = g_ref[:, 0, :, :].reshape(block, HD)
     key_rows = k_s[...]
     value_rows = v_s[...]
-    scores = contract(queries, key_rows, 1, 1) * factor
+    scores = contract(queries * jnp.asarray(factor, queries.dtype), key_rows, 1, 1)
     raised = jnp.exp(scores - jnp.max(scores, axis=1, keepdims=True))
     attention = raised / jnp.sum(raised, axis=1, keepdims=True)
     d_attention = contract(upstream, value_rows, 1, 1)
     inner_sum = jnp.sum(attention * d_attention, axis=1, keepdims=True)
-    d_scores = (attention * (d_attention - inner_sum) * factor).astype(jnp.bfloat16)
-    grad_query = contract(d_scores, key_rows, 1, 0).astype(jnp.bfloat16)
-    out_ref[pl.ds(first, per_block), 0, :, 0:HD] = grad_query.reshape(per_block, slots, HD)
+    d_scores = (attention * (d_attention - inner_sum)).astype(jnp.bfloat16)
+    grad_query = contract(d_scores, key_rows, 1, 0) * factor
+    out_ref[pl.ds(first, per_block), 0, :, 0:HD] = grad_query.astype(jnp.bfloat16).reshape(
+        per_block, slots, HD
+    )
     dk_acc[...] += contract(d_scores, queries, 0, 0)
     dv_acc[...] += contract(attention.astype(jnp.bfloat16), upstream, 0, 0)
 
     @pl.when(step == pl.num_programs(1) - 1)
     def _():
-        out_ref[:, 0, :, HD : 2 * HD] = dk_acc[...].astype(jnp.bfloat16).reshape(owners, slots, HD)
+        out_ref[:, 0, :, HD : 2 * HD] = (dk_acc[...] * factor).astype(jnp.bfloat16).reshape(
+            owners, slots, HD
+        )
         out_ref[:, 0, :, 2 * HD : 3 * HD] = dv_acc[...].astype(jnp.bfloat16).reshape(owners, slots, HD)
 
 
@@ -216,7 +220,14 @@
     ).astype(jnp.bfloat16)
     chosen = select(to_slot, arrived[:, :, :PATCH]).astype(jnp.bfloat16).reshape(row_total, PATCH)
     full_embed = (
-        lax.all_gather(embed_weight, "tm", axis=1, tiled=True)
+        lax.all_to_all(
+            jnp.broadcast_to(embed_weight[None], (tm_count,) + embed_weight.shape),
+            "tm",
+            split_axis=0,
+            concat_axis=0,
+            tiled=True,
+        )
+        .transpose(1, 0, 2)
         .reshape(4, 6, 6, 6, D)
         .transpose(0, 3, 1, 2, 4)
         .reshape(PATCH, D)

time: 335 us -> 333 us (level)
  waiting for transfers between devices: 95.4 us -> 76 us
  blocking collectives: 85.3 us -> 103 us
    all_gather x1, waiting for transfers between devices: 28.2 us -> 0.02 us  [body(): full_qkv = lax.all_gather(wide_rows, 'space', axis=0, tiled=True)]
    all_to_all x0 -> x1, blocking collectives: none -> 20 us  [body(): lax.all_to_all(payload, 'space', split_axis=1, concat_axis=1, tiled=True)]
    all_to_all x1, waiting for transfers between devices: 11.1 us -> 20.4 us  [body(): lax.all_to_all(jnp.broadcast_to(embed_weight[None], (tm_count,) + embed_w...]
  transfers between devices with their start and end apart: 8 -> 7, of which waited for: 5 -> 4; matrix products, arithmetic and copies ran while one was open for 14% -> 15% of each run, Pallas kernels for 3% -> 3%
where the time goes in v8:
time: 333 us; the launch traced here: 332 us
  blocking collectives  103 us (31%)
  waiting for transfers between devices  76 us (23%)
  local copies, waits for them, and re-layouts  46.2 us (14%)
  Pallas kernels  46 us (14%)
  starting transfers between devices  28.7 us (9%)
  between operations  14.5 us (4%)
  matrix products  14.3 us (4%)
    pallas_call x1, Pallas kernels, attention_grads(): pl.pallas_call(attention_kernel, grid=(windows, owners // per_block), in_...  36.6 us
    all_to_all x1, blocking collectives, body(): lax.all_to_all(embed_partial.astype(jnp.bfloat16).reshape(PATCH, tm_count...  30.6 us
    reduce_scatter x1, waiting for transfers between devices, body(): lax.psum_scatter(contract(hidden, d_packed, 0, 0).astype(jnp.bfloat16), '...  29.7 us
    all_to_all x1, blocking collectives, body(): lax.all_to_all(grads, 'space', split_axis=0, concat_axis=0, tiled=True)  22.7 us
    all_to_all x1, waiting for transfers between devices, body(): lax.all_to_all(jnp.broadcast_to(embed_weight[None], (tm_count,) + embed_w...  20.4 us
    all_to_all x1, blocking collectives, body(): lax.all_to_all(payload, 'space', split_axis=1, concat_axis=1, tiled=True)  20 us
    all_to_all x1, waiting for transfers between devices, body(): lax.all_to_all(lanes_out, 'space', split_axis=0, concat_axis=0, tiled=True)  19.2 us
    all_gather x1, blocking collectives, body(): wide_rows = lax.all_gather(qkv_weight, 'tm', axis=1, tiled=True)  16.2 us
  transfers between devices with their start and end apart: 7, of which 4 were waited for; matrix products, arithmetic and copies ran while one was open for 15% of the time, Pallas kernels for 3%

profile of v8, /device:TPU:1, one launch (start us, length us, event | category | flops | bytes accessed | tf_op | source)
XLA Modules:
  0.0 332.1 jit_solution(6281175504876196713)
XLA Ops:
  7.2 16.2 %all_gather.6 = bf16[64,3072]{1,0:T(8,128)(2,1)} all-gather(bf16[64,384]{1,0:T(8,128)(2,1)} %param.10), channel_id=1, replica_groups=mesh['space'=16,'tm'=8] {'tm'}, dimensions={1}, use_global_device_ids=true | all-gather | bytes 442368 | tf_op jit(solution)/shard_map/all_gather | solution.py:241
  23.4 0.7 fusion.39
  24.3 0.7 fusion.43
  25.7 1.2 reshape.232.rows_ref
  27.4 0.6 reshape.233.keep_ref
  28.5 9.4 %shard_map.77 = bf16[2,256,864]{2,1,0:T(8,128)(2,1)S(1)} custom-call(bf16[2,4,576,96]{3,2,1,0:T(8,128)(2,1)S(1)} %reshape.232.rows_ref, bf16[2,96,1536]{2,1,0:T(8,128)(2,1)S(1)} %fusion.10.pick_ref, bf16[2,96,1536]{2,1,0:T(8,128)(2,1)S(1)} %reshape.233.keep_ref, bf16[36,576]{1,0:T(8,128)(2,1)S(1)} %reshape.249.fold_ref), custom_call_target="tpu_custom_call" | custom-call | flops 2717908992 | bytes 1769472 | tf_op jit(solution)/shard_map/pallas_call | solution.py:67
  38.2 0.7 copy.48
  38.9 20.0 %all_to_all.45 = bf16[2,16,12,896]{3,0,2,1:T(2,128)(2,1)S(1)} all-to-all(bf16[2,16,12,896]{3,0,2,1:T(2,128)(2,1)S(1)} %bitcast.97), channel_id=1, replica_groups=mesh['space'=16,'tm'=8] {'space'}, dimensions={1} | all-to-all | bytes 1376256 | tf_op jit(solution)/shard_map/all_to_all | solution.py:214
  59.0 1.4 broadcast_in_dim.22
  60.4 5.3 %all-to-all-start.1 = ((bf16[8,864,128]{2,1,0:T(8,128)(2,1)}), bf16[8,864,128]{2,1,0:T(8,128)(2,1)S(1)}, u32[]{:S(2)}, u32[]{:S(2)}) async-start(bf16[8,864,128]{2,1,0:T(8,128)(2,1)} %broadcast_in_dim.22), calls=%async_computation.1 | async-start | bytes 3538944 | tf_op jit(solution)/shard_map/all_to_all | solution.py:223
  66.0 0.9 copy.59
  67.2 0.6 convolution_convert_fusion.3
  68.0 20.4 %all-to-all-done.1 = bf16[8,864,128]{2,1,0:T(8,128)(2,1)S(1)} async-done(((bf16[8,864,128]{2,1,0:T(8,128)(2,1)}), bf16[8,864,128]{2,1,0:T(8,128)(2,1)S(1)}, u32[]{:S(2)}, u32[]{:S(2)}) %all-to-all-start.1) | async-done | bytes 1769504 | tf_op jit(solution)/shard_map/all_to_all | solution.py:223
  88.4 4.4 %all-to-all-start.3 = ((bf16[16,2,128,64]{2,3,1,0:T(8,128)(2,1)}), bf16[16,2,128,64]{2,3,1,0:T(8,128)(2,1)}, u32[]{:S(2)}, u32[]{:S(2)}) async-start(bf16[16,2,128,64]{2,3,1,0:T(8,128)(2,1)} %copy.59), calls=%async_computation.3 | async-start | bytes 1048576 | tf_op jit(solution)/shard_map/all_to_all | solution.py:249
  92.9 1.9 copy.52
  94.8 3.6 %reshape.237 = bf16[4,6,6,6,1024]{4,3,2,1,0:T(8,128)(2,1)S(1)} reshape(bf16[864,8,128]{2,1,0:T(8,128)(2,1)} %copy.52) | data formatting | bytes 3538944 | tf_op jit(solution)/shard_map/reshape | solution.py:231
  98.4 2.4 copy.53
  100.8 2.7 reshape.238
  103.5 0.8 convert_reduce_fusion.1
  104.6 8.6 %copy.54 = bf16[1024,3072]{0,1:T(8,128)(2,1)} copy(bf16[1024,3072]{1,0:T(8,128)(2,1)} %all-gather.2.cloned.1.call-done) | data formatting | bytes 12582912 | tf_op jit(solution)/shard_map/all_gather | solution.py:242
  113.3 3.5 %copy.55 = bf16[1024,16,3,64]{0,3,2,1:T(8,128)(2,1)S(1)} copy(bf16[1024,16,3,64]{0,3,1,2:T(8,128)(2,1)} %bitcast.86) | data formatting | bytes 12582912 | tf_op jit(solution)/shard_map/transpose | solution.py:244
  116.8 1.9 convolution_convert_fusion.1
  118.7 0.7 copy.56
  119.4 0.4 reshape.241
  119.8 1.5 copy.57
  121.4 6.4 %all-to-all-start.2 = ((bf16[16,2,128,192]{2,3,1,0:T(8,128)(2,1)}), bf16[16,2,128,192]{2,3,1,0:T(8,128)(2,1)}, u32[]{:S(2)}, u32[]{:S(2)}) async-start(bf16[16,2,128,192]{2,3,1,0:T(8,128)(2,1)} %copy.57), calls=%async_computation.2 | async-start | bytes 3145728 | tf_op jit(solution)/shard_map/all_to_all | solution.py:248
  127.8 1.5 copy.61.g_ref
  129.3 19.2 %all-to-all-done.2 = bf16[16,2,128,192]{2,3,1,0:T(8,128)(2,1)} async-done(((bf16[16,2,128,192]{2,3,1,0:T(8,128)(2,1)}), bf16[16,2,128,192]{2,3,1,0:T(8,128)(2,1)}, u32[]{:S(2)}, u32[]{:S(2)}) %all-to-all-start.2) | async-done | bytes 1572896 | tf_op jit(solution)/shard_map/all_to_all | solution.py:248
  148.5 2.7 copy.60.lanes_ref
  151.3 36.6 %shard_map.78 = bf16[16,2,128,192]{3,2,1,0:T(8,128)(2,1)S(1)} custom-call(bf16[16,2,128,192]{3,2,1,0:T(8,128)(2,1)S(1)} %copy.60.lanes_ref, bf16[16,2,128,64]{3,2,1,0:T(8,128)(2,1)S(1)} %copy.61.g_ref), custom_call_target="tpu_custom_call" | custom-call | flops 5368709120 | bytes 3670016 | tf_op jit(solution)/shard_map/pallas_call | solution.py:141
  187.9 1.3 copy-done
  189.2 3.1 copy.62
  192.3 22.7 %all_to_all.46 = bf16[16,2,128,192]{2,3,1,0:T(8,128)(2,1)S(1)} all-to-all(bf16[16,2,128,192]{2,3,1,0:T(8,128)(2,1)S(1)} %copy.62), channel_id=1, replica_groups=mesh['space'=16,'tm'=8] {'space'}, dimensions={0} | all-to-all | bytes 3145728 | tf_op jit(solution)/shard_map/all_to_all | solution.py:251
  215.1 1.6 copy.63
  216.7 4.7 %convolution_convert_fusion = bf16[1024,3072]{1,0:T(8,128)(2,1)} fusion(bf16[384,8,2,128]{3,2,1,0:T(2,128)(2,1)S(1)} %bitcast.93, bf16[256,1024]{1,0:T(8,128)(2,1)S(1)} %copy-done.2, f32[256]{0:T(256)S(1)} %add_rsqrt_fusion, f32[256]{0:T(256)S(1)} %broadcast_multiply_fusion.2), kind=kOutput, calls=%fused_computation | convolution fusion | flops 1614807040 | bytes 8390656 | tf_op jit(solution)/shard_map/dot_general | solution.py:26
  221.4 4.9 %fusion.46 = (f32[256]{0:T(256)S(1)}, f32[256]{0:T(256)S(1)}, f32[256,1024]{1,0:T(8,128)S(1)}) fusion(f32[256]{0:T(256)S(1)} %add_rsqrt_fusion, f32[256]{0:T(256)S(1)} %broadcast_multiply_fusion.2, bf16[256,1024]{1,0:T(8,128)(2,1)S(1)} %copy-done.2, bf16[1024,3072]{1,0:T(8,128)(2,1)} %all-gather.2.cloned.1.call-done, bf16[384,8,2,128]{3,2,1,0:T(2,128)(2,1)S(1)} %bitcast.94), kind=kOutput, calls=%fused_computation.97 | convolution fusion | flops 1612185088 | bytes 9441280 | tf_op jit(solution)/shard_map/dot_general | solution.py:26
  226.3 0.9 convert_bitcast_fusion
  227.2 0.3 copy.104
  227.5 30.6 %all_to_all.47 = bf16[8,864,128]{2,1,0:T(8,128)(2,1)S(1)} all-to-all(bf16[8,864,128]{2,1,0:T(8,128)(2,1)S(1)} %bitcast.89), channel_id=1, replica_groups=mesh['space'=16,'tm'=8] {'tm'}, dimensions={0} | all-to-all | bytes 3538944 | tf_op jit(solution)/shard_map/all_to_all | solution.py:279
  258.4 13.6 %all_to_all.48 = f32[16,54,128]{2,1,0:T(8,128)S(1)} all-to-all(f32[16,54,128]{2,1,0:T(8,128)S(1)} %reshape.247), channel_id=1, replica_groups=mesh['space'=16,'tm'=8] {'space'}, dimensions={0} | all-to-all | bytes 884736 | tf_op jit(solution)/shard_map/all_to_all | solution.py:289
  272.0 0.8 broadcast_in_dim.23
  272.8 5.9 %all-to-all-start.8 = ((f32[16,54,128]{2,1,0:T(8,128)}), f32[16,54,128]{2,1,0:T(8,128)S(1)}, u32[]{:S(2)}, u32[]{:S(2)}) async-start(f32[16,54,128]{2,1,0:T(8,128)} %broadcast_in_dim.23), calls=%async_computation.9 | async-start | bytes 917504 | tf_op jit(solution)/shard_map/all_to_all | solution.py:293
  278.7 29.7 %reduce-scatter.2.cloned.1.call-done = bf16[64,3072]{1,0:T(8,128)(2,1)} async-done(((bf16[1024,3072]{1,0:T(8,128)(2,1)}), bf16[64,3072]{1,0:T(8,128)(2,1)}) %reduce-scatter.2.cloned.1.call-update) | async-done | bytes 393232 | tf_op jit(solution)/shard_map/reduce_scatter | solution.py:257
  308.4 1.8 copy.105
  310.1 6.7 %all-to-all-start.5 = ((bf16[8,64,384]{2,1,0:T(8,128)(2,1)}), bf16[8,64,384]{2,1,0:T(8,128)(2,1)S(1)}, u32[]{:S(2)}, u32[]{:S(2)}) async-start(bf16[8,64,384]{2,1,0:T(8,128)(2,1)} %bitcast.81), calls=%async_computation.6 | async-start | bytes 786432 | tf_op jit(solution)/shard_map/all_to_all | solution.py:265
  317.0 0.8 reshape.248
  317.9 6.7 %all-to-all-done.5 = bf16[8,64,384]{2,1,0:T(8,128)(2,1)S(1)} async-done(((bf16[8,64,384]{2,1,0:T(8,128)(2,1)}), bf16[8,64,384]{2,1,0:T(8,128)(2,1)S(1)}, u32[]{:S(2)}, u32[]{:S(2)}) %all-to-all-start.5) | async-done | bytes 393248 | tf_op jit(solution)/shard_map/all_to_all | solution.py:265
  324.5 0.7 convert_reduce_fusion.2
  (64 shorter events, 3.7 us)
Async XLA Ops:
  7.2 18.2 %copy-start.5 = (bf16[2,4,6,9216]{3,1,2,0:T(4,128)(2,1)S(1)}, bf16[2,4,6,9216]{3,1,2,0:T(4,128)(2,1)}, u32[]{:S(2)}) copy-start(bf16[2,4,6,9216]{3,1,2,0:T(4,128)(2,1)} %param.6) | copy-start | bytes 2654212
  7.2 97.4 %all-gather.2.cloned.1.call-start = ((), (), s32[]{:S(2)}) async-start(), calls=%async_computation.10 | async-start | bytes 6684672 | tf_op jit(solution)/shard_map/all_gather | solution.py:242
  25.4 1.5 copy-start.8
  38.1 20.9 %copy-start.7 = (bf16[864,128]{1,0:T(8,128)(2,1)S(1)}, bf16[864,128]{1,0:T(8,128)(2,1)}, u32[]{:S(2)}) copy-start(bf16[864,128]{1,0:T(8,128)(2,1)} %param.9) | copy-start | bytes 663556
  60.4 5.3 %copy-start.6 = (bf16[2,1,128,1024]{3,2,1,0:T(8,128)(2,1)S(1)}, bf16[2,1,128,1024]{3,2,1,0:T(8,128)(2,1)}, u32[]{:S(2)}) copy-start(bf16[2,1,128,1024]{3,2,1,0:T(8,128)(2,1)} %param.11) | copy-start | bytes 1572868
  60.4 28.0 %all-to-all-start.1 = ((bf16[8,864,128]{2,1,0:T(8,128)(2,1)}), bf16[8,864,128]{2,1,0:T(8,128)(2,1)S(1)}, u32[]{:S(2)}, u32[]{:S(2)}) async-start(bf16[8,864,128]{2,1,0:T(8,128)(2,1)} %broadcast_in_dim.22), calls=%async_computation.1 | async-start | bytes 3538944 | tf_op jit(solution)/shard_map/all_to_all | solution.py:223
  68.0 35.5 %copy-start.3 = (bf16[2,128,864]{2,1,0:T(8,128)(2,1)}, bf16[2,128,864]{2,1,0:T(8,128)(2,1)S(1)}, u32[]{:S(2)}) copy-start(bf16[2,128,864]{2,1,0:T(8,128)(2,1)S(1)} %copy.51) | copy-start | bytes 1327108
  88.4 32.9 %all-to-all-start.3 = ((bf16[16,2,128,64]{2,3,1,0:T(8,128)(2,1)}), bf16[16,2,128,64]{2,3,1,0:T(8,128)(2,1)}, u32[]{:S(2)}, u32[]{:S(2)}) async-start(bf16[16,2,128,64]{2,3,1,0:T(8,128)(2,1)} %copy.59), calls=%async_computation.3 | async-start | bytes 1048576 | tf_op jit(solution)/shard_map/all_to_all | solution.py:249
  104.3 12.5 %copy-start.1 = (bf16[256,1024]{1,0:T(8,128)(2,1)}, bf16[256,1024]{1,0:T(8,128)(2,1)S(1)}, u32[]{:S(2)}) copy-start(bf16[256,1024]{1,0:T(8,128)(2,1)S(1)} %get-tuple-element.9) | copy-start | bytes 1572868
  121.4 27.2 %all-to-all-start.2 = ((bf16[16,2,128,192]{2,3,1,0:T(8,128)(2,1)}), bf16[16,2,128,192]{2,3,1,0:T(8,128)(2,1)}, u32[]{:S(2)}, u32[]{:S(2)}) async-start(bf16[16,2,128,192]{2,3,1,0:T(8,128)(2,1)} %copy.57), calls=%async_computation.2 | async-start | bytes 3145728 | tf_op jit(solution)/shard_map/all_to_all | solution.py:248
  127.8 180.6 %reduce-scatter.2.cloned.1.call-start = ((), (), s32[]{:S(2)}) async-start(), calls=%async_computation.11 | async-start | bytes 6684672 | tf_op jit(solution)/shard_map/reduce_scatter | solution.py:257
  187.9 1.3 copy-start
  215.1 1.6 copy-start.2
  221.4 4.9 %copy-start.4 = (bf16[2,128,864]{2,1,0:T(8,128)(2,1)S(1)}, bf16[2,128,864]{2,1,0:T(8,128)(2,1)}, u32[]{:S(2)}) copy-start(bf16[2,128,864]{2,1,0:T(8,128)(2,1)} %copy-done.3) | copy-start | bytes 1327108
  272.8 37.3 %all-to-all-start.8 = ((f32[16,54,128]{2,1,0:T(8,128)}), f32[16,54,128]{2,1,0:T(8,128)S(1)}, u32[]{:S(2)}, u32[]{:S(2)}) async-start(f32[16,54,128]{2,1,0:T(8,128)} %broadcast_in_dim.23), calls=%async_computation.9 | async-start | bytes 917504 | tf_op jit(solution)/shard_map/all_to_all | solution.py:293
  310.1 14.4 %all-to-all-start.5 = ((bf16[8,64,384]{2,1,0:T(8,128)(2,1)}), bf16[8,64,384]{2,1,0:T(8,128)(2,1)S(1)}, u32[]{:S(2)}, u32[]{:S(2)}) async-start(bf16[8,64,384]{2,1,0:T(8,128)(2,1)} %bitcast.81), calls=%async_computation.6 | async-start | bytes 786432 | tf_op jit(solution)/shard_map/all_to_all | solution.py:265
Sparse Core Ops, SparseCore 0:
  23.5 65.3 all-gather.1
  221.5 86.7 reduce-scatter.1

commit v9 on v8

--- a/solution.py
+++ b/solution.py
@@ -241,9 +241,12 @@
     wide_rows = lax.all_gather(qkv_weight, "tm", axis=1, tiled=True)
     full_qkv = lax.all_gather(wide_rows, "space", axis=0, tiled=True)
     heads = D // HD
-    head_qkv = full_qkv.reshape(D, 3, heads, HD).transpose(0, 2, 1, 3).reshape(D, 3 * D)
-    packed = jnp.dot(hidden, head_qkv, preferred_element_type=jnp.float32).astype(jnp.bfloat16)
-    lanes_out = packed.reshape(windows, OWN, heads, 3 * HD).transpose(2, 0, 1, 3)
+    packed = jnp.dot(hidden, full_qkv, preferred_element_type=jnp.float32).astype(jnp.bfloat16)
+    lanes_out = (
+        packed.reshape(windows, OWN, 3, heads, HD)
+        .transpose(3, 0, 1, 2, 4)
+        .reshape(heads, windows, OWN, 3 * HD)
+    )
     upstream_out = cotangent.reshape(windows, OWN, heads, HD).transpose(2, 0, 1, 3)
     lanes = lax.all_to_all(lanes_out, "space", split_axis=0, concat_axis=0, tiled=True)
     upstream = lax.all_to_all(upstream_out, "space", split_axis=0, concat_axis=0, tiled=True)

time: 333 us -> 329 us (0.988)
  local copies, waits for them, and re-layouts: 46.2 us -> 39.1 us
  matrix products: 14.3 us -> 19 us
    all_gather x1 -> x0, local copies, waits for them, and re-layouts: 8.63 us -> none  [body(): full_qkv = lax.all_gather(wide_rows, 'space', axis=0, tiled=True)]
    dot_general x1, matrix products: 1.92 us -> 5.83 us  [body(): jnp.dot(hidden, full_qkv, preferred_element_type=jnp.float32)]
where the time goes in v9:
time: 329 us; the launch traced here: 328 us
  blocking collectives  103 us (31%)
  waiting for transfers between devices  74.8 us (23%)
  Pallas kernels  46 us (14%)
  local copies, waits for them, and re-layouts  39.1 us (12%)
  starting transfers between devices  28 us (9%)
  matrix products  19 us (6%)
  between operations  14.4 us (4%)
  other arithmetic  3.86 us (1%)
    pallas_call x1, Pallas kernels, attention_grads(): pl.pallas_call(attention_kernel, grid=(windows, owners // per_block), in_...  36.6 us
    all_to_all x1, blocking collectives, body(): lax.all_to_all(embed_partial.astype(jnp.bfloat16).reshape(PATCH, tm_count...  30.3 us
    reduce_scatter x1, waiting for transfers between devices, body(): lax.psum_scatter(contract(hidden, d_packed, 0, 0).astype(jnp.bfloat16), '...  29.2 us
    all_to_all x1, blocking collectives, body(): lax.all_to_all(grads, 'space', split_axis=0, concat_axis=0, tiled=True)  22.7 us
    all_to_all x1, waiting for transfers between devices, body(): lax.all_to_all(lanes_out, 'space', split_axis=0, concat_axis=0, tiled=True)  20.2 us
    all_to_all x1, blocking collectives, body(): lax.all_to_all(payload, 'space', split_axis=1, concat_axis=1, tiled=True)  20 us
    all_to_all x1, waiting for transfers between devices, body(): lax.all_to_all(jnp.broadcast_to(embed_weight[None], (tm_count,) + embed_w...  18.6 us
    all_gather x1, blocking collectives, body(): wide_rows = lax.all_gather(qkv_weight, 'tm', axis=1, tiled=True)  16 us
  transfers between devices with their start and end apart: 7, of which 4 were waited for; matrix products, arithmetic and copies ran while one was open for 15% of the time, Pallas kernels for 3%

profile of v9, /device:TPU:1, one launch (start us, length us, event | category | flops | bytes accessed | tf_op | source)
XLA Modules:
  0.0 328.0 jit_solution(17242835122362738752)
XLA Ops:
  7.2 16.0 %all_gather.6 = bf16[64,3072]{1,0:T(8,128)(2,1)} all-gather(bf16[64,384]{1,0:T(8,128)(2,1)} %param.10), channel_id=1, replica_groups=mesh['space'=16,'tm'=8] {'tm'}, dimensions={1}, use_global_device_ids=true | all-gather | bytes 442368 | tf_op jit(solution)/shard_map/all_gather | solution.py:241
  23.3 0.7 fusion.39
  24.2 0.7 fusion.43
  25.1 0.7 fusion.41
  26.7 0.6 reshape.230.keep_ref
  27.3 1.4 copy.44
  28.8 1.2 reshape.229.rows_ref
  30.1 9.5 %shard_map.77 = bf16[2,256,864]{2,1,0:T(8,128)(2,1)S(1)} custom-call(bf16[2,4,576,96]{3,2,1,0:T(8,128)(2,1)S(1)} %reshape.229.rows_ref, bf16[2,96,1536]{2,1,0:T(8,128)(2,1)S(1)} %fusion.10.pick_ref, bf16[2,96,1536]{2,1,0:T(8,128)(2,1)S(1)} %reshape.230.keep_ref, bf16[36,576]{1,0:T(8,128)(2,1)S(1)} %reshape.245.fold_ref), custom_call_target="tpu_custom_call" | custom-call | flops 2717908992 | bytes 1769472 | tf_op jit(solution)/shard_map/pallas_call | solution.py:67
  40.0 0.7 copy.46
  40.7 20.0 %all_to_all.45 = bf16[2,16,12,896]{3,0,2,1:T(2,128)(2,1)S(1)} all-to-all(bf16[2,16,12,896]{3,0,2,1:T(2,128)(2,1)S(1)} %bitcast.92), channel_id=1, replica_groups=mesh['space'=16,'tm'=8] {'space'}, dimensions={1} | all-to-all | bytes 1376256 | tf_op jit(solution)/shard_map/all_to_all | solution.py:214
  60.7 1.4 broadcast_in_dim.22
  62.1 5.3 %all-to-all-start.1 = ((bf16[8,864,128]{2,1,0:T(8,128)(2,1)}), bf16[8,864,128]{2,1,0:T(8,128)(2,1)S(1)}, u32[]{:S(2)}, u32[]{:S(2)}) async-start(bf16[8,864,128]{2,1,0:T(8,128)(2,1)} %broadcast_in_dim.22), calls=%async_computation.1 | async-start | bytes 3538944 | tf_op jit(solution)/shard_map/all_to_all | solution.py:223
  67.7 0.8 copy.55
  68.9 1.4 convolution_convert_fusion.3
  70.2 1.3 copy.49
  71.5 18.6 %all-to-all-done.1 = bf16[8,864,128]{2,1,0:T(8,128)(2,1)S(1)} async-done(((bf16[8,864,128]{2,1,0:T(8,128)(2,1)}), bf16[8,864,128]{2,1,0:T(8,128)(2,1)S(1)}, u32[]{:S(2)}, u32[]{:S(2)}) %all-to-all-start.1) | async-done | bytes 1769504 | tf_op jit(solution)/shard_map/all_to_all | solution.py:223
  90.2 3.8 %all-to-all-start.3 = ((bf16[16,2,128,64]{2,3,1,0:T(8,128)(2,1)}), bf16[16,2,128,64]{2,3,1,0:T(8,128)(2,1)S(1)}, u32[]{:S(2)}, u32[]{:S(2)}) async-start(bf16[16,2,128,64]{2,3,1,0:T(8,128)(2,1)} %copy.55), calls=%async_computation.3 | async-start | bytes 1048576 | tf_op jit(solution)/shard_map/all_to_all | solution.py:252
  93.9 1.9 copy.50
  95.8 3.6 %reshape.234 = bf16[4,6,6,6,1024]{4,3,2,1,0:T(8,128)(2,1)S(1)} reshape(bf16[864,8,128]{2,1,0:T(8,128)(2,1)} %copy.50) | data formatting | bytes 3538944 | tf_op jit(solution)/shard_map/reshape | solution.py:231
  99.4 2.4 copy.51
  101.9 2.7 reshape.235
  104.5 0.8 convert_reduce_fusion.1
  105.7 5.8 %convolution_convert_fusion.1 = bf16[256,3072]{1,0:T(8,128)(2,1)} fusion(bf16[1024,3072]{1,0:T(8,128)(2,1)} %all-gather.2.cloned.1.call-done, bf16[256,1024]{1,0:T(8,128)(2,1)S(1)} %get-tuple-element.9, f32[256]{0:T(256)S(1)} %add_rsqrt_fusion, f32[256]{0:T(256)S(1)} %broadcast_multiply_fusion.2), kind=kOutput, calls=%fused_computation.1 | convolution fusion | flops 1612447744 | bytes 8390656 | tf_op jit(solution)/shard_map/dot_general | solution.py:244
  111.5 1.7 copy.52
  113.2 1.9 reshape.236
  115.1 3.0 copy.53
  118.1 6.5 %all-to-all-start.2 = ((bf16[16,2,128,192]{2,3,1,0:T(8,128)(2,1)}), bf16[16,2,128,192]{2,3,1,0:T(8,128)(2,1)}, u32[]{:S(2)}, u32[]{:S(2)}) async-start(bf16[16,2,128,192]{2,3,1,0:T(8,128)(2,1)} %bitcast.14), calls=%async_computation.2 | async-start | bytes 3145728 | tf_op jit(solution)/shard_map/all_to_all | solution.py:251
  124.6 0.5 copy.57.g_ref
  125.1 20.2 %all-to-all-done.2 = bf16[16,2,128,192]{2,3,1,0:T(8,128)(2,1)} async-done(((bf16[16,2,128,192]{2,3,1,0:T(8,128)(2,1)}), bf16[16,2,128,192]{2,3,1,0:T(8,128)(2,1)}, u32[]{:S(2)}, u32[]{:S(2)}) %all-to-all-start.2) | async-done | bytes 1572896 | tf_op jit(solution)/shard_map/all_to_all | solution.py:251
  145.3 2.7 copy.56.lanes_ref
  148.1 36.6 %shard_map.78 = bf16[16,2,128,192]{3,2,1,0:T(8,128)(2,1)S(1)} custom-call(bf16[16,2,128,192]{3,2,1,0:T(8,128)(2,1)S(1)} %copy.56.lanes_ref, bf16[16,2,128,64]{3,2,1,0:T(8,128)(2,1)S(1)} %copy.57.g_ref), custom_call_target="tpu_custom_call" | custom-call | flops 5368709120 | bytes 3670016 | tf_op jit(solution)/shard_map/pallas_call | solution.py:141
  184.7 1.3 copy-done
  186.0 3.1 copy.58
  189.1 22.7 %all_to_all.46 = bf16[16,2,128,192]{2,3,1,0:T(8,128)(2,1)S(1)} all-to-all(bf16[16,2,128,192]{2,3,1,0:T(8,128)(2,1)S(1)} %copy.58), channel_id=1, replica_groups=mesh['space'=16,'tm'=8] {'space'}, dimensions={0} | all-to-all | bytes 3145728 | tf_op jit(solution)/shard_map/all_to_all | solution.py:254
  211.8 1.6 copy.59
  213.4 4.7 %convolution_convert_fusion = bf16[1024,3072]{1,0:T(8,128)(2,1)} fusion(bf16[384,8,2,128]{3,2,1,0:T(2,128)(2,1)S(1)} %bitcast.88, bf16[256,1024]{1,0:T(8,128)(2,1)S(1)} %copy-done.2, f32[256]{0:T(256)S(1)} %add_rsqrt_fusion, f32[256]{0:T(256)S(1)} %broadcast_multiply_fusion.2), kind=kOutput, calls=%fused_computation | convolution fusion | flops 1614807040 | bytes 8390656 | tf_op jit(solution)/shard_map/dot_general | solution.py:26
  218.2 4.9 %fusion.46 = (f32[256]{0:T(256)S(1)}, f32[256]{0:T(256)S(1)}, f32[256,1024]{1,0:T(8,128)S(1)}) fusion(f32[256]{0:T(256)S(1)} %add_rsqrt_fusion, f32[256]{0:T(256)S(1)} %broadcast_multiply_fusion.2, bf16[256,1024]{1,0:T(8,128)(2,1)S(1)} %copy-done.2, bf16[1024,3072]{1,0:T(8,128)(2,1)} %all-gather.2.cloned.1.call-done, bf16[384,8,2,128]{3,2,1,0:T(2,128)(2,1)S(1)} %bitcast.89), kind=kOutput, calls=%fused_computation.97 | convolution fusion | flops 1612185088 | bytes 9441280 | tf_op jit(solution)/shard_map/dot_general | solution.py:26
  223.0 0.9 convert_bitcast_fusion
  224.2 30.3 %all_to_all.47 = bf16[8,864,128]{2,1,0:T(8,128)(2,1)S(1)} all-to-all(bf16[8,864,128]{2,1,0:T(8,128)(2,1)S(1)} %bitcast.85), channel_id=1, replica_groups=mesh['space'=16,'tm'=8] {'tm'}, dimensions={0} | all-to-all | bytes 3538944 | tf_op jit(solution)/shard_map/all_to_all | solution.py:282
  254.8 13.8 %all_to_all.48 = f32[16,54,128]{2,1,0:T(8,128)S(1)} all-to-all(f32[16,54,128]{2,1,0:T(8,128)S(1)} %reshape.243), channel_id=1, replica_groups=mesh['space'=16,'tm'=8] {'space'}, dimensions={0} | all-to-all | bytes 884736 | tf_op jit(solution)/shard_map/all_to_all | solution.py:292
  268.6 0.8 broadcast_in_dim.23
  269.4 5.7 %all-to-all-start.8 = ((f32[16,54,128]{2,1,0:T(8,128)}), f32[16,54,128]{2,1,0:T(8,128)S(1)}, u32[]{:S(2)}, u32[]{:S(2)}) async-start(f32[16,54,128]{2,1,0:T(8,128)} %broadcast_in_dim.23), calls=%async_computation.9 | async-start | bytes 917504 | tf_op jit(solution)/shard_map/all_to_all | solution.py:296
  275.1 29.2 %reduce-scatter.2.cloned.1.call-done = bf16[64,3072]{1,0:T(8,128)(2,1)} async-done(((bf16[1024,3072]{1,0:T(8,128)(2,1)}), bf16[64,3072]{1,0:T(8,128)(2,1)}) %reduce-scatter.2.cloned.1.call-update) | async-done | bytes 393232 | tf_op jit(solution)/shard_map/reduce_scatter | solution.py:260
  304.3 1.8 copy.101
  306.1 6.7 %all-to-all-start.5 = ((bf16[8,64,384]{2,1,0:T(8,128)(2,1)}), bf16[8,64,384]{2,1,0:T(8,128)(2,1)S(1)}, u32[]{:S(2)}, u32[]{:S(2)}) async-start(bf16[8,64,384]{2,1,0:T(8,128)(2,1)} %bitcast.78), calls=%async_computation.6 | async-start | bytes 786432 | tf_op jit(solution)/shard_map/all_to_all | solution.py:268
  313.0 0.8 reshape.244
  313.8 6.7 %all-to-all-done.5 = bf16[8,64,384]{2,1,0:T(8,128)(2,1)S(1)} async-done(((bf16[8,64,384]{2,1,0:T(8,128)(2,1)}), bf16[8,64,384]{2,1,0:T(8,128)(2,1)S(1)}, u32[]{:S(2)}, u32[]{:S(2)}) %all-to-all-start.5) | async-done | bytes 393248 | tf_op jit(solution)/shard_map/all_to_all | solution.py:268
  320.5 0.7 convert_reduce_fusion.2
  (58 shorter events, 3.5 us)
Async XLA Ops:
  7.2 98.5 %all-gather.2.cloned.1.call-start = ((), (), s32[]{:S(2)}) async-start(), calls=%async_computation.10 | async-start | bytes 6684672 | tf_op jit(solution)/shard_map/all_gather | solution.py:242
  39.8 20.9 %copy-start.6 = (bf16[864,128]{1,0:T(8,128)(2,1)S(1)}, bf16[864,128]{1,0:T(8,128)(2,1)}, u32[]{:S(2)}) copy-start(bf16[864,128]{1,0:T(8,128)(2,1)} %param.9) | copy-start | bytes 663556
  62.1 5.3 %copy-start.5 = (bf16[2,1,128,1024]{3,2,1,0:T(8,128)(2,1)S(1)}, bf16[2,1,128,1024]{3,2,1,0:T(8,128)(2,1)}, u32[]{:S(2)}) copy-start(bf16[2,1,128,1024]{3,2,1,0:T(8,128)(2,1)} %param.11) | copy-start | bytes 1572868
  62.1 28.0 %all-to-all-start.1 = ((bf16[8,864,128]{2,1,0:T(8,128)(2,1)}), bf16[8,864,128]{2,1,0:T(8,128)(2,1)S(1)}, u32[]{:S(2)}, u32[]{:S(2)}) async-start(bf16[8,864,128]{2,1,0:T(8,128)(2,1)} %broadcast_in_dim.22), calls=%async_computation.1 | async-start | bytes 3538944 | tf_op jit(solution)/shard_map/all_to_all | solution.py:223
  71.5 33.0 %copy-start.3 = (bf16[2,128,864]{2,1,0:T(8,128)(2,1)}, bf16[2,128,864]{2,1,0:T(8,128)(2,1)S(1)}, u32[]{:S(2)}) copy-start(bf16[2,128,864]{2,1,0:T(8,128)(2,1)S(1)} %copy.49) | copy-start | bytes 1327108
  90.2 28.0 %all-to-all-start.3 = ((bf16[16,2,128,64]{2,3,1,0:T(8,128)(2,1)}), bf16[16,2,128,64]{2,3,1,0:T(8,128)(2,1)S(1)}, u32[]{:S(2)}, u32[]{:S(2)}) async-start(bf16[16,2,128,64]{2,3,1,0:T(8,128)(2,1)} %copy.55), calls=%async_computation.3 | async-start | bytes 1048576 | tf_op jit(solution)/shard_map/all_to_all | solution.py:252
  105.3 6.2 %copy-start.1 = (bf16[256,1024]{1,0:T(8,128)(2,1)}, bf16[256,1024]{1,0:T(8,128)(2,1)S(1)}, u32[]{:S(2)}) copy-start(bf16[256,1024]{1,0:T(8,128)(2,1)S(1)} %get-tuple-element.9) | copy-start | bytes 1572868
  118.1 27.2 %all-to-all-start.2 = ((bf16[16,2,128,192]{2,3,1,0:T(8,128)(2,1)}), bf16[16,2,128,192]{2,3,1,0:T(8,128)(2,1)}, u32[]{:S(2)}, u32[]{:S(2)}) async-start(bf16[16,2,128,192]{2,3,1,0:T(8,128)(2,1)} %bitcast.14), calls=%async_computation.2 | async-start | bytes 3145728 | tf_op jit(solution)/shard_map/all_to_all | solution.py:251
  124.6 179.7 %reduce-scatter.2.cloned.1.call-start = ((), (), s32[]{:S(2)}) async-start(), calls=%async_computation.11 | async-start | bytes 6684672 | tf_op jit(solution)/shard_map/reduce_scatter | solution.py:260
  184.7 1.3 copy-start
  211.8 1.6 copy-start.2
  218.1 4.9 %copy-start.4 = (bf16[2,128,864]{2,1,0:T(8,128)(2,1)S(1)}, bf16[2,128,864]{2,1,0:T(8,128)(2,1)}, u32[]{:S(2)}) copy-start(bf16[2,128,864]{2,1,0:T(8,128)(2,1)} %copy-done.3) | copy-start | bytes 1327108
  269.4 36.7 %all-to-all-start.8 = ((f32[16,54,128]{2,1,0:T(8,128)}), f32[16,54,128]{2,1,0:T(8,128)S(1)}, u32[]{:S(2)}, u32[]{:S(2)}) async-start(f32[16,54,128]{2,1,0:T(8,128)} %broadcast_in_dim.23), calls=%async_computation.9 | async-start | bytes 917504 | tf_op jit(solution)/shard_map/all_to_all | solution.py:296
  306.1 14.4 %all-to-all-start.5 = ((bf16[8,64,384]{2,1,0:T(8,128)(2,1)}), bf16[8,64,384]{2,1,0:T(8,128)(2,1)S(1)}, u32[]{:S(2)}, u32[]{:S(2)}) async-start(bf16[8,64,384]{2,1,0:T(8,128)(2,1)} %bitcast.78), calls=%async_computation.6 | async-start | bytes 786432 | tf_op jit(solution)/shard_map/all_to_all | solution.py:268
Sparse Core Ops, SparseCore 0:
  23.4 63.5 all-gather.1
  218.3 86.0 reduce-scatter.1

commit v10 on v8

--- a/solution.py
+++ b/solution.py
@@ -90,10 +90,10 @@
 QUERY_BLOCK = 256
 
 
-def attention_kernel(lanes_ref, g_ref, out_ref, k_s, v_s, dk_acc, dv_acc):
+def attention_kernel(lanes_ref, out_ref, k_s, v_s, dk_acc, dv_acc):
     step = pl.program_id(1)
     owners, _, slots, _ = lanes_ref.shape
-    per_block = g_ref.shape[0]
+    per_block = max(1, QUERY_BLOCK // slots)
     length = owners * slots
     block = per_block * slots
     factor = HD ** (-0.5)
@@ -107,7 +107,7 @@
 
     first = pl.multiple_of(step * per_block, per_block)
     queries = lanes_ref[pl.ds(first, per_block), 0, :, 0:HD].reshape(block, HD)
-    upstream = g_ref[:, 0, :, :].reshape(block, HD)
+    upstream = lanes_ref[pl.ds(first, per_block), 0, :, 3 * HD : 4 * HD].reshape(block, HD)
     key_rows = k_s[...]
     value_rows = v_s[...]
     scores = contract(queries * jnp.asarray(factor, queries.dtype), key_rows, 1, 1)
@@ -131,19 +131,19 @@
         out_ref[:, 0, :, 2 * HD : 3 * HD] = dv_acc[...].astype(jnp.bfloat16).reshape(owners, slots, HD)
 
 
-def attention_grads(lanes, upstream):
+def attention_grads(lanes):
     owners, windows, slots, width = lanes.shape
     length = owners * slots
     per_block = max(1, QUERY_BLOCK // slots)
     lanes_spec = pl.BlockSpec((owners, 1, slots, width), lambda w, i: (0, w, 0, 0))
-    g_spec = pl.BlockSpec((per_block, 1, slots, HD), lambda w, i: (i, w, 0, 0))
+    out_spec = pl.BlockSpec((owners, 1, slots, 3 * HD), lambda w, i: (0, w, 0, 0))
     flops = 10 * windows * length * length * HD
     return pl.pallas_call(
         attention_kernel,
         grid=(windows, owners // per_block),
-        in_specs=[lanes_spec, g_spec],
-        out_specs=lanes_spec,
-        out_shape=jax.ShapeDtypeStruct(lanes.shape, jnp.bfloat16),
+        in_specs=[lanes_spec],
+        out_specs=out_spec,
+        out_shape=jax.ShapeDtypeStruct((owners, windows, slots, 3 * HD), jnp.bfloat16),
         scratch_shapes=[
             pltpu.VMEM((length, HD), jnp.bfloat16),
             pltpu.VMEM((length, HD), jnp.bfloat16),
@@ -159,7 +159,7 @@
             transcendentals=windows * length * length,
             bytes_accessed=7 * windows * length * HD * 2,
         ),
-    )(lanes, upstream)
+    )(lanes)
 
 
 def body(voxels, brain_list, owner_slot, embed_weight, qkv_weight, cotangent):
@@ -219,20 +219,21 @@
         arrival_slot[:, None, :] == jnp.arange(OWN, dtype=jnp.int32)[None, :, None]
     ).astype(jnp.bfloat16)
     chosen = select(to_slot, arrived[:, :, :PATCH]).astype(jnp.bfloat16).reshape(row_total, PATCH)
-    full_embed = (
-        lax.all_to_all(
-            jnp.broadcast_to(embed_weight[None], (tm_count,) + embed_weight.shape),
-            "tm",
-            split_axis=0,
-            concat_axis=0,
-            tiled=True,
-        )
-        .transpose(1, 0, 2)
-        .reshape(4, 6, 6, 6, D)
-        .transpose(0, 3, 1, 2, 4)
-        .reshape(PATCH, D)
-    )
-    tokens = jnp.dot(chosen, full_embed, preferred_element_type=jnp.float32).astype(jnp.bfloat16)
+    local_embed = (
+        embed_weight.reshape(4, 6, 6, 6, -1).transpose(0, 3, 1, 2, 4).reshape(PATCH, -1)
+    )
+    embed_blocks = lax.all_to_all(
+        jnp.broadcast_to(local_embed[None], (tm_count,) + local_embed.shape),
+        "tm",
+        split_axis=0,
+        concat_axis=0,
+        tiled=True,
+    )
+    tokens = (
+        jnp.einsum("nr,trc->ntc", chosen, embed_blocks, preferred_element_type=jnp.float32)
+        .astype(jnp.bfloat16)
+        .reshape(row_total, D)
+    )
     widened = tokens.astype(jnp.float32)
     center = widened - jnp.mean(widened, axis=1, keepdims=True)
     inverse = lax.rsqrt(jnp.mean(center * center, axis=1, keepdims=True) + 1e-05)
@@ -241,13 +242,13 @@
     wide_rows = lax.all_gather(qkv_weight, "tm", axis=1, tiled=True)
     full_qkv = lax.all_gather(wide_rows, "space", axis=0, tiled=True)
     heads = D // HD
-    head_qkv = full_qkv.reshape(D, 3, heads, HD).transpose(0, 2, 1, 3).reshape(D, 3 * D)
-    packed = jnp.dot(hidden, head_qkv, preferred_element_type=jnp.float32).astype(jnp.bfloat16)
-    lanes_out = packed.reshape(windows, OWN, heads, 3 * HD).transpose(2, 0, 1, 3)
-    upstream_out = cotangent.reshape(windows, OWN, heads, HD).transpose(2, 0, 1, 3)
+    packed = jnp.dot(hidden, full_qkv, preferred_element_type=jnp.float32).astype(jnp.bfloat16)
+    lanes_out = jnp.concatenate(
+        [packed.reshape(windows, OWN, 3, heads, HD), cotangent.reshape(windows, OWN, 1, heads, HD)],
+        axis=2,
+    ).transpose(3, 0, 1, 2, 4).reshape(heads, windows, OWN, 4 * HD)
     lanes = lax.all_to_all(lanes_out, "space", split_axis=0, concat_axis=0, tiled=True)
-    upstream = lax.all_to_all(upstream_out, "space", split_axis=0, concat_axis=0, tiled=True)
-    grads = attention_grads(lanes, upstream)
+    grads = attention_grads(lanes)
     returned = lax.all_to_all(grads, "space", split_axis=0, concat_axis=0, tiled=True)
     d_packed = (
         returned.reshape(heads, windows, OWN, 3, HD)

time: 333 us -> 321 us (0.964)
  local copies, waits for them, and re-layouts: 46.2 us -> 29.9 us
  blocking collectives: 103 us -> 90.7 us
  waiting for transfers between devices: 76 us -> 81.5 us
  other arithmetic: 3.17 us -> 8.18 us
  matrix products: 14.3 us -> 18.8 us
    all_to_all x2 -> x1, blocking collectives: 42.8 us -> 30.8 us  [body(): lax.all_to_all(lanes_out, 'space', split_axis=0, concat_axis=0, tiled=True)]
    transpose x5 -> x2, local copies, waits for them, and re-layouts: 10.2 us -> 0.6 us  [the longest x1 0.54 us: body(): lanes_out = jnp.concatenate([packed.reshape(windows, OWN, 3, heads, HD),...]
    all_to_all x3, waiting for transfers between devices: 39.6 us -> 48.8 us  [the longest x1 20.4 us: body(): lax.all_to_all(grads, 'space', split_axis=0, concat_axis=0, tiled=True)]
    all_gather x1 -> x0, local copies, waits for them, and re-layouts: 8.63 us -> none  [body(): full_qkv = lax.all_gather(wide_rows, 'space', axis=0, tiled=True)]
    unnamed x24 -> x22, local copies, waits for them, and re-layouts: 2.2 us -> 6.7 us
    transpose x0 -> x1, other arithmetic: none -> 4.32 us  [body(): lanes_out = jnp.concatenate([packed.reshape(windows, OWN, 3, heads, HD),...]
    all_to_all x2 -> x0, local copies, waits for them, and re-layouts: 4.26 us -> none  [the longest x1 2.74 us: body(): lax.all_to_all(lanes_out, 'space', split_axis=0, concat_axis=0, tiled=True)]
    dot_general x2, matrix products: 2.71 us -> 6.67 us  [the longest x1 5.79 us: body(): jnp.dot(hidden, full_qkv, preferred_element_type=jnp.float32)]
  transfers between devices with their start and end apart: 7 -> 7, of which waited for: 4 -> 5; matrix products, arithmetic and copies ran while one was open for 15% -> 9% of each run, Pallas kernels for 3% -> 3%
where the time goes in v10:
time: 321 us; the launch traced here: 320 us
  blocking collectives  90.7 us (28%)
  waiting for transfers between devices  81.5 us (25%)
  Pallas kernels  45.9 us (14%)
  starting transfers between devices  30.4 us (9%)
  local copies, waits for them, and re-layouts  29.9 us (9%)
  matrix products  18.8 us (6%)
  between operations  14.4 us (4%)
  other arithmetic  8.18 us (3%)
    pallas_call x1, Pallas kernels, attention_grads(): pl.pallas_call(attention_kernel, grid=(windows, owners // per_block), in_...  36.4 us
    all_to_all x1, blocking collectives, body(): lax.all_to_all(lanes_out, 'space', split_axis=0, concat_axis=0, tiled=True)  30.8 us
    all_to_all x1, blocking collectives, body(): lax.all_to_all(embed_partial.astype(jnp.bfloat16).reshape(PATCH, tm_count...  29.4 us
    reduce_scatter x1, waiting for transfers between devices, body(): lax.psum_scatter(contract(hidden, d_packed, 0, 0).astype(jnp.bfloat16), '...  25.9 us
    all_to_all x1, waiting for transfers between devices, body(): lax.all_to_all(grads, 'space', split_axis=0, concat_axis=0, tiled=True)  20.4 us
    all_to_all x1, waiting for transfers between devices, body(): lax.all_to_all(jnp.broadcast_to(local_embed[None], (tm_count,) + local_em...  17 us
    all_gather x1, blocking collectives, body(): wide_rows = lax.all_gather(qkv_weight, 'tm', axis=1, tiled=True)  16 us
    all_to_all x1, blocking collectives, body(): lax.all_to_all(padded.reshape(slab_count, chunk, -1), 'space', split_axis...  14.5 us
  transfers between devices with their start and end apart: 7, of which 5 were waited for; matrix products, arithmetic and copies ran while one was open for 9% of the time, Pallas kernels for 3%

profile of v10, /device:TPU:1, one launch (start us, length us, event | category | flops | bytes accessed | tf_op | source)
XLA Modules:
  0.0 319.7 jit_solution(5175756370061259540)
XLA Ops:
  7.2 16.0 %all_gather.6 = bf16[64,3072]{1,0:T(8,128)(2,1)} all-gather(bf16[64,384]{1,0:T(8,128)(2,1)} %param.10), channel_id=1, replica_groups=mesh['space'=16,'tm'=8] {'tm'}, dimensions={1}, use_global_device_ids=true | all-gather | bytes 442368 | tf_op jit(solution)/shard_map/all_gather | solution.py:242
  23.3 0.7 fusion.33
  24.2 0.7 fusion.37
  25.1 0.7 fusion.35
  26.7 0.6 reshape.246.keep_ref
  27.3 1.4 copy.49
  28.8 1.2 reshape.245.rows_ref
  30.1 9.5 %shard_map.77 = bf16[2,256,864]{2,1,0:T(8,128)(2,1)S(1)} custom-call(bf16[2,4,576,96]{3,2,1,0:T(8,128)(2,1)S(1)} %reshape.245.rows_ref, bf16[2,96,1536]{2,1,0:T(8,128)(2,1)S(1)} %fusion.6.pick_ref, bf16[2,96,1536]{2,1,0:T(8,128)(2,1)S(1)} %reshape.246.keep_ref, bf16[36,576]{1,0:T(8,128)(2,1)S(1)} %reshape.260.fold_ref), custom_call_target="tpu_custom_call" | custom-call | flops 2717908992 | bytes 1769472 | tf_op jit(solution)/shard_map/pallas_call | solution.py:67
  40.0 1.6 copy.51
  41.5 7.8 %all-to-all-start = ((bf16[2,16,12,896]{3,0,2,1:T(2,128)(2,1)}), bf16[2,16,12,896]{3,0,2,1:T(2,128)(2,1)S(1)}, u32[]{:S(2)}, u32[]{:S(2)}) async-start(bf16[2,16,12,896]{3,0,2,1:T(2,128)(2,1)} %bitcast.9), calls=%async_computation | async-start | bytes 1376256 | tf_op jit(solution)/shard_map/all_to_all | solution.py:214
  49.5 11.4 %all-to-all-done = bf16[2,16,12,896]{3,0,2,1:T(2,128)(2,1)S(1)} async-done(((bf16[2,16,12,896]{3,0,2,1:T(2,128)(2,1)}), bf16[2,16,12,896]{3,0,2,1:T(2,128)(2,1)S(1)}, u32[]{:S(2)}, u32[]{:S(2)}) %all-to-all-start) | async-done | bytes 688160 | tf_op jit(solution)/shard_map/all_to_all | solution.py:214
  61.0 1.4 broadcast_in_dim.25
  62.4 6.4 %all-to-all-start.1 = ((bf16[8,864,128]{2,1,0:T(8,128)(2,1)}), bf16[8,864,128]{2,1,0:T(8,128)(2,1)S(1)}, u32[]{:S(2)}, u32[]{:S(2)}) async-start(bf16[8,864,128]{2,1,0:T(8,128)(2,1)} %broadcast_in_dim.25), calls=%async_computation.1 | async-start | bytes 3538944 | tf_op jit(solution)/shard_map/all_to_all | solution.py:225
  68.8 1.3 copy.59
  70.2 1.4 copy.60
  71.8 1.4 convolution_convert_fusion.3
  73.2 1.3 copy.54
  74.5 17.0 %all-to-all-done.1 = bf16[8,864,128]{2,1,0:T(8,128)(2,1)S(1)} async-done(((bf16[8,864,128]{2,1,0:T(8,128)(2,1)}), bf16[8,864,128]{2,1,0:T(8,128)(2,1)S(1)}, u32[]{:S(2)}, u32[]{:S(2)}) %all-to-all-start.1) | async-done | bytes 1769504 | tf_op jit(solution)/shard_map/all_to_all | solution.py:225
  91.5 0.9 fusion.39
  92.4 0.3 copy.57
  93.0 0.8 copy-done.2
  93.7 5.8 %convolution_convert_fusion.1 = bf16[256,3072]{1,0:T(8,128)(2,1)} fusion(bf16[1024,3072]{1,0:T(8,128)(2,1)} %all-gather.2.cloned.1.call-done, f32[256,1024]{1,0:T(8,128)S(1)} %copy.57, f32[256]{0:T(256)S(1)} %add_rsqrt_fusion, f32[256]{0:T(256)S(1)} %broadcast_multiply_fusion.2), kind=kOutput, calls=%fused_computation.1 | convolution fusion | flops 1612185600 | bytes 8914944 | tf_op jit(solution)/shard_map/dot_general | solution.py:245
  99.5 1.7 copy.58
  101.2 1.9 reshape.251
  103.1 4.3 %maximum_bitcast_fusion = bf16[16,2,128,4,64]{2,1,4,0,3:T(2,128)(2,1)S(1)} fusion(bf16[2,128,1,16,64]{1,0,4,3,2:T(2,128)(2,1)S(1)} %copy-done.6, bf16[2,128,3,16,64]{1,0,4,3,2:T(2,128)(2,1)} %reshape.251), kind=kLoop, calls=%fused_computation.3 | loop fusion | flops 1048576 | bytes 4194304 | tf_op jit(solution)/shard_map/transpose | solution.py:249
  107.4 0.5 copy.61
  108.0 2.6 copy.62
  110.6 30.8 %all_to_all.40.lanes_ref = bf16[16,2,128,256]{3,2,1,0:T(8,128)(2,1)S(1)} all-to-all(bf16[16,2,128,256]{3,2,1,0:T(8,128)(2,1)} %copy.62), channel_id=1, replica_groups=mesh['space'=16,'tm'=8] {'space'}, dimensions={0} | all-to-all | bytes 4194304 | tf_op jit(solution)/shard_map/all_to_all | solution.py:250
  141.5 36.4 %shard_map.78 = bf16[16,2,128,192]{3,2,1,0:T(8,128)(2,1)S(1)} custom-call(bf16[16,2,128,256]{3,2,1,0:T(8,128)(2,1)S(1)} %all_to_all.40.lanes_ref), custom_call_target="tpu_custom_call" | custom-call | flops 5368709120 | bytes 3670016 | tf_op jit(solution)/shard_map/pallas_call | solution.py:141
  177.9 2.3 copy.63
  180.1 4.0 %all-to-all-start.3 = ((bf16[16,2,128,192]{2,3,1,0:T(8,128)(2,1)}), bf16[16,2,128,192]{2,3,1,0:T(8,128)(2,1)S(1)}, u32[]{:S(2)}, u32[]{:S(2)}) async-start(bf16[16,2,128,192]{2,3,1,0:T(8,128)(2,1)} %copy.63), calls=%async_computation.3 | async-start | bytes 3145728 | tf_op jit(solution)/shard_map/all_to_all | solution.py:252
  184.3 20.4 %all-to-all-done.3 = bf16[16,2,128,192]{2,3,1,0:T(8,128)(2,1)S(1)} async-done(((bf16[16,2,128,192]{2,3,1,0:T(8,128)(2,1)}), bf16[16,2,128,192]{2,3,1,0:T(8,128)(2,1)S(1)}, u32[]{:S(2)}, u32[]{:S(2)}) %all-to-all-start.3) | async-done | bytes 1572896 | tf_op jit(solution)/shard_map/all_to_all | solution.py:252
  204.7 1.6 copy.64
  206.3 1.2 copy-done
  207.5 4.5 %convolution_convert_fusion = bf16[1024,3072]{1,0:T(8,128)(2,1)} fusion(bf16[256,1024]{0,1:T(8,128)(2,1)S(1)} %bitcast.95, bf16[384,8,2,128]{3,2,1,0:T(2,128)(2,1)S(1)} %bitcast.91), kind=kOutput, calls=%fused_computation | convolution fusion | flops 1613758464 | bytes 8388608 | tf_op jit(solution)/shard_map/dot_general | solution.py:26
  212.0 1.4 copy-done.1
  213.7 4.8 %fusion.38 = (f32[256]{0:T(256)S(1)}, f32[256]{0:T(256)S(1)}, f32[256,1024]{1,0:T(8,128)S(1)}) fusion(f32[256]{0:T(256)S(1)} %add_rsqrt_fusion, f32[256,1024]{1,0:T(8,128)S(1)} %copy-done.3, f32[256]{0:T(256)S(1)} %broadcast_multiply_fusion.2, bf16[1024,3072]{1,0:T(8,128)(2,1)} %all-gather.2.cloned.1.call-done, bf16[384,8,2,128]{3,2,1,0:T(2,128)(2,1)S(1)} %bitcast.92), kind=kOutput, calls=%fused_computation.95 | convolution fusion | flops 1611922944 | bytes 9965568 | tf_op jit(solution)/shard_map/dot_general | solution.py:26
  218.6 0.8 convert_bitcast_fusion
  219.7 29.4 %all_to_all.41 = bf16[8,864,128]{2,1,0:T(8,128)(2,1)S(1)} all-to-all(bf16[8,864,128]{2,1,0:T(8,128)(2,1)S(1)} %bitcast.89), channel_id=1, replica_groups=mesh['space'=16,'tm'=8] {'tm'}, dimensions={0} | all-to-all | bytes 3538944 | tf_op jit(solution)/shard_map/all_to_all | solution.py:280
  249.4 14.5 %all_to_all.42 = f32[16,54,128]{2,1,0:T(8,128)S(1)} all-to-all(f32[16,54,128]{2,1,0:T(8,128)S(1)} %reshape.258), channel_id=1, replica_groups=mesh['space'=16,'tm'=8] {'space'}, dimensions={0} | all-to-all | bytes 884736 | tf_op jit(solution)/shard_map/all_to_all | solution.py:290
  263.9 0.8 broadcast_in_dim.26
  264.7 5.4 %all-to-all-start.7 = ((f32[16,54,128]{2,1,0:T(8,128)}), f32[16,54,128]{2,1,0:T(8,128)S(1)}, u32[]{:S(2)}, u32[]{:S(2)}) async-start(f32[16,54,128]{2,1,0:T(8,128)} %broadcast_in_dim.26), calls=%async_computation.8 | async-start | bytes 917504 | tf_op jit(solution)/shard_map/all_to_all | solution.py:294
  270.1 25.9 %reduce-scatter.2.cloned.1.call-done = bf16[64,3072]{1,0:T(8,128)(2,1)} async-done(((bf16[1024,3072]{1,0:T(8,128)(2,1)}), bf16[64,3072]{1,0:T(8,128)(2,1)}) %reduce-scatter.2.cloned.1.call-update) | async-done | bytes 393232 | tf_op jit(solution)/shard_map/reduce_scatter | solution.py:258
  296.0 1.8 copy.108
  297.8 6.7 %all-to-all-start.4 = ((bf16[8,64,384]{2,1,0:T(8,128)(2,1)}), bf16[8,64,384]{2,1,0:T(8,128)(2,1)S(1)}, u32[]{:S(2)}, u32[]{:S(2)}) async-start(bf16[8,64,384]{2,1,0:T(8,128)(2,1)} %bitcast.82), calls=%async_computation.5 | async-start | bytes 786432 | tf_op jit(solution)/shard_map/all_to_all | solution.py:266
  304.7 0.8 reshape.259
  305.5 6.7 %all-to-all-done.4 = bf16[8,64,384]{2,1,0:T(8,128)(2,1)S(1)} async-done(((bf16[8,64,384]{2,1,0:T(8,128)(2,1)}), bf16[8,64,384]{2,1,0:T(8,128)(2,1)S(1)}, u32[]{:S(2)}, u32[]{:S(2)}) %all-to-all-start.4) | async-done | bytes 393248 | tf_op jit(solution)/shard_map/all_to_all | solution.py:266
  312.2 0.7 convert_reduce_fusion.1
  (60 shorter events, 3.7 us)
Async XLA Ops:
  7.2 85.8 %all-gather.2.cloned.1.call-start = ((), (), s32[]{:S(2)}) async-start(), calls=%async_computation.9 | async-start | bytes 6684672 | tf_op jit(solution)/shard_map/all_gather | solution.py:243
  39.8 9.5 %copy-start.7 = (bf16[864,128]{1,0:T(8,128)(2,1)S(1)}, bf16[864,128]{1,0:T(8,128)(2,1)}, u32[]{:S(2)}) copy-start(bf16[864,128]{1,0:T(8,128)(2,1)} %param.9) | copy-start | bytes 663556
  41.5 19.4 %all-to-all-start = ((bf16[2,16,12,896]{3,0,2,1:T(2,128)(2,1)}), bf16[2,16,12,896]{3,0,2,1:T(2,128)(2,1)S(1)}, u32[]{:S(2)}, u32[]{:S(2)}) async-start(bf16[2,16,12,896]{3,0,2,1:T(2,128)(2,1)} %bitcast.9), calls=%async_computation | async-start | bytes 1376256 | tf_op jit(solution)/shard_map/all_to_all | solution.py:214
  62.4 29.1 %all-to-all-start.1 = ((bf16[8,864,128]{2,1,0:T(8,128)(2,1)}), bf16[8,864,128]{2,1,0:T(8,128)(2,1)S(1)}, u32[]{:S(2)}, u32[]{:S(2)}) async-start(bf16[8,864,128]{2,1,0:T(8,128)(2,1)} %broadcast_in_dim.25), calls=%async_computation.1 | async-start | bytes 3538944 | tf_op jit(solution)/shard_map/all_to_all | solution.py:225
  74.5 18.3 %copy-start.4 = (bf16[2,128,864]{2,1,0:T(8,128)(2,1)}, bf16[2,128,864]{2,1,0:T(8,128)(2,1)S(1)}, u32[]{:S(2)}) copy-start(bf16[2,128,864]{2,1,0:T(8,128)(2,1)S(1)} %copy.54) | copy-start | bytes 1327108
  92.7 1.0 copy-start.2
  101.2 1.9 copy-start.6
  180.1 24.5 %all-to-all-start.3 = ((bf16[16,2,128,192]{2,3,1,0:T(8,128)(2,1)}), bf16[16,2,128,192]{2,3,1,0:T(8,128)(2,1)S(1)}, u32[]{:S(2)}, u32[]{:S(2)}) async-start(bf16[16,2,128,192]{2,3,1,0:T(8,128)(2,1)} %copy.63), calls=%async_computation.3 | async-start | bytes 3145728 | tf_op jit(solution)/shard_map/all_to_all | solution.py:252
  184.1 111.9 %reduce-scatter.2.cloned.1.call-start = ((), (), s32[]{:S(2)}) async-start(), calls=%async_computation.10 | async-start | bytes 6684672 | tf_op jit(solution)/shard_map/reduce_scatter | solution.py:258
  206.3 1.2 copy-start
  212.0 1.4 copy-start.1
  212.0 1.7 copy-start.3
  213.7 4.9 %copy-start.5 = (bf16[2,128,864]{2,1,0:T(8,128)(2,1)S(1)}, bf16[2,128,864]{2,1,0:T(8,128)(2,1)}, u32[]{:S(2)}) copy-start(bf16[2,128,864]{2,1,0:T(8,128)(2,1)} %copy-done.4) | copy-start | bytes 1327108
  264.7 33.2 %all-to-all-start.7 = ((f32[16,54,128]{2,1,0:T(8,128)}), f32[16,54,128]{2,1,0:T(8,128)S(1)}, u32[]{:S(2)}, u32[]{:S(2)}) async-start(f32[16,54,128]{2,1,0:T(8,128)} %broadcast_in_dim.26), calls=%async_computation.8 | async-start | bytes 917504 | tf_op jit(solution)/shard_map/all_to_all | solution.py:294
  297.8 14.4 %all-to-all-start.4 = ((bf16[8,64,384]{2,1,0:T(8,128)(2,1)}), bf16[8,64,384]{2,1,0:T(8,128)(2,1)S(1)}, u32[]{:S(2)}, u32[]{:S(2)}) async-start(bf16[8,64,384]{2,1,0:T(8,128)(2,1)} %bitcast.82), calls=%async_computation.5 | async-start | bytes 786432 | tf_op jit(solution)/shard_map/all_to_all | solution.py:266
Sparse Core Ops, SparseCore 0:
  23.4 64.3 all-gather.1
  212.1 83.8 reduce-scatter.1

commit v11 on v10

--- a/solution.py
+++ b/solution.py
@@ -87,7 +87,7 @@
     )(rows, pick_z, keep_y, fold)
 
 
-QUERY_BLOCK = 256
+QUERY_BLOCK = 512
 
 
 def attention_kernel(lanes_ref, out_ref, k_s, v_s, dk_acc, dv_acc):
@@ -112,7 +112,7 @@
     value_rows = v_s[...]
     scores = contract(queries * jnp.asarray(factor, queries.dtype), key_rows, 1, 1)
     raised = jnp.exp(scores - jnp.max(scores, axis=1, keepdims=True))
-    attention = raised / jnp.sum(raised, axis=1, keepdims=True)
+    attention = raised * (1.0 / jnp.sum(raised, axis=1, keepdims=True))
     d_attention = contract(upstream, value_rows, 1, 1)
     inner_sum = jnp.sum(attention * d_attention, axis=1, keepdims=True)
     d_scores = (attention * (d_attention - inner_sum)).astype(jnp.bfloat16)

time: 321 us -> 317 us (0.988)
  Pallas kernels: 45.9 us -> 42.4 us
    pallas_call x1, Pallas kernels: 36.4 us -> 32.9 us  [attention_grads(): pl.pallas_call(attention_kernel, grid=(windows, owners // per_block), in_...]
where the time goes in v11:
time: 317 us; the launch traced here: 316 us
  blocking collectives  90.6 us (29%)
  waiting for transfers between devices  81 us (26%)
  Pallas kernels  42.4 us (13%)
  starting transfers between devices  30.5 us (10%)
  local copies, waits for them, and re-layouts  29.9 us (9%)
  matrix products  18.8 us (6%)
  between operations  14.4 us (5%)
  other arithmetic  8.18 us (3%)
    pallas_call x1, Pallas kernels, attention_grads(): pl.pallas_call(attention_kernel, grid=(windows, owners // per_block), in_...  32.9 us
    all_to_all x1, blocking collectives, body(): lax.all_to_all(lanes_out, 'space', split_axis=0, concat_axis=0, tiled=True)  30.8 us
    all_to_all x1, blocking collectives, body(): lax.all_to_all(embed_partial.astype(jnp.bfloat16).reshape(PATCH, tm_count...  29.3 us
    reduce_scatter x1, waiting for transfers between devices, body(): lax.psum_scatter(contract(hidden, d_packed, 0, 0).astype(jnp.bfloat16), '...  25.7 us
    all_to_all x1, waiting for transfers between devices, body(): lax.all_to_all(grads, 'space', split_axis=0, concat_axis=0, tiled=True)  20.1 us
    all_to_all x1, waiting for transfers between devices, body(): lax.all_to_all(jnp.broadcast_to(local_embed[None], (tm_count,) + local_em...  17 us
    all_gather x1, blocking collectives, body(): wide_rows = lax.all_gather(qkv_weight, 'tm', axis=1, tiled=True)  16 us
    all_to_all x1, blocking collectives, body(): lax.all_to_all(padded.reshape(slab_count, chunk, -1), 'space', split_axis...  14.4 us
  transfers between devices with their start and end apart: 7, of which 5 were waited for; matrix products, arithmetic and copies ran while one was open for 9% of the time, Pallas kernels for 3%

profile of v11, /device:TPU:1, one launch (start us, length us, event | category | flops | bytes accessed | tf_op | source)
XLA Modules:
  0.0 315.8 jit_solution(10387454931749118661)
XLA Ops:
  7.2 16.0 %all_gather.6 = bf16[64,3072]{1,0:T(8,128)(2,1)} all-gather(bf16[64,384]{1,0:T(8,128)(2,1)} %param.10), channel_id=1, replica_groups=mesh['space'=16,'tm'=8] {'tm'}, dimensions={1}, use_global_device_ids=true | all-gather | bytes 442368 | tf_op jit(solution)/shard_map/all_gather | solution.py:242
  23.3 0.7 fusion.33
  24.2 0.7 fusion.37
  25.1 0.7 fusion.35
  26.7 0.6 reshape.246.keep_ref
  27.3 1.4 copy.49
  28.8 1.2 reshape.245.rows_ref
  30.1 9.5 %shard_map.77 = bf16[2,256,864]{2,1,0:T(8,128)(2,1)S(1)} custom-call(bf16[2,4,576,96]{3,2,1,0:T(8,128)(2,1)S(1)} %reshape.245.rows_ref, bf16[2,96,1536]{2,1,0:T(8,128)(2,1)S(1)} %fusion.6.pick_ref, bf16[2,96,1536]{2,1,0:T(8,128)(2,1)S(1)} %reshape.246.keep_ref, bf16[36,576]{1,0:T(8,128)(2,1)S(1)} %reshape.260.fold_ref), custom_call_target="tpu_custom_call" | custom-call | flops 2717908992 | bytes 1769472 | tf_op jit(solution)/shard_map/pallas_call | solution.py:67
  40.0 1.6 copy.51
  41.5 7.8 %all-to-all-start = ((bf16[2,16,12,896]{3,0,2,1:T(2,128)(2,1)}), bf16[2,16,12,896]{3,0,2,1:T(2,128)(2,1)S(1)}, u32[]{:S(2)}, u32[]{:S(2)}) async-start(bf16[2,16,12,896]{3,0,2,1:T(2,128)(2,1)} %bitcast.9), calls=%async_computation | async-start | bytes 1376256 | tf_op jit(solution)/shard_map/all_to_all | solution.py:214
  49.5 11.4 %all-to-all-done = bf16[2,16,12,896]{3,0,2,1:T(2,128)(2,1)S(1)} async-done(((bf16[2,16,12,896]{3,0,2,1:T(2,128)(2,1)}), bf16[2,16,12,896]{3,0,2,1:T(2,128)(2,1)S(1)}, u32[]{:S(2)}, u32[]{:S(2)}) %all-to-all-start) | async-done | bytes 688160 | tf_op jit(solution)/shard_map/all_to_all | solution.py:214
  61.0 1.4 broadcast_in_dim.25
  62.4 6.4 %all-to-all-start.1 = ((bf16[8,864,128]{2,1,0:T(8,128)(2,1)}), bf16[8,864,128]{2,1,0:T(8,128)(2,1)S(1)}, u32[]{:S(2)}, u32[]{:S(2)}) async-start(bf16[8,864,128]{2,1,0:T(8,128)(2,1)} %broadcast_in_dim.25), calls=%async_computation.1 | async-start | bytes 3538944 | tf_op jit(solution)/shard_map/all_to_all | solution.py:225
  68.8 1.3 copy.59
  70.2 1.4 copy.60
  71.8 1.4 convolution_convert_fusion.3
  73.2 1.3 copy.54
  74.5 17.0 %all-to-all-done.1 = bf16[8,864,128]{2,1,0:T(8,128)(2,1)S(1)} async-done(((bf16[8,864,128]{2,1,0:T(8,128)(2,1)}), bf16[8,864,128]{2,1,0:T(8,128)(2,1)S(1)}, u32[]{:S(2)}, u32[]{:S(2)}) %all-to-all-start.1) | async-done | bytes 1769504 | tf_op jit(solution)/shard_map/all_to_all | solution.py:225
  91.5 0.9 fusion.39
  92.4 0.3 copy.57
  93.0 0.8 copy-done.2
  93.7 5.8 %convolution_convert_fusion.1 = bf16[256,3072]{1,0:T(8,128)(2,1)} fusion(bf16[1024,3072]{1,0:T(8,128)(2,1)} %all-gather.2.cloned.1.call-done, f32[256,1024]{1,0:T(8,128)S(1)} %copy.57, f32[256]{0:T(256)S(1)} %add_rsqrt_fusion, f32[256]{0:T(256)S(1)} %broadcast_multiply_fusion.2), kind=kOutput, calls=%fused_computation.1 | convolution fusion | flops 1612185600 | bytes 8914944 | tf_op jit(solution)/shard_map/dot_general | solution.py:245
  99.5 1.7 copy.58
  101.2 1.9 reshape.251
  103.1 4.3 %maximum_bitcast_fusion = bf16[16,2,128,4,64]{2,1,4,0,3:T(2,128)(2,1)S(1)} fusion(bf16[2,128,1,16,64]{1,0,4,3,2:T(2,128)(2,1)S(1)} %copy-done.6, bf16[2,128,3,16,64]{1,0,4,3,2:T(2,128)(2,1)} %reshape.251), kind=kLoop, calls=%fused_computation.3 | loop fusion | flops 1048576 | bytes 4194304 | tf_op jit(solution)/shard_map/transpose | solution.py:249
  107.4 0.5 copy.61
  108.0 2.6 copy.62
  110.6 30.8 %all_to_all.40.lanes_ref = bf16[16,2,128,256]{3,2,1,0:T(8,128)(2,1)S(1)} all-to-all(bf16[16,2,128,256]{3,2,1,0:T(8,128)(2,1)} %copy.62), channel_id=1, replica_groups=mesh['space'=16,'tm'=8] {'space'}, dimensions={0} | all-to-all | bytes 4194304 | tf_op jit(solution)/shard_map/all_to_all | solution.py:250
  141.5 32.9 %shard_map.78 = bf16[16,2,128,192]{3,2,1,0:T(8,128)(2,1)S(1)} custom-call(bf16[16,2,128,256]{3,2,1,0:T(8,128)(2,1)S(1)} %all_to_all.40.lanes_ref), custom_call_target="tpu_custom_call" | custom-call | flops 5368709120 | bytes 3670016 | tf_op jit(solution)/shard_map/pallas_call | solution.py:141
  174.4 2.3 copy.63
  176.7 3.8 %all-to-all-start.3 = ((bf16[16,2,128,192]{2,3,1,0:T(8,128)(2,1)}), bf16[16,2,128,192]{2,3,1,0:T(8,128)(2,1)S(1)}, u32[]{:S(2)}, u32[]{:S(2)}) async-start(bf16[16,2,128,192]{2,3,1,0:T(8,128)(2,1)} %copy.63), calls=%async_computation.3 | async-start | bytes 3145728 | tf_op jit(solution)/shard_map/all_to_all | solution.py:252
  180.9 20.1 %all-to-all-done.3 = bf16[16,2,128,192]{2,3,1,0:T(8,128)(2,1)S(1)} async-done(((bf16[16,2,128,192]{2,3,1,0:T(8,128)(2,1)}), bf16[16,2,128,192]{2,3,1,0:T(8,128)(2,1)S(1)}, u32[]{:S(2)}, u32[]{:S(2)}) %all-to-all-start.3) | async-done | bytes 1572896 | tf_op jit(solution)/shard_map/all_to_all | solution.py:252
  201.0 1.6 copy.64
  202.6 1.2 copy-done
  203.8 4.5 %convolution_convert_fusion = bf16[1024,3072]{1,0:T(8,128)(2,1)} fusion(bf16[256,1024]{0,1:T(8,128)(2,1)S(1)} %bitcast.95, bf16[384,8,2,128]{3,2,1,0:T(2,128)(2,1)S(1)} %bitcast.91), kind=kOutput, calls=%fused_computation | convolution fusion | flops 1613758464 | bytes 8388608 | tf_op jit(solution)/shard_map/dot_general | solution.py:26
  208.3 1.4 copy-done.1
  210.0 4.8 %fusion.38 = (f32[256]{0:T(256)S(1)}, f32[256]{0:T(256)S(1)}, f32[256,1024]{1,0:T(8,128)S(1)}) fusion(f32[256]{0:T(256)S(1)} %add_rsqrt_fusion, f32[256,1024]{1,0:T(8,128)S(1)} %copy-done.3, f32[256]{0:T(256)S(1)} %broadcast_multiply_fusion.2, bf16[1024,3072]{1,0:T(8,128)(2,1)} %all-gather.2.cloned.1.call-done, bf16[384,8,2,128]{3,2,1,0:T(2,128)(2,1)S(1)} %bitcast.92), kind=kOutput, calls=%fused_computation.95 | convolution fusion | flops 1611922944 | bytes 9965568 | tf_op jit(solution)/shard_map/dot_general | solution.py:26
  214.9 0.8 convert_bitcast_fusion
  216.0 29.3 %all_to_all.41 = bf16[8,864,128]{2,1,0:T(8,128)(2,1)S(1)} all-to-all(bf16[8,864,128]{2,1,0:T(8,128)(2,1)S(1)} %bitcast.89), channel_id=1, replica_groups=mesh['space'=16,'tm'=8] {'tm'}, dimensions={0} | all-to-all | bytes 3538944 | tf_op jit(solution)/shard_map/all_to_all | solution.py:280
  245.6 14.4 %all_to_all.42 = f32[16,54,128]{2,1,0:T(8,128)S(1)} all-to-all(f32[16,54,128]{2,1,0:T(8,128)S(1)} %reshape.258), channel_id=1, replica_groups=mesh['space'=16,'tm'=8] {'space'}, dimensions={0} | all-to-all | bytes 884736 | tf_op jit(solution)/shard_map/all_to_all | solution.py:290
  260.0 0.8 broadcast_in_dim.26
  260.9 5.6 %all-to-all-start.7 = ((f32[16,54,128]{2,1,0:T(8,128)}), f32[16,54,128]{2,1,0:T(8,128)S(1)}, u32[]{:S(2)}, u32[]{:S(2)}) async-start(f32[16,54,128]{2,1,0:T(8,128)} %broadcast_in_dim.26), calls=%async_computation.8 | async-start | bytes 917504 | tf_op jit(solution)/shard_map/all_to_all | solution.py:294
  266.4 25.7 %reduce-scatter.2.cloned.1.call-done = bf16[64,3072]{1,0:T(8,128)(2,1)} async-done(((bf16[1024,3072]{1,0:T(8,128)(2,1)}), bf16[64,3072]{1,0:T(8,128)(2,1)}) %reduce-scatter.2.cloned.1.call-update) | async-done | bytes 393232 | tf_op jit(solution)/shard_map/reduce_scatter | solution.py:258
  292.1 1.8 copy.108
  293.9 6.7 %all-to-all-start.4 = ((bf16[8,64,384]{2,1,0:T(8,128)(2,1)}), bf16[8,64,384]{2,1,0:T(8,128)(2,1)S(1)}, u32[]{:S(2)}, u32[]{:S(2)}) async-start(bf16[8,64,384]{2,1,0:T(8,128)(2,1)} %bitcast.82), calls=%async_computation.5 | async-start | bytes 786432 | tf_op jit(solution)/shard_map/all_to_all | solution.py:266
  300.8 0.8 reshape.259
  301.6 6.7 %all-to-all-done.4 = bf16[8,64,384]{2,1,0:T(8,128)(2,1)S(1)} async-done(((bf16[8,64,384]{2,1,0:T(8,128)(2,1)}), bf16[8,64,384]{2,1,0:T(8,128)(2,1)S(1)}, u32[]{:S(2)}, u32[]{:S(2)}) %all-to-all-start.4) | async-done | bytes 393248 | tf_op jit(solution)/shard_map/all_to_all | solution.py:266
  308.3 0.7 convert_reduce_fusion.1
  (60 shorter events, 4.0 us)
Async XLA Ops:
  7.2 85.8 %all-gather.2.cloned.1.call-start = ((), (), s32[]{:S(2)}) async-start(), calls=%async_computation.9 | async-start | bytes 6684672 | tf_op jit(solution)/shard_map/all_gather | solution.py:243
  39.8 9.5 %copy-start.7 = (bf16[864,128]{1,0:T(8,128)(2,1)S(1)}, bf16[864,128]{1,0:T(8,128)(2,1)}, u32[]{:S(2)}) copy-start(bf16[864,128]{1,0:T(8,128)(2,1)} %param.9) | copy-start | bytes 663556
  41.5 19.4 %all-to-all-start = ((bf16[2,16,12,896]{3,0,2,1:T(2,128)(2,1)}), bf16[2,16,12,896]{3,0,2,1:T(2,128)(2,1)S(1)}, u32[]{:S(2)}, u32[]{:S(2)}) async-start(bf16[2,16,12,896]{3,0,2,1:T(2,128)(2,1)} %bitcast.9), calls=%async_computation | async-start | bytes 1376256 | tf_op jit(solution)/shard_map/all_to_all | solution.py:214
  62.4 29.1 %all-to-all-start.1 = ((bf16[8,864,128]{2,1,0:T(8,128)(2,1)}), bf16[8,864,128]{2,1,0:T(8,128)(2,1)S(1)}, u32[]{:S(2)}, u32[]{:S(2)}) async-start(bf16[8,864,128]{2,1,0:T(8,128)(2,1)} %broadcast_in_dim.25), calls=%async_computation.1 | async-start | bytes 3538944 | tf_op jit(solution)/shard_map/all_to_all | solution.py:225
  74.5 18.3 %copy-start.4 = (bf16[2,128,864]{2,1,0:T(8,128)(2,1)}, bf16[2,128,864]{2,1,0:T(8,128)(2,1)S(1)}, u32[]{:S(2)}) copy-start(bf16[2,128,864]{2,1,0:T(8,128)(2,1)S(1)} %copy.54) | copy-start | bytes 1327108
  92.7 1.0 copy-start.2
  101.2 1.9 copy-start.6
  176.7 24.3 %all-to-all-start.3 = ((bf16[16,2,128,192]{2,3,1,0:T(8,128)(2,1)}), bf16[16,2,128,192]{2,3,1,0:T(8,128)(2,1)S(1)}, u32[]{:S(2)}, u32[]{:S(2)}) async-start(bf16[16,2,128,192]{2,3,1,0:T(8,128)(2,1)} %copy.63), calls=%async_computation.3 | async-start | bytes 3145728 | tf_op jit(solution)/shard_map/all_to_all | solution.py:252
  180.4 111.7 %reduce-scatter.2.cloned.1.call-start = ((), (), s32[]{:S(2)}) async-start(), calls=%async_computation.10 | async-start | bytes 6684672 | tf_op jit(solution)/shard_map/reduce_scatter | solution.py:258
  202.6 1.2 copy-start
  208.3 1.4 copy-start.1
  208.3 1.7 copy-start.3
  210.0 4.9 %copy-start.5 = (bf16[2,128,864]{2,1,0:T(8,128)(2,1)S(1)}, bf16[2,128,864]{2,1,0:T(8,128)(2,1)}, u32[]{:S(2)}) copy-start(bf16[2,128,864]{2,1,0:T(8,128)(2,1)} %copy-done.4) | copy-start | bytes 1327108
  260.9 33.1 %all-to-all-start.7 = ((f32[16,54,128]{2,1,0:T(8,128)}), f32[16,54,128]{2,1,0:T(8,128)S(1)}, u32[]{:S(2)}, u32[]{:S(2)}) async-start(f32[16,54,128]{2,1,0:T(8,128)} %broadcast_in_dim.26), calls=%async_computation.8 | async-start | bytes 917504 | tf_op jit(solution)/shard_map/all_to_all | solution.py:294
  293.9 14.4 %all-to-all-start.4 = ((bf16[8,64,384]{2,1,0:T(8,128)(2,1)}), bf16[8,64,384]{2,1,0:T(8,128)(2,1)S(1)}, u32[]{:S(2)}, u32[]{:S(2)}) async-start(bf16[8,64,384]{2,1,0:T(8,128)(2,1)} %bitcast.82), calls=%async_computation.5 | async-start | bytes 786432 | tf_op jit(solution)/shard_map/all_to_all | solution.py:266
Sparse Core Ops, SparseCore 0:
  23.4 64.3 all-gather.1
  208.4 83.6 reduce-scatter.1

commit v12 on v11

--- a/solution.py
+++ b/solution.py
@@ -239,7 +239,17 @@
     inverse = lax.rsqrt(jnp.mean(center * center, axis=1, keepdims=True) + 1e-05)
     normed = center * inverse
     hidden = normed.astype(jnp.bfloat16)
-    wide_rows = lax.all_gather(qkv_weight, "tm", axis=1, tiled=True)
+    wide_rows = (
+        lax.all_to_all(
+            jnp.broadcast_to(qkv_weight[None], (tm_count,) + qkv_weight.shape),
+            "tm",
+            split_axis=0,
+            concat_axis=0,
+            tiled=True,
+        )
+        .transpose(1, 0, 2)
+        .reshape(qkv_weight.shape[0], -1)
+    )
     full_qkv = lax.all_gather(wide_rows, "space", axis=0, tiled=True)
     heads = D // HD
     packed = jnp.dot(hidden, full_qkv, preferred_element_type=jnp.float32).astype(jnp.bfloat16)

time: 317 us -> 314 us (level)
    all_gather x1 -> x0, blocking collectives: 16 us -> none  [body(): wide_rows = lax.all_gather(qkv_weight, 'tm', axis=1, tiled=True)]
    all_to_all x0 -> x1, blocking collectives: none -> 13.6 us  [body(): lax.all_to_all(jnp.broadcast_to(qkv_weight[None], (tm_count,) + qkv_weigh...]
    unnamed x22 -> x26, local copies, waits for them, and re-layouts: 6.7 us -> 6.69 us
  transfers between devices with their start and end apart: 7 -> 7, of which waited for: 5 -> 5; matrix products, arithmetic and copies ran while one was open for 9% -> 8% of each run, Pallas kernels for 3% -> 3%
where the time goes in v12:
time: 314 us; the launch traced here: 312 us
  blocking collectives  88.8 us (28%)
  waiting for transfers between devices  81.1 us (26%)
  Pallas kernels  42.4 us (14%)
  local copies, waits for them, and re-layouts  31.5 us (10%)
  starting transfers between devices  29.2 us (9%)
  matrix products  18.8 us (6%)
  between operations  14.5 us (5%)
  other arithmetic  6.13 us (2%)
    pallas_call x1, Pallas kernels, attention_grads(): pl.pallas_call(attention_kernel, grid=(windows, owners // per_block), in_...  32.9 us
    all_to_all x1, blocking collectives, body(): lax.all_to_all(lanes_out, 'space', split_axis=0, concat_axis=0, tiled=True)  30.9 us
    all_to_all x1, blocking collectives, body(): lax.all_to_all(embed_partial.astype(jnp.bfloat16).reshape(PATCH, tm_count...  29.4 us
    reduce_scatter x1, waiting for transfers between devices, body(): lax.psum_scatter(contract(hidden, d_packed, 0, 0).astype(jnp.bfloat16), '...  25.6 us
    all_to_all x1, waiting for transfers between devices, body(): lax.all_to_all(grads, 'space', split_axis=0, concat_axis=0, tiled=True)  20.1 us
    all_to_all x1, waiting for transfers between devices, body(): lax.all_to_all(jnp.broadcast_to(local_embed[None], (tm_count,) + local_em...  17 us
    all_to_all x1, blocking collectives, body(): lax.all_to_all(padded.reshape(slab_count, chunk, -1), 'space', split_axis...  14.9 us
    all_to_all x1, blocking collectives, body(): lax.all_to_all(jnp.broadcast_to(qkv_weight[None], (tm_count,) + qkv_weigh...  13.6 us
  transfers between devices with their start and end apart: 7, of which 5 were waited for; matrix products, arithmetic and copies ran while one was open for 8% of the time, Pallas kernels for 3%

profile of v12, /device:TPU:1, one launch (start us, length us, event | category | flops | bytes accessed | tf_op | source)
XLA Modules:
  0.0 312.5 jit_solution(15300761800797417472)
XLA Ops:
  7.2 0.8 broadcast_in_dim.28
  8.1 13.6 %all_to_all.45 = bf16[8,64,384]{2,1,0:T(8,128)(2,1)S(1)} all-to-all(bf16[8,64,384]{2,1,0:T(8,128)(2,1)S(1)} %broadcast_in_dim.28), channel_id=1, replica_groups=mesh['space'=16,'tm'=8] {'tm'}, dimensions={0} | all-to-all | bytes 786432 | tf_op jit(solution)/shard_map/all_to_all | solution.py:243
  21.7 0.8 copy.81
  23.9 0.6 reshape.250.keep_ref
  24.6 1.4 copy.50
  26.0 1.2 reshape.249.rows_ref
  27.4 9.5 %shard_map.77 = bf16[2,256,864]{2,1,0:T(8,128)(2,1)S(1)} custom-call(bf16[2,4,576,96]{3,2,1,0:T(8,128)(2,1)S(1)} %reshape.249.rows_ref, bf16[2,96,1536]{2,1,0:T(8,128)(2,1)S(1)} %fusion.6.pick_ref, bf16[2,96,1536]{2,1,0:T(8,128)(2,1)S(1)} %reshape.250.keep_ref, bf16[36,576]{1,0:T(8,128)(2,1)S(1)} %reshape.265.fold_ref), custom_call_target="tpu_custom_call" | custom-call | flops 2717908992 | bytes 1769472 | tf_op jit(solution)/shard_map/pallas_call | solution.py:67
  37.2 1.6 copy.52
  38.8 7.8 %all-to-all-start = ((bf16[2,16,12,896]{3,0,2,1:T(2,128)(2,1)}), bf16[2,16,12,896]{3,0,2,1:T(2,128)(2,1)S(1)}, u32[]{:S(2)}, u32[]{:S(2)}) async-start(bf16[2,16,12,896]{3,0,2,1:T(2,128)(2,1)} %bitcast.9), calls=%async_computation | async-start | bytes 1376256 | tf_op jit(solution)/shard_map/all_to_all | solution.py:214
  46.8 11.7 %all-to-all-done = bf16[2,16,12,896]{3,0,2,1:T(2,128)(2,1)S(1)} async-done(((bf16[2,16,12,896]{3,0,2,1:T(2,128)(2,1)}), bf16[2,16,12,896]{3,0,2,1:T(2,128)(2,1)S(1)}, u32[]{:S(2)}, u32[]{:S(2)}) %all-to-all-start) | async-done | bytes 688160 | tf_op jit(solution)/shard_map/all_to_all | solution.py:214
  58.5 1.4 broadcast_in_dim.27
  59.9 5.8 %all-to-all-start.1 = ((bf16[8,864,128]{2,1,0:T(8,128)(2,1)}), bf16[8,864,128]{2,1,0:T(8,128)(2,1)S(1)}, u32[]{:S(2)}, u32[]{:S(2)}) async-start(bf16[8,864,128]{2,1,0:T(8,128)(2,1)} %broadcast_in_dim.27), calls=%async_computation.1 | async-start | bytes 3538944 | tf_op jit(solution)/shard_map/all_to_all | solution.py:225
  65.7 1.3 copy.61
  67.0 1.4 copy.62
  68.7 1.4 convolution_convert_fusion.3
  70.1 1.3 copy.55
  71.4 17.0 %all-to-all-done.1 = bf16[8,864,128]{2,1,0:T(8,128)(2,1)S(1)} async-done(((bf16[8,864,128]{2,1,0:T(8,128)(2,1)}), bf16[8,864,128]{2,1,0:T(8,128)(2,1)S(1)}, u32[]{:S(2)}, u32[]{:S(2)}) %all-to-all-start.1) | async-done | bytes 1769504 | tf_op jit(solution)/shard_map/all_to_all | solution.py:225
  88.4 0.9 fusion.39
  89.3 0.3 copy.58
  89.9 0.7 copy-done.2
  90.6 5.8 %convolution_convert_fusion.1 = bf16[256,3072]{1,0:T(8,128)(2,1)} fusion(bf16[1024,3072]{1,0:T(8,128)(2,1)} %all-gather.2.cloned.1.call-done, f32[256,1024]{1,0:T(8,128)S(1)} %copy.58, f32[256]{0:T(256)S(1)} %add_rsqrt_fusion, f32[256]{0:T(256)S(1)} %broadcast_multiply_fusion.2), kind=kOutput, calls=%fused_computation.1 | convolution fusion | flops 1612185600 | bytes 8914944 | tf_op jit(solution)/shard_map/dot_general | solution.py:255
  96.4 1.7 copy.60
  98.1 1.9 reshape.256
  100.0 4.3 %maximum_bitcast_fusion = bf16[16,2,128,4,64]{2,1,4,0,3:T(2,128)(2,1)S(1)} fusion(bf16[2,128,1,16,64]{1,0,4,3,2:T(2,128)(2,1)S(1)} %copy-done.6, bf16[2,128,3,16,64]{1,0,4,3,2:T(2,128)(2,1)} %reshape.256), kind=kLoop, calls=%fused_computation.3 | loop fusion | flops 1048576 | bytes 4194304 | tf_op jit(solution)/shard_map/transpose | solution.py:259
  104.3 0.5 copy.63
  104.8 2.6 copy.64
  107.5 30.9 %all_to_all.46.lanes_ref = bf16[16,2,128,256]{3,2,1,0:T(8,128)(2,1)S(1)} all-to-all(bf16[16,2,128,256]{3,2,1,0:T(8,128)(2,1)} %copy.64), channel_id=1, replica_groups=mesh['space'=16,'tm'=8] {'space'}, dimensions={0} | all-to-all | bytes 4194304 | tf_op jit(solution)/shard_map/all_to_all | solution.py:260
  138.3 32.9 %shard_map.78 = bf16[16,2,128,192]{3,2,1,0:T(8,128)(2,1)S(1)} custom-call(bf16[16,2,128,256]{3,2,1,0:T(8,128)(2,1)S(1)} %all_to_all.46.lanes_ref), custom_call_target="tpu_custom_call" | custom-call | flops 5368709120 | bytes 3670016 | tf_op jit(solution)/shard_map/pallas_call | solution.py:141
  171.2 2.3 copy.65
  173.5 3.8 %all-to-all-start.4 = ((bf16[16,2,128,192]{2,3,1,0:T(8,128)(2,1)}), bf16[16,2,128,192]{2,3,1,0:T(8,128)(2,1)S(1)}, u32[]{:S(2)}, u32[]{:S(2)}) async-start(bf16[16,2,128,192]{2,3,1,0:T(8,128)(2,1)} %copy.65), calls=%async_computation.4 | async-start | bytes 3145728 | tf_op jit(solution)/shard_map/all_to_all | solution.py:262
  177.7 20.1 %all-to-all-done.4 = bf16[16,2,128,192]{2,3,1,0:T(8,128)(2,1)S(1)} async-done(((bf16[16,2,128,192]{2,3,1,0:T(8,128)(2,1)}), bf16[16,2,128,192]{2,3,1,0:T(8,128)(2,1)S(1)}, u32[]{:S(2)}, u32[]{:S(2)}) %all-to-all-start.4) | async-done | bytes 1572896 | tf_op jit(solution)/shard_map/all_to_all | solution.py:262
  197.8 1.6 copy.66
  199.5 1.2 copy-done
  200.6 4.5 %convolution_convert_fusion = bf16[1024,3072]{1,0:T(8,128)(2,1)} fusion(bf16[256,1024]{0,1:T(8,128)(2,1)S(1)} %bitcast.98, bf16[384,8,2,128]{3,2,1,0:T(2,128)(2,1)S(1)} %bitcast.94), kind=kOutput, calls=%fused_computation | convolution fusion | flops 1613758464 | bytes 8388608 | tf_op jit(solution)/shard_map/dot_general | solution.py:26
  205.2 1.4 copy-done.1
  206.8 4.8 %fusion.38 = (f32[256]{0:T(256)S(1)}, f32[256]{0:T(256)S(1)}, f32[256,1024]{1,0:T(8,128)S(1)}) fusion(f32[256]{0:T(256)S(1)} %add_rsqrt_fusion, f32[256,1024]{1,0:T(8,128)S(1)} %copy-done.3, f32[256]{0:T(256)S(1)} %broadcast_multiply_fusion.2, bf16[1024,3072]{1,0:T(8,128)(2,1)} %all-gather.2.cloned.1.call-done, bf16[384,8,2,128]{3,2,1,0:T(2,128)(2,1)S(1)} %bitcast.95), kind=kOutput, calls=%fused_computation.95 | convolution fusion | flops 1611922944 | bytes 9965568 | tf_op jit(solution)/shard_map/dot_general | solution.py:26
  211.7 0.8 convert_bitcast_fusion
  212.5 0.3 copy.110
  212.8 29.4 %all_to_all.47 = bf16[8,864,128]{2,1,0:T(8,128)(2,1)S(1)} all-to-all(bf16[8,864,128]{2,1,0:T(8,128)(2,1)S(1)} %bitcast.92), channel_id=1, replica_groups=mesh['space'=16,'tm'=8] {'tm'}, dimensions={0} | all-to-all | bytes 3538944 | tf_op jit(solution)/shard_map/all_to_all | solution.py:290
  242.5 14.9 %all_to_all.48 = f32[16,54,128]{2,1,0:T(8,128)S(1)} all-to-all(f32[16,54,128]{2,1,0:T(8,128)S(1)} %reshape.263), channel_id=1, replica_groups=mesh['space'=16,'tm'=8] {'space'}, dimensions={0} | all-to-all | bytes 884736 | tf_op jit(solution)/shard_map/all_to_all | solution.py:300
  257.5 0.8 broadcast_in_dim.29
  258.3 4.9 %all-to-all-start.8 = ((f32[16,54,128]{2,1,0:T(8,128)}), f32[16,54,128]{2,1,0:T(8,128)S(1)}, u32[]{:S(2)}, u32[]{:S(2)}) async-start(f32[16,54,128]{2,1,0:T(8,128)} %broadcast_in_dim.29), calls=%async_computation.9 | async-start | bytes 917504 | tf_op jit(solution)/shard_map/all_to_all | solution.py:304
  263.2 25.6 %reduce-scatter.2.cloned.1.call-done = bf16[64,3072]{1,0:T(8,128)(2,1)} async-done(((bf16[1024,3072]{1,0:T(8,128)(2,1)}), bf16[64,3072]{1,0:T(8,128)(2,1)}) %reduce-scatter.2.cloned.1.call-update) | async-done | bytes 393232 | tf_op jit(solution)/shard_map/reduce_scatter | solution.py:268
  288.8 1.8 copy.111
  290.6 6.7 %all-to-all-start.5 = ((bf16[8,64,384]{2,1,0:T(8,128)(2,1)}), bf16[8,64,384]{2,1,0:T(8,128)(2,1)S(1)}, u32[]{:S(2)}, u32[]{:S(2)}) async-start(bf16[8,64,384]{2,1,0:T(8,128)(2,1)} %bitcast.85), calls=%async_computation.6 | async-start | bytes 786432 | tf_op jit(solution)/shard_map/all_to_all | solution.py:276
  297.5 0.8 reshape.264
  298.3 6.7 %all-to-all-done.5 = bf16[8,64,384]{2,1,0:T(8,128)(2,1)S(1)} async-done(((bf16[8,64,384]{2,1,0:T(8,128)(2,1)}), bf16[8,64,384]{2,1,0:T(8,128)(2,1)S(1)}, u32[]{:S(2)}, u32[]{:S(2)}) %all-to-all-start.5) | async-done | bytes 393248 | tf_op jit(solution)/shard_map/all_to_all | solution.py:276
  304.9 0.7 convert_reduce_fusion.1
  (66 shorter events, 3.7 us)
Async XLA Ops:
  7.2 15.4 %copy-start.8 = (s32[2,256]{1,0:T(2,128)S(1)}, s32[2,256]{1,0:T(2,128)}, u32[]{:S(2)}) copy-start(s32[2,256]{1,0:T(2,128)} %param.8) | copy-start | bytes 6148
  7.2 15.8 %copy-start.9 = (s32[2,256]{1,0:T(2,128)S(1)}, s32[2,256]{1,0:T(2,128)}, u32[]{:S(2)}) copy-start(s32[2,256]{1,0:T(2,128)} %param.7) | copy-start | bytes 6148
  7.2 82.7 %all-gather.2.cloned.1.call-start = ((), (), s32[]{:S(2)}) async-start(), calls=%async_computation.10 | async-start | bytes 6684672 | tf_op jit(solution)/shard_map/all_gather | solution.py:253
  37.0 9.5 %copy-start.7 = (bf16[864,128]{1,0:T(8,128)(2,1)S(1)}, bf16[864,128]{1,0:T(8,128)(2,1)}, u32[]{:S(2)}) copy-start(bf16[864,128]{1,0:T(8,128)(2,1)} %param.9) | copy-start | bytes 663556
  38.8 19.7 %all-to-all-start = ((bf16[2,16,12,896]{3,0,2,1:T(2,128)(2,1)}), bf16[2,16,12,896]{3,0,2,1:T(2,128)(2,1)S(1)}, u32[]{:S(2)}, u32[]{:S(2)}) async-start(bf16[2,16,12,896]{3,0,2,1:T(2,128)(2,1)} %bitcast.9), calls=%async_computation | async-start | bytes 1376256 | tf_op jit(solution)/shard_map/all_to_all | solution.py:214
  59.9 28.5 %all-to-all-start.1 = ((bf16[8,864,128]{2,1,0:T(8,128)(2,1)}), bf16[8,864,128]{2,1,0:T(8,128)(2,1)S(1)}, u32[]{:S(2)}, u32[]{:S(2)}) async-start(bf16[8,864,128]{2,1,0:T(8,128)(2,1)} %broadcast_in_dim.27), calls=%async_computation.1 | async-start | bytes 3538944 | tf_op jit(solution)/shard_map/all_to_all | solution.py:225
  71.3 18.3 %copy-start.4 = (bf16[2,128,864]{2,1,0:T(8,128)(2,1)}, bf16[2,128,864]{2,1,0:T(8,128)(2,1)S(1)}, u32[]{:S(2)}) copy-start(bf16[2,128,864]{2,1,0:T(8,128)(2,1)S(1)} %copy.55) | copy-start | bytes 1327108
  89.6 1.0 copy-start.2
  98.1 1.9 copy-start.6
  173.5 24.3 %all-to-all-start.4 = ((bf16[16,2,128,192]{2,3,1,0:T(8,128)(2,1)}), bf16[16,2,128,192]{2,3,1,0:T(8,128)(2,1)S(1)}, u32[]{:S(2)}, u32[]{:S(2)}) async-start(bf16[16,2,128,192]{2,3,1,0:T(8,128)(2,1)} %copy.65), calls=%async_computation.4 | async-start | bytes 3145728 | tf_op jit(solution)/shard_map/all_to_all | solution.py:262
  177.3 111.5 %reduce-scatter.2.cloned.1.call-start = ((), (), s32[]{:S(2)}) async-start(), calls=%async_computation.11 | async-start | bytes 6684672 | tf_op jit(solution)/shard_map/reduce_scatter | solution.py:268
  199.4 1.2 copy-start
  205.1 1.4 copy-start.1
  205.1 1.7 copy-start.3
  206.8 4.9 %copy-start.5 = (bf16[2,128,864]{2,1,0:T(8,128)(2,1)S(1)}, bf16[2,128,864]{2,1,0:T(8,128)(2,1)}, u32[]{:S(2)}) copy-start(bf16[2,128,864]{2,1,0:T(8,128)(2,1)} %copy-done.4) | copy-start | bytes 1327108
  258.3 32.3 %all-to-all-start.8 = ((f32[16,54,128]{2,1,0:T(8,128)}), f32[16,54,128]{2,1,0:T(8,128)S(1)}, u32[]{:S(2)}, u32[]{:S(2)}) async-start(f32[16,54,128]{2,1,0:T(8,128)} %broadcast_in_dim.29), calls=%async_computation.9 | async-start | bytes 917504 | tf_op jit(solution)/shard_map/all_to_all | solution.py:304
  290.6 14.4 %all-to-all-start.5 = ((bf16[8,64,384]{2,1,0:T(8,128)(2,1)}), bf16[8,64,384]{2,1,0:T(8,128)(2,1)S(1)}, u32[]{:S(2)}, u32[]{:S(2)}) async-start(bf16[8,64,384]{2,1,0:T(8,128)(2,1)} %bitcast.85), calls=%async_computation.6 | async-start | bytes 786432 | tf_op jit(solution)/shard_map/all_to_all | solution.py:276
Sparse Core Ops, SparseCore 0:
  22.7 63.4 all-gather.1
  205.3 83.4 reduce-scatter.1

commit v13 on v12

--- a/solution.py
+++ b/solution.py
@@ -87,7 +87,7 @@
     )(rows, pick_z, keep_y, fold)
 
 
-QUERY_BLOCK = 512
+QUERY_BLOCK = 1024
 
 
 def attention_kernel(lanes_ref, out_ref, k_s, v_s, dk_acc, dv_acc):

time: 314 us -> 311 us (level)
  no operation moved by 1% of the time
where the time goes in v13:
time: 311 us; the launch traced here: 310 us
  blocking collectives  88.3 us (28%)
  waiting for transfers between devices  80.9 us (26%)
  Pallas kernels  40.4 us (13%)
  local copies, waits for them, and re-layouts  31.5 us (10%)
  starting transfers between devices  29.7 us (10%)
  matrix products  18.8 us (6%)
  between operations  14.5 us (5%)
  other arithmetic  6.13 us (2%)
    pallas_call x1, Pallas kernels, attention_grads(): pl.pallas_call(attention_kernel, grid=(windows, owners // per_block), in_...  30.9 us
    all_to_all x1, blocking collectives, body(): lax.all_to_all(lanes_out, 'space', split_axis=0, concat_axis=0, tiled=True)  30.9 us
    all_to_all x1, blocking collectives, body(): lax.all_to_all(embed_partial.astype(jnp.bfloat16).reshape(PATCH, tm_count...  29.3 us
    reduce_scatter x1, waiting for transfers between devices, body(): lax.psum_scatter(contract(hidden, d_packed, 0, 0).astype(jnp.bfloat16), '...  25.4 us
    all_to_all x1, waiting for transfers between devices, body(): lax.all_to_all(grads, 'space', split_axis=0, concat_axis=0, tiled=True)  20.1 us
    all_to_all x1, waiting for transfers between devices, body(): lax.all_to_all(jnp.broadcast_to(local_embed[None], (tm_count,) + local_em...  17 us
    all_to_all x1, blocking collectives, body(): lax.all_to_all(padded.reshape(slab_count, chunk, -1), 'space', split_axis...  14.5 us
    all_to_all x1, blocking collectives, body(): lax.all_to_all(jnp.broadcast_to(qkv_weight[None], (tm_count,) + qkv_weigh...  13.6 us
  transfers between devices with their start and end apart: 7, of which 5 were waited for; matrix products, arithmetic and copies ran while one was open for 8% of the time, Pallas kernels for 3%

profile of v13, /device:TPU:1, one launch (start us, length us, event | category | flops | bytes accessed | tf_op | source)
XLA Modules:
  0.0 310.3 jit_solution(17361205318463716615)
XLA Ops:
  7.2 0.8 broadcast_in_dim.28
  8.1 13.6 %all_to_all.45 = bf16[8,64,384]{2,1,0:T(8,128)(2,1)S(1)} all-to-all(bf16[8,64,384]{2,1,0:T(8,128)(2,1)S(1)} %broadcast_in_dim.28), channel_id=1, replica_groups=mesh['space'=16,'tm'=8] {'tm'}, dimensions={0} | all-to-all | bytes 786432 | tf_op jit(solution)/shard_map/all_to_all | solution.py:243
  21.7 0.8 copy.81
  23.9 0.6 reshape.250.keep_ref
  24.6 1.4 copy.50
  26.0 1.2 reshape.249.rows_ref
  27.4 9.5 %shard_map.77 = bf16[2,256,864]{2,1,0:T(8,128)(2,1)S(1)} custom-call(bf16[2,4,576,96]{3,2,1,0:T(8,128)(2,1)S(1)} %reshape.249.rows_ref, bf16[2,96,1536]{2,1,0:T(8,128)(2,1)S(1)} %fusion.6.pick_ref, bf16[2,96,1536]{2,1,0:T(8,128)(2,1)S(1)} %reshape.250.keep_ref, bf16[36,576]{1,0:T(8,128)(2,1)S(1)} %reshape.265.fold_ref), custom_call_target="tpu_custom_call" | custom-call | flops 2717908992 | bytes 1769472 | tf_op jit(solution)/shard_map/pallas_call | solution.py:67
  37.2 1.6 copy.52
  38.8 7.8 %all-to-all-start = ((bf16[2,16,12,896]{3,0,2,1:T(2,128)(2,1)}), bf16[2,16,12,896]{3,0,2,1:T(2,128)(2,1)S(1)}, u32[]{:S(2)}, u32[]{:S(2)}) async-start(bf16[2,16,12,896]{3,0,2,1:T(2,128)(2,1)} %bitcast.9), calls=%async_computation | async-start | bytes 1376256 | tf_op jit(solution)/shard_map/all_to_all | solution.py:214
  46.8 11.7 %all-to-all-done = bf16[2,16,12,896]{3,0,2,1:T(2,128)(2,1)S(1)} async-done(((bf16[2,16,12,896]{3,0,2,1:T(2,128)(2,1)}), bf16[2,16,12,896]{3,0,2,1:T(2,128)(2,1)S(1)}, u32[]{:S(2)}, u32[]{:S(2)}) %all-to-all-start) | async-done | bytes 688160 | tf_op jit(solution)/shard_map/all_to_all | solution.py:214
  58.5 1.4 broadcast_in_dim.27
  59.9 5.8 %all-to-all-start.1 = ((bf16[8,864,128]{2,1,0:T(8,128)(2,1)}), bf16[8,864,128]{2,1,0:T(8,128)(2,1)S(1)}, u32[]{:S(2)}, u32[]{:S(2)}) async-start(bf16[8,864,128]{2,1,0:T(8,128)(2,1)} %broadcast_in_dim.27), calls=%async_computation.1 | async-start | bytes 3538944 | tf_op jit(solution)/shard_map/all_to_all | solution.py:225
  65.7 1.3 copy.61
  67.0 1.4 copy.62
  68.7 1.4 convolution_convert_fusion.3
  70.1 1.3 copy.55
  71.4 17.0 %all-to-all-done.1 = bf16[8,864,128]{2,1,0:T(8,128)(2,1)S(1)} async-done(((bf16[8,864,128]{2,1,0:T(8,128)(2,1)}), bf16[8,864,128]{2,1,0:T(8,128)(2,1)S(1)}, u32[]{:S(2)}, u32[]{:S(2)}) %all-to-all-start.1) | async-done | bytes 1769504 | tf_op jit(solution)/shard_map/all_to_all | solution.py:225
  88.4 0.9 fusion.39
  89.3 0.3 copy.58
  89.9 0.7 copy-done.2
  90.6 5.8 %convolution_convert_fusion.1 = bf16[256,3072]{1,0:T(8,128)(2,1)} fusion(bf16[1024,3072]{1,0:T(8,128)(2,1)} %all-gather.2.cloned.1.call-done, f32[256,1024]{1,0:T(8,128)S(1)} %copy.58, f32[256]{0:T(256)S(1)} %add_rsqrt_fusion, f32[256]{0:T(256)S(1)} %broadcast_multiply_fusion.2), kind=kOutput, calls=%fused_computation.1 | convolution fusion | flops 1612185600 | bytes 8914944 | tf_op jit(solution)/shard_map/dot_general | solution.py:255
  96.4 1.7 copy.60
  98.1 1.9 reshape.256
  100.0 4.3 %maximum_bitcast_fusion = bf16[16,2,128,4,64]{2,1,4,0,3:T(2,128)(2,1)S(1)} fusion(bf16[2,128,1,16,64]{1,0,4,3,2:T(2,128)(2,1)S(1)} %copy-done.6, bf16[2,128,3,16,64]{1,0,4,3,2:T(2,128)(2,1)} %reshape.256), kind=kLoop, calls=%fused_computation.3 | loop fusion | flops 1048576 | bytes 4194304 | tf_op jit(solution)/shard_map/transpose | solution.py:259
  104.3 0.5 copy.63
  104.8 2.6 copy.64
  107.5 30.9 %all_to_all.46.lanes_ref = bf16[16,2,128,256]{3,2,1,0:T(8,128)(2,1)S(1)} all-to-all(bf16[16,2,128,256]{3,2,1,0:T(8,128)(2,1)} %copy.64), channel_id=1, replica_groups=mesh['space'=16,'tm'=8] {'space'}, dimensions={0} | all-to-all | bytes 4194304 | tf_op jit(solution)/shard_map/all_to_all | solution.py:260
  138.3 30.9 %shard_map.78 = bf16[16,2,128,192]{3,2,1,0:T(8,128)(2,1)S(1)} custom-call(bf16[16,2,128,256]{3,2,1,0:T(8,128)(2,1)S(1)} %all_to_all.46.lanes_ref), custom_call_target="tpu_custom_call" | custom-call | flops 5368709120 | bytes 3670016 | tf_op jit(solution)/shard_map/pallas_call | solution.py:141
  169.3 2.3 copy.65
  171.5 3.8 %all-to-all-start.4 = ((bf16[16,2,128,192]{2,3,1,0:T(8,128)(2,1)}), bf16[16,2,128,192]{2,3,1,0:T(8,128)(2,1)S(1)}, u32[]{:S(2)}, u32[]{:S(2)}) async-start(bf16[16,2,128,192]{2,3,1,0:T(8,128)(2,1)} %copy.65), calls=%async_computation.4 | async-start | bytes 3145728 | tf_op jit(solution)/shard_map/all_to_all | solution.py:262
  175.8 20.1 %all-to-all-done.4 = bf16[16,2,128,192]{2,3,1,0:T(8,128)(2,1)S(1)} async-done(((bf16[16,2,128,192]{2,3,1,0:T(8,128)(2,1)}), bf16[16,2,128,192]{2,3,1,0:T(8,128)(2,1)S(1)}, u32[]{:S(2)}, u32[]{:S(2)}) %all-to-all-start.4) | async-done | bytes 1572896 | tf_op jit(solution)/shard_map/all_to_all | solution.py:262
  195.8 1.6 copy.66
  197.5 1.2 copy-done
  198.7 4.5 %convolution_convert_fusion = bf16[1024,3072]{1,0:T(8,128)(2,1)} fusion(bf16[256,1024]{0,1:T(8,128)(2,1)S(1)} %bitcast.98, bf16[384,8,2,128]{3,2,1,0:T(2,128)(2,1)S(1)} %bitcast.94), kind=kOutput, calls=%fused_computation | convolution fusion | flops 1613758464 | bytes 8388608 | tf_op jit(solution)/shard_map/dot_general | solution.py:26
  203.2 1.4 copy-done.1
  204.9 4.8 %fusion.38 = (f32[256]{0:T(256)S(1)}, f32[256]{0:T(256)S(1)}, f32[256,1024]{1,0:T(8,128)S(1)}) fusion(f32[256]{0:T(256)S(1)} %add_rsqrt_fusion, f32[256,1024]{1,0:T(8,128)S(1)} %copy-done.3, f32[256]{0:T(256)S(1)} %broadcast_multiply_fusion.2, bf16[1024,3072]{1,0:T(8,128)(2,1)} %all-gather.2.cloned.1.call-done, bf16[384,8,2,128]{3,2,1,0:T(2,128)(2,1)S(1)} %bitcast.95), kind=kOutput, calls=%fused_computation.95 | convolution fusion | flops 1611922944 | bytes 9965568 | tf_op jit(solution)/shard_map/dot_general | solution.py:26
  209.7 0.8 convert_bitcast_fusion
  210.6 0.3 copy.110
  210.9 29.3 %all_to_all.47 = bf16[8,864,128]{2,1,0:T(8,128)(2,1)S(1)} all-to-all(bf16[8,864,128]{2,1,0:T(8,128)(2,1)S(1)} %bitcast.92), channel_id=1, replica_groups=mesh['space'=16,'tm'=8] {'tm'}, dimensions={0} | all-to-all | bytes 3538944 | tf_op jit(solution)/shard_map/all_to_all | solution.py:290
  240.5 14.5 %all_to_all.48 = f32[16,54,128]{2,1,0:T(8,128)S(1)} all-to-all(f32[16,54,128]{2,1,0:T(8,128)S(1)} %reshape.263), channel_id=1, replica_groups=mesh['space'=16,'tm'=8] {'space'}, dimensions={0} | all-to-all | bytes 884736 | tf_op jit(solution)/shard_map/all_to_all | solution.py:300
  255.0 0.8 broadcast_in_dim.29
  255.8 5.4 %all-to-all-start.8 = ((f32[16,54,128]{2,1,0:T(8,128)}), f32[16,54,128]{2,1,0:T(8,128)S(1)}, u32[]{:S(2)}, u32[]{:S(2)}) async-start(f32[16,54,128]{2,1,0:T(8,128)} %broadcast_in_dim.29), calls=%async_computation.9 | async-start | bytes 917504 | tf_op jit(solution)/shard_map/all_to_all | solution.py:304
  261.2 25.4 %reduce-scatter.2.cloned.1.call-done = bf16[64,3072]{1,0:T(8,128)(2,1)} async-done(((bf16[1024,3072]{1,0:T(8,128)(2,1)}), bf16[64,3072]{1,0:T(8,128)(2,1)}) %reduce-scatter.2.cloned.1.call-update) | async-done | bytes 393232 | tf_op jit(solution)/shard_map/reduce_scatter | solution.py:268
  286.6 1.8 copy.111
  288.4 6.7 %all-to-all-start.5 = ((bf16[8,64,384]{2,1,0:T(8,128)(2,1)}), bf16[8,64,384]{2,1,0:T(8,128)(2,1)S(1)}, u32[]{:S(2)}, u32[]{:S(2)}) async-start(bf16[8,64,384]{2,1,0:T(8,128)(2,1)} %bitcast.85), calls=%async_computation.6 | async-start | bytes 786432 | tf_op jit(solution)/shard_map/all_to_all | solution.py:276
  295.3 0.8 reshape.264
  296.1 6.7 %all-to-all-done.5 = bf16[8,64,384]{2,1,0:T(8,128)(2,1)S(1)} async-done(((bf16[8,64,384]{2,1,0:T(8,128)(2,1)}), bf16[8,64,384]{2,1,0:T(8,128)(2,1)S(1)}, u32[]{:S(2)}, u32[]{:S(2)}) %all-to-all-start.5) | async-done | bytes 393248 | tf_op jit(solution)/shard_map/all_to_all | solution.py:276
  302.8 0.7 convert_reduce_fusion.1
  (66 shorter events, 3.7 us)
Async XLA Ops:
  7.2 15.4 %copy-start.8 = (s32[2,256]{1,0:T(2,128)S(1)}, s32[2,256]{1,0:T(2,128)}, u32[]{:S(2)}) copy-start(s32[2,256]{1,0:T(2,128)} %param.8) | copy-start | bytes 6148
  7.2 15.8 %copy-start.9 = (s32[2,256]{1,0:T(2,128)S(1)}, s32[2,256]{1,0:T(2,128)}, u32[]{:S(2)}) copy-start(s32[2,256]{1,0:T(2,128)} %param.7) | copy-start | bytes 6148
  7.2 82.7 %all-gather.2.cloned.1.call-start = ((), (), s32[]{:S(2)}) async-start(), calls=%async_computation.10 | async-start | bytes 6684672 | tf_op jit(solution)/shard_map/all_gather | solution.py:253
  37.0 9.5 %copy-start.7 = (bf16[864,128]{1,0:T(8,128)(2,1)S(1)}, bf16[864,128]{1,0:T(8,128)(2,1)}, u32[]{:S(2)}) copy-start(bf16[864,128]{1,0:T(8,128)(2,1)} %param.9) | copy-start | bytes 663556
  38.8 19.7 %all-to-all-start = ((bf16[2,16,12,896]{3,0,2,1:T(2,128)(2,1)}), bf16[2,16,12,896]{3,0,2,1:T(2,128)(2,1)S(1)}, u32[]{:S(2)}, u32[]{:S(2)}) async-start(bf16[2,16,12,896]{3,0,2,1:T(2,128)(2,1)} %bitcast.9), calls=%async_computation | async-start | bytes 1376256 | tf_op jit(solution)/shard_map/all_to_all | solution.py:214
  59.9 28.5 %all-to-all-start.1 = ((bf16[8,864,128]{2,1,0:T(8,128)(2,1)}), bf16[8,864,128]{2,1,0:T(8,128)(2,1)S(1)}, u32[]{:S(2)}, u32[]{:S(2)}) async-start(bf16[8,864,128]{2,1,0:T(8,128)(2,1)} %broadcast_in_dim.27), calls=%async_computation.1 | async-start | bytes 3538944 | tf_op jit(solution)/shard_map/all_to_all | solution.py:225
  71.3 18.3 %copy-start.4 = (bf16[2,128,864]{2,1,0:T(8,128)(2,1)}, bf16[2,128,864]{2,1,0:T(8,128)(2,1)S(1)}, u32[]{:S(2)}) copy-start(bf16[2,128,864]{2,1,0:T(8,128)(2,1)S(1)} %copy.55) | copy-start | bytes 1327108
  89.6 1.0 copy-start.2
  98.1 1.9 copy-start.6
  171.5 24.3 %all-to-all-start.4 = ((bf16[16,2,128,192]{2,3,1,0:T(8,128)(2,1)}), bf16[16,2,128,192]{2,3,1,0:T(8,128)(2,1)S(1)}, u32[]{:S(2)}, u32[]{:S(2)}) async-start(bf16[16,2,128,192]{2,3,1,0:T(8,128)(2,1)} %copy.65), calls=%async_computation.4 | async-start | bytes 3145728 | tf_op jit(solution)/shard_map/all_to_all | solution.py:262
  175.3 111.3 %reduce-scatter.2.cloned.1.call-start = ((), (), s32[]{:S(2)}) async-start(), calls=%async_computation.11 | async-start | bytes 6684672 | tf_op jit(solution)/shard_map/reduce_scatter | solution.py:268
  197.5 1.2 copy-start
  203.2 1.4 copy-start.1
  203.2 1.7 copy-start.3
  204.9 4.9 %copy-start.5 = (bf16[2,128,864]{2,1,0:T(8,128)(2,1)S(1)}, bf16[2,128,864]{2,1,0:T(8,128)(2,1)}, u32[]{:S(2)}) copy-start(bf16[2,128,864]{2,1,0:T(8,128)(2,1)} %copy-done.4) | copy-start | bytes 1327108
  255.8 32.6 %all-to-all-start.8 = ((f32[16,54,128]{2,1,0:T(8,128)}), f32[16,54,128]{2,1,0:T(8,128)S(1)}, u32[]{:S(2)}, u32[]{:S(2)}) async-start(f32[16,54,128]{2,1,0:T(8,128)} %broadcast_in_dim.29), calls=%async_computation.9 | async-start | bytes 917504 | tf_op jit(solution)/shard_map/all_to_all | solution.py:304
  288.4 14.4 %all-to-all-start.5 = ((bf16[8,64,384]{2,1,0:T(8,128)(2,1)}), bf16[8,64,384]{2,1,0:T(8,128)(2,1)S(1)}, u32[]{:S(2)}, u32[]{:S(2)}) async-start(bf16[8,64,384]{2,1,0:T(8,128)(2,1)} %bitcast.85), calls=%async_computation.6 | async-start | bytes 786432 | tf_op jit(solution)/shard_map/all_to_all | solution.py:276
Sparse Core Ops, SparseCore 0:
  22.7 63.4 all-gather.1
  203.3 83.2 reduce-scatter.1
